TPU v7x, 256 devices: a whole 4x4x8 slice. The times are simulated.
256 devices in a mesh: dp: 32 (over z, y), expert: 8 (over x, core).
Axes of the slice: x: 4, y: 4, z: 8, core: 2. Of those that a mesh axis runs over, the one named last changes fastest.
Arguments:
- residual: bfloat16 [2048, 4096], P(('dp', 'expert')), may hold values from -8.2 to 8.2
- queries: bfloat16 [2048, 4096], P('dp', 'expert'), may hold values from -24 to 24
- new_keys: bfloat16 [2048, 1024], P('dp', 'expert'), may hold values from -6 to 6
- new_values: bfloat16 [2048, 1024], P('dp', 'expert'), may hold values from -6 to 6
- cache_keys: bfloat16 [64, 1024, 1024], P('dp', None, 'expert'), may hold values from -8 to 8
- cache_values: bfloat16 [64, 1024, 1024], P('dp', None, 'expert'), may hold values from -6 to 6
- out_weight: bfloat16 [4096, 4096], P('expert', 'dp'), may hold values from -1 to 1
- ffn_gain: float32 [4096], replicated, may hold values from 0.1 to 1.9
- router: bfloat16 [4096, 8], replicated, may hold values from -0.0234375 to 0.0234375
- routes: int32 [2048, 2], P(('dp', 'expert')), may hold values from 0 to 7, all different within a row; in each aligned block of 64 rows (0 to 63, 64 to 127, ...) at most 24 rows name the same one
- w_gate: bfloat16 [8, 4096, 14336], P('expert', None, 'dp'), may hold values from -0.09375 to 0.09375
- w_up: bfloat16 [8, 4096, 14336], P('expert', None, 'dp'), may hold values from -0.09375 to 0.09375
- w_down: bfloat16 [8, 14336, 4096], P('expert', 'dp'), may hold values from -0.046875 to 0.046875
- summary_gain: float32 [4096], P('expert'), may hold values from 0.1 to 1.9
- reduce_scale: float32 [32], P('expert'), may hold values from 0.1 to 30
- assign: int32 [64], replicated, may hold values from 0 to 3
Outputs:
- summary: bfloat16 [64, 4096], P('dp', 'expert')
- reduced: bfloat16 [64, 4096], P('dp', 'expert')
Inputs may be any that keep to these rules, and one draw needn't show every extreme that they name: `routes`: each token names 2 different experts and every expert is named by some token; among the tokens of one dp index (aligned blocks of 64 rows) no expert is named by more than 24 tokens, and that bound is reached in some block.
All inputs are finite; a program needn't handle non-finite values.
Results may differ from a plain program's by a relative error of at most 0.017.
Values may be sent and summed in bfloat16 or wider, within the bound.
No kernel may reach another device: no remote copies, remote signals or barrier semaphores. Data moves between devices by JAX's collectives and lax.ppermute only.
A program may use at most 128 MiB of HBM per device.

v0:
```python
import math

import jax
import jax.numpy as jnp
from jax import lax
from jax.sharding import PartitionSpec as P

HEADS = 32
KVH = 8
HD = 128
EXPERTS = 8
WIN = 32
GROUP_CAP = 24


EPSILON = 1e-05


def attend(queries, new_keys, new_values, cache_keys, cache_values):
    span_count, cache_len, kv_width = cache_keys.shape
    kv_local = kv_width // HD
    group = HEADS // KVH
    window = queries.shape[0] // span_count
    query_view = queries.reshape(span_count, window, kv_local, group, HD)
    fresh_keys = new_keys.reshape(span_count, window, kv_local, HD)
    fresh_values = new_values.reshape(span_count, window, kv_local, HD)
    stored_keys = cache_keys.reshape(span_count, cache_len, kv_local, HD)
    stored_values = cache_values.reshape(span_count, cache_len, kv_local, HD)
    factor = 1.0 / math.sqrt(HD)
    past_scores = (
        jnp.einsum("ctkgd,cpkd->ckgtp", query_view, stored_keys, preferred_element_type=jnp.float32)
        * factor
    )
    fresh_scores = (
        jnp.einsum("ctkgd,cskd->ckgts", query_view, fresh_keys, preferred_element_type=jnp.float32)
        * factor
    )
    causal = jnp.arange(window)[:, None] >= jnp.arange(window)[None, :]
    fresh_scores = jnp.where(causal, fresh_scores, -jnp.inf)
    highest = jnp.maximum(jnp.max(past_scores, axis=-1), jnp.max(fresh_scores, axis=-1))[..., None]
    past_exp = jnp.exp(past_scores - highest)
    fresh_exp = jnp.exp(fresh_scores - highest)
    totals = jnp.sum(past_exp, axis=-1, keepdims=True) + jnp.sum(fresh_exp, axis=-1, keepdims=True)
    past_weights = (past_exp / totals).astype(jnp.bfloat16)
    fresh_weights = (fresh_exp / totals).astype(jnp.bfloat16)
    context = jnp.einsum(
        "ckgtp,cpkd->ctkgd", past_weights, stored_values, preferred_element_type=jnp.float32
    )
    context = context + jnp.einsum(
        "ckgts,cskd->ctkgd", fresh_weights, fresh_values, preferred_element_type=jnp.float32
    )
    return context.astype(jnp.bfloat16).reshape(span_count * window, kv_local * group * HD)


def expert_rows(rows, w_gate, w_up, w_down):
    gate_proj = jnp.einsum("ned,edf->nef", rows, w_gate, preferred_element_type=jnp.float32)
    up_proj = jnp.einsum("ned,edf->nef", rows, w_up, preferred_element_type=jnp.float32)
    hidden = (jax.nn.silu(gate_proj) * up_proj).astype(jnp.bfloat16)
    return jnp.einsum("nef,efd->ned", hidden, w_down, preferred_element_type=jnp.float32)


def shards(
    residual,
    queries,
    new_keys,
    new_values,
    cache_keys,
    cache_values,
    out_weight,
    ffn_gain,
    router,
    routes,
    w_gate,
    w_up,
    w_down,
    summary_gain,
    reduce_scale,
    assign,
):
    expert_count = lax.axis_size("expert")
    dp_index = lax.axis_index("dp")
    column = lax.axis_index("expert")
    span_local = cache_keys.shape[0]
    tok_local = residual.shape[0]
    width = residual.shape[1]
    slice_width = width // expert_count
    highest_precision = lax.Precision.HIGHEST
    attended = attend(queries, new_keys, new_values, cache_keys, cache_values)
    head_terms = jnp.dot(
        attended,
        lax.all_gather(out_weight, "dp", axis=1, tiled=True),
        preferred_element_type=jnp.float32,
    )
    mixed = residual.astype(jnp.float32) + lax.psum_scatter(
        head_terms, "expert", scatter_dimension=0, tiled=True
    )
    normed = (
        mixed * lax.rsqrt(jnp.mean(mixed * mixed, axis=-1, keepdims=True) + EPSILON) * ffn_gain
    ).astype(jnp.bfloat16)
    logits = jnp.dot(normed, router, preferred_element_type=jnp.float32)
    expert_ids = jnp.arange(EXPERTS, dtype=jnp.int32)
    first = routes[:, 0:1] == expert_ids[None, :]
    second = routes[:, 1:2] == expert_ids[None, :]
    first_logit = jnp.sum(jnp.where(first, logits, 0.0), axis=-1)
    second_logit = jnp.sum(jnp.where(second, logits, 0.0), axis=-1)
    partner = jnp.where(first, routes[:, 1:2], jnp.where(second, routes[:, 0:1], -1))
    outgoing = jnp.where((partner >= 0).T[:, :, None], normed[None, :, :], 0)
    arrived_rows, arrived_partner = (
        lax.all_to_all(outgoing, "expert", split_axis=0, concat_axis=1, tiled=True),
        lax.all_to_all(partner.T, "expert", split_axis=0, concat_axis=1, tiled=True),
    )
    present = (arrived_partner >= 0).astype(jnp.int32)
    position = jnp.cumsum(present, axis=1) - 1
    picker = (present[:, None, :] > 0) & (
        position[:, None, :] == jnp.arange(GROUP_CAP)[None, :, None]
    )
    compact = jnp.einsum(
        "eks,esd->ked",
        picker.astype(jnp.bfloat16),
        arrived_rows,
        preferred_element_type=jnp.float32,
    ).astype(jnp.bfloat16)
    token_span = (column * tok_local + jnp.arange(tok_local)) // WIN
    pool_matrix = (token_span[None, :] == jnp.arange(span_local)[:, None]).astype(jnp.float32)
    gathered = lax.all_gather(compact, "dp", axis=0, tiled=True)
    returned = lax.psum_scatter(
        expert_rows(gathered, w_gate, w_up, w_down), "dp", scatter_dimension=0, tiled=True
    )
    spread = jnp.einsum(
        "eks,ked->esd", picker.astype(jnp.float32), returned, precision=highest_precision
    )
    back = lax.all_to_all(spread, "expert", split_axis=1, concat_axis=0, tiled=True)
    gate_table = jnp.where(first, jax.nn.sigmoid(first_logit - second_logit)[:, None], 0.0)
    gate_table = gate_table + jnp.where(
        second, jax.nn.sigmoid(second_logit - first_logit)[:, None], 0.0
    )
    token_out = mixed + jnp.einsum("te,etd->td", gate_table, back, precision=highest_precision)
    pooled_local = jnp.dot(pool_matrix, token_out, precision=highest_precision)
    pooled = lax.psum_scatter(pooled_local, "expert", scatter_dimension=1, tiled=True)
    squares = lax.psum(jnp.sum(pooled * pooled, axis=-1), "expert")
    summary = (pooled * lax.rsqrt(squares / width + EPSILON)[:, None] * summary_gain).astype(
        jnp.bfloat16
    )
    everyone = lax.all_gather(summary, "dp", axis=0, tiled=True)
    heads_local = slice_width // HD
    mine = summary.reshape(span_local, heads_local, HD)
    others = everyone.reshape(everyone.shape[0], heads_local, HD)
    factor = reduce_scale / math.sqrt(HD)
    scores = (
        jnp.einsum("chd,khd->hck", mine, others, preferred_element_type=jnp.float32)
        * factor[:, None, None]
    )
    own_assign = lax.dynamic_slice_in_dim(assign, dp_index * span_local, span_local)
    same = own_assign[:, None] == assign[None, :]
    scores = jnp.where(same[None], scores, -jnp.inf)
    highest = jnp.max(scores, axis=-1, keepdims=True)
    expo = jnp.exp(scores - highest)
    weights = (expo / jnp.sum(expo, axis=-1, keepdims=True)).astype(jnp.bfloat16)
    reduced = jnp.einsum("hck,khd->chd", weights, others, preferred_element_type=jnp.float32)
    reduced = reduced.reshape(span_local, slice_width).astype(jnp.bfloat16)
    return (summary, reduced)


def solution(mesh):
    return jax.shard_map(
        shards,
        mesh=mesh,
        in_specs=(
            P(("dp", "expert"), None),
            P("dp", "expert"),
            P("dp", "expert"),
            P("dp", "expert"),
            P("dp", None, "expert"),
            P("dp", None, "expert"),
            P("expert", "dp"),
            P(),
            P(),
            P(("dp", "expert"), None),
            P("expert", None, "dp"),
            P("expert", None, "dp"),
            P("expert", "dp", None),
            P("expert"),
            P("expert"),
            P(),
        ),
        out_specs=(P("dp", "expert"), P("dp", "expert")),
        check_vma=False,
    )
```

profile of v0, /device:TPU:2, one launch (start us, length us, event | category | flops | bytes accessed | tf_op | source)
XLA Modules:
  0.0 633.6 jit_solution(1223442760722272505)
XLA Ops:
  7.2 0.7 all-gather.4.cloned.1.call-update
  8.0 0.9 reshape.508
  9.2 1.0 fusion.83
  10.6 0.9 fusion.61
  11.5 0.4 fusion.42
  12.0 84.1 %all-gather.4.cloned.1.call-done = bf16[512,4096]{1,0:T(8,128)(2,1)} async-done(((bf16[512,128]{1,0:T(8,128)(2,1)}), bf16[512,4096]{1,0:T(8,128)(2,1)}) %all-gather.4.cloned.1.call-update) | async-done | bytes 4194320 | tf_op jit(solution)/shard_map/all_gather | solution.py:91
  96.1 4.0 fusion.58
  100.2 0.6 compare_select_fusion.1
  100.8 4.8 all-to-all-start
  105.6 27.0 %reduce-scatter.6.cloned.1.call-done = f32[8,4096]{1,0:T(8,128)} async-done(((f32[64,4096]{1,0:T(8,128)}), f32[8,4096]{1,0:T(8,128)}) %reduce-scatter.6.cloned.1.call-update) | async-done | bytes 131088 | tf_op jit(solution)/shard_map/reduce_scatter | solution.py:94
  132.6 1.1 multiply_reduce_fusion
  133.7 1.0 multiply_convert_fusion
  134.6 0.9 broadcast_select_fusion
  135.5 7.0 %all-to-all-start.1 = ((bf16[8,8,4096]{2,1,0:T(8,128)(2,1)}), bf16[8,8,4096]{2,1,0:T(8,128)(2,1)S(1)}, u32[]{:S(2)}, u32[]{:S(2)}) async-start(bf16[8,8,4096]{2,1,0:T(8,128)(2,1)} %broadcast_select_fusion), calls=%async_computation.2 | async-start | bytes 1048576 | tf_op jit(solution)/shard_map/all_to_all | solution.py:109
  142.9 8.5 %all-to-all-done.1 = bf16[8,8,4096]{2,1,0:T(8,128)(2,1)S(1)} async-done(((bf16[8,8,4096]{2,1,0:T(8,128)(2,1)}), bf16[8,8,4096]{2,1,0:T(8,128)(2,1)S(1)}, u32[]{:S(2)}, u32[]{:S(2)}) %all-to-all-start.1) | async-done | bytes 524320 | tf_op jit(solution)/shard_map/all_to_all | solution.py:109
  151.4 0.9 fusion.5
  152.5 88.6 %all-gather.6.cloned.1.call-done = bf16[768,1,4096]{2,0,1:T(8,128)(2,1)} async-done(((bf16[24,1,4096]{2,0,1:T(8,128)(2,1)}), bf16[768,1,4096]{2,0,1:T(8,128)(2,1)}) %all-gather.6.cloned.1.call-update) | async-done | bytes 6291472 | tf_op jit(solution)/shard_map/all_gather | solution.py:125
  241.1 6.9 %fusion.9 = f32[768,1,448]{0,2,1:T(8,128)S(1)} fusion(bf16[1,4096,448]{1,2,0:T(8,128)(2,1)} %param.26, bf16[768,1,4096]{2,0,1:T(8,128)(2,1)} %all-gather.6.cloned.1.call-done), kind=kOutput, calls=%fused_computation.13 | convolution fusion | flops 2818572288 | bytes 11337728 | tf_op jit(solution)/shard_map/ned,edf->nef/dot_general | solution.py:56
  248.0 17.8 %convolution_bitcast_fusion = f32[768,1,4096]{2,0,1:T(8,128)} fusion(bf16[1,448,4096]{2,1,0:T(8,128)(2,1)} %param.28, bf16[1,4096,448]{1,2,0:T(8,128)(2,1)} %param.27, bf16[768,1,4096]{2,0,1:T(8,128)(2,1)} %all-gather.6.cloned.1.call-done, f32[768,1,448]{0,2,1:T(8,128)S(1)} %fusion.9), kind=kOutput, calls=%fused_computation.1 | convolution fusion | flops 5639208960 | bytes 27590656 | tf_op jit(solution)/shard_map/nef,efd->ned/dot_general | solution.py:59
  265.9 236.3 %reduce-scatter.8.cloned.1.call-done = f32[24,1,4096]{2,0,1:T(8,128)} async-done(((f32[768,1,4096]{2,0,1:T(8,128)}), f32[24,1,4096]{2,0,1:T(8,128)}) %reduce-scatter.8.cloned.1.call-update) | async-done | bytes 393232 | tf_op jit(solution)/shard_map/reduce_scatter | solution.py:126
  502.2 1.6 convolution_bitcast_fusion.2
  503.8 2.1 copy.45
  505.9 4.8 all-to-all-start.2
  511.0 14.1 %all-to-all-done.2 = f32[1,64,4096]{2,0,1:T(1,128)S(1)} async-done(((f32[1,64,4096]{2,0,1:T(1,128)}), f32[1,64,4096]{2,0,1:T(1,128)S(1)}, u32[]{:S(2)}, u32[]{:S(2)}) %all-to-all-start.2) | async-done | bytes 1048608 | tf_op jit(solution)/shard_map/all_to_all | solution.py:132
  525.1 0.6 copy.86
  525.7 1.5 fusion.47
  527.2 3.2 convolution_bitcast_fusion.1
  530.5 31.0 %reduce-scatter.10.cloned.1.call-done = f32[512,2]{1,0:T(8,128)} async-done(((f32[4096,2]{1,0:T(8,128)}), f32[512,2]{1,0:T(8,128)}) %reduce-scatter.10.cloned.1.call-update) | async-done | bytes 4112
  561.5 1.1 copy.58
  562.7 13.4 %psum.7 = f32[2]{0:T(128)S(1)} all-reduce(f32[2]{0:T(128)S(1)} %multiply_reduce_fusion.1), channel_id=1, replica_groups=mesh['dp'=32,'expert'=8] {'expert'}, use_global_device_ids=true, to_apply=%region_12.13 | all-reduce | flops 2 | bytes 16 | tf_op jit(solution)/shard_map/psum | solution.py:140
  576.3 49.6 %all-gather = bf16[32,2,512]{2,1,0:T(2,128)(2,1)S(1)} all-gather(bf16[1,2,512]{2,1,0:T(2,128)(2,1)S(1)} %fusion.95), channel_id=1, replica_groups=mesh['dp'=32,'expert'=8] {'dp'}, dimensions={0}, use_global_device_ids=true | all-gather | bytes 67584 | tf_op jit(solution)/shard_map/all_gather | solution.py:144
  626.3 0.8 fusion.46
  (62 shorter events, 2.7 us)
Async XLA Ops:
  7.2 1.7 copy-start
  7.2 4.3 copy-start.8
  7.2 88.9 %all-gather.4.cloned.1.call-start = ((), (), s32[]{:S(2)}) async-start(), calls=%async_computation.6 | async-start | bytes 4325376 | tf_op jit(solution)/shard_map/all_gather | solution.py:91
  7.9 124.7 %reduce-scatter.6.cloned.1.call-start = ((), (), s32[]{:S(2)}) async-start(), calls=%async_computation.7 | async-start | bytes 1179648 | tf_op jit(solution)/shard_map/reduce_scatter | solution.py:94
  11.9 88.3 %copy-start.7 = (s32[8,2]{0,1:T(2,128)S(1)}, s32[8,2]{0,1:T(2,128)}, u32[]{:S(2)}) copy-start(s32[8,2]{0,1:T(2,128)} %param.25) | copy-start | bytes 196
  11.9 120.7 %copy-start.2 = (bf16[8,4096]{1,0:T(8,128)(2,1)S(1)}, bf16[8,4096]{1,0:T(8,128)(2,1)}, u32[]{:S(2)}) copy-start(bf16[8,4096]{1,0:T(8,128)(2,1)} %param.16) | copy-start | bytes 196612
  11.9 121.7 %copy-start.4 = (f32[4096]{0:T(1024)S(1)}, f32[4096]{0:T(1024)}, u32[]{:S(2)}) copy-start(f32[4096]{0:T(1024)} %param.23) | copy-start | bytes 49156
  100.8 34.8 %all-to-all-start = ((s32[8,1,8]{2,1,0:T(1,128)}), s32[8,1,8]{2,1,0:T(1,128)S(1)}, u32[]{:S(2)}, u32[]{:S(2)}) async-start(s32[8,1,8]{2,1,0:T(1,128)} %compare_select_fusion.1), calls=%async_computation.1 | async-start | bytes 8192 | tf_op jit(solution)/shard_map/all_to_all | solution.py:110
  135.5 15.9 %all-to-all-start.1 = ((bf16[8,8,4096]{2,1,0:T(8,128)(2,1)}), bf16[8,8,4096]{2,1,0:T(8,128)(2,1)S(1)}, u32[]{:S(2)}, u32[]{:S(2)}) async-start(bf16[8,8,4096]{2,1,0:T(8,128)(2,1)} %broadcast_select_fusion), calls=%async_computation.2 | async-start | bytes 1048576 | tf_op jit(solution)/shard_map/all_to_all | solution.py:109
  142.5 98.6 %all-gather.6.cloned.1.call-start = ((), (), s32[]{:S(2)}) async-start(), calls=%async_computation.8 | async-start | bytes 6488064 | tf_op jit(solution)/shard_map/all_gather | solution.py:125
  152.3 349.9 %reduce-scatter.8.cloned.1.call-start = ((), (), s32[]{:S(2)}) async-start(), calls=%async_computation.9 | async-start | bytes 12976128 | tf_op jit(solution)/shard_map/reduce_scatter | solution.py:126
  265.9 244.8 %copy-start.9 = (s32[64]{0:T(128)S(1)}, s32[64]{0:T(128)}, u32[]{:S(2)}) copy-start(s32[64]{0:T(128)} %param.31) | copy-start | bytes 772
  265.9 244.9 %copy-start.3 = (bf16[4096,8]{0,1:T(8,128)(2,1)S(1)}, bf16[4096,8]{0,1:T(8,128)(2,1)}, u32[]{:S(2)}) copy-start(bf16[4096,8]{0,1:T(8,128)(2,1)} %param.24) | copy-start | bytes 196612
  503.8 23.4 %copy-start.1 = (f32[8,4096]{1,0:T(8,128)S(1)}, f32[8,4096]{1,0:T(8,128)}, u32[]{:S(2)}) copy-start(f32[8,4096]{1,0:T(8,128)} %reduce-scatter.6.cloned.1.call-done) | copy-start | bytes 393220
  505.9 19.2 %all-to-all-start.2 = ((f32[1,64,4096]{2,0,1:T(1,128)}), f32[1,64,4096]{2,0,1:T(1,128)S(1)}, u32[]{:S(2)}, u32[]{:S(2)}) async-start(f32[1,64,4096]{2,0,1:T(1,128)} %copy.45), calls=%async_computation.4 | async-start | bytes 2097152 | tf_op jit(solution)/shard_map/all_to_all | solution.py:132
  510.6 50.9 %reduce-scatter.10.cloned.1.call-start = ((), (), s32[]{:S(2)}) async-start(), calls=%async_computation.10 | async-start | bytes 2359296
  511.0 51.7 %copy-start.10 = (f32[4]{0:T(128)S(1)}, f32[4]{0:T(128)}, u32[]{:S(2)}) copy-start(f32[4]{0:T(128)} %param.30) | copy-start | bytes 52
  511.0 65.2 %copy-start.5 = (f32[512]{0:T(512)S(1)}, f32[512]{0:T(512)}, u32[]{:S(2)}) copy-start(f32[512]{0:T(512)} %param.29) | copy-start | bytes 6148
  576.2 50.8 %copy-start.6 = (bf16[2,512]{1,0:T(2,128)(2,1)}, bf16[2,512]{1,0:T(2,128)(2,1)S(1)}, u32[]{:S(2)}) copy-start(bf16[2,512]{1,0:T(2,128)(2,1)S(1)} %multiply_convert_fusion.1) | copy-start | bytes 6148
Sparse Core Ops, SparseCore 0:
  10.5 85.6 all-gather.3
  100.3 32.2 reduce-scatter.5
  152.4 88.6 all-gather.5
  266.0 236.1 reduce-scatter.7
  530.6 30.9 reduce-scatter.9
where the time goes:
time: 636 us; the launch traced here: 634 us
  waiting for transfers between devices  490 us (77%)
  blocking collectives  63 us (10%)
  matrix products  39.8 us (6%)
  starting transfers between devices  16.8 us (3%)
  between operations  14 us (2%)
    reduce_scatter x1, waiting for transfers between devices, shards(): lax.psum_scatter(expert_rows(gathered, w_gate, w_up, w_down), 'dp', scatt...  236 us
    all_gather x1, waiting for transfers between devices, shards(): gathered = lax.all_gather(compact, 'dp', axis=0, tiled=True)  88.6 us
    all_gather x1, waiting for transfers between devices, shards(): lax.all_gather(out_weight, 'dp', axis=1, tiled=True)  84.1 us
    all_gather x1, blocking collectives, shards(): everyone = lax.all_gather(summary, 'dp', axis=0, tiled=True)  49.6 us
    unnamed x6, waiting for transfers between devices  31.8 us
    reduce_scatter x1, waiting for transfers between devices, shards(): lax.psum_scatter(head_terms, 'expert', scatter_dimension=0, tiled=True)  27 us
    dot_general x1, matrix products, expert_rows(): jnp.einsum('nef,efd->ned', hidden, w_down, preferred_element_type=jnp.flo...  17.8 us
    all_to_all x1, waiting for transfers between devices, shards(): lax.all_to_all(spread, 'expert', split_axis=1, concat_axis=0, tiled=True)  14.1 us
  transfers between devices with their start and end apart: 8, of which 7 were waited for; matrix products, arithmetic and copies ran while one was open for 1% of the time, Pallas kernels for 0%

commit v1 on v0

--- a/solution.py
+++ b/solution.py
@@ -52,13 +52,6 @@
     return context.astype(jnp.bfloat16).reshape(span_count * window, kv_local * group * HD)
 
 
-def expert_rows(rows, w_gate, w_up, w_down):
-    gate_proj = jnp.einsum("ned,edf->nef", rows, w_gate, preferred_element_type=jnp.float32)
-    up_proj = jnp.einsum("ned,edf->nef", rows, w_up, preferred_element_type=jnp.float32)
-    hidden = (jax.nn.silu(gate_proj) * up_proj).astype(jnp.bfloat16)
-    return jnp.einsum("nef,efd->ned", hidden, w_down, preferred_element_type=jnp.float32)
-
-
 def shards(
     residual,
     queries,
@@ -97,12 +90,9 @@
     normed = (
         mixed * lax.rsqrt(jnp.mean(mixed * mixed, axis=-1, keepdims=True) + EPSILON) * ffn_gain
     ).astype(jnp.bfloat16)
-    logits = jnp.dot(normed, router, preferred_element_type=jnp.float32)
     expert_ids = jnp.arange(EXPERTS, dtype=jnp.int32)
     first = routes[:, 0:1] == expert_ids[None, :]
     second = routes[:, 1:2] == expert_ids[None, :]
-    first_logit = jnp.sum(jnp.where(first, logits, 0.0), axis=-1)
-    second_logit = jnp.sum(jnp.where(second, logits, 0.0), axis=-1)
     partner = jnp.where(first, routes[:, 1:2], jnp.where(second, routes[:, 0:1], -1))
     outgoing = jnp.where((partner >= 0).T[:, :, None], normed[None, :, :], 0)
     arrived_rows, arrived_partner = (
@@ -120,28 +110,49 @@
         arrived_rows,
         preferred_element_type=jnp.float32,
     ).astype(jnp.bfloat16)
-    token_span = (column * tok_local + jnp.arange(tok_local)) // WIN
-    pool_matrix = (token_span[None, :] == jnp.arange(span_local)[:, None]).astype(jnp.float32)
+    arrived_count = arrived_partner.shape[1]
+    pick = picker[0]
+    slot_present = jnp.any(pick, axis=1)
+    slot_partner = jnp.sum(jnp.where(pick, arrived_partner[0][None, :], 0), axis=1)
+    local_span = jnp.arange(arrived_count) // WIN
+    slot_span = jnp.sum(jnp.where(pick, local_span[None, :], 0), axis=1)
+    slot_logits = jnp.dot(compact[:, 0, :], router, preferred_element_type=jnp.float32)
+    own_logit = jnp.sum(jnp.where(expert_ids[None, :] == column, slot_logits, 0.0), axis=-1)
+    partner_logit = jnp.sum(
+        jnp.where(expert_ids[None, :] == slot_partner[:, None], slot_logits, 0.0), axis=-1
+    )
+    slot_gate = jnp.where(slot_present, jax.nn.sigmoid(own_logit - partner_logit), 0.0)
+    pool_weight = jnp.where(
+        slot_span[:, None] == jnp.arange(span_local)[None, :], slot_gate[:, None], 0.0
+    )
     gathered = lax.all_gather(compact, "dp", axis=0, tiled=True)
-    returned = lax.psum_scatter(
-        expert_rows(gathered, w_gate, w_up, w_down), "dp", scatter_dimension=0, tiled=True
+    gathered_weight = lax.all_gather(pool_weight, "dp", axis=0, tiled=True)
+    n_dp = gathered.shape[0] // GROUP_CAP
+    gate_proj = jnp.einsum("ned,edf->nf", gathered, w_gate, preferred_element_type=jnp.float32)
+    up_proj = jnp.einsum("ned,edf->nf", gathered, w_up, preferred_element_type=jnp.float32)
+    hidden = (jax.nn.silu(gate_proj) * up_proj).astype(jnp.bfloat16)
+    span_hidden = jnp.einsum(
+        "iks,ikf->isf",
+        gathered_weight.reshape(n_dp, GROUP_CAP, span_local),
+        hidden.reshape(n_dp, GROUP_CAP, -1).astype(jnp.float32),
+        precision=highest_precision,
+    ).reshape(n_dp * span_local, -1)
+    pooled_part = jnp.dot(
+        span_hidden, w_down[0].astype(jnp.float32), precision=highest_precision
     )
-    spread = jnp.einsum(
-        "eks,ked->esd", picker.astype(jnp.float32), returned, precision=highest_precision
+    own_span = dp_index * span_local + (column * tok_local) // WIN
+    span_count = n_dp * span_local
+    mixed_sum = jnp.sum(mixed, axis=0)
+    pooled_part = pooled_part + jnp.where(
+        (jnp.arange(span_count) == own_span)[:, None], mixed_sum[None, :], 0.0
     )
-    back = lax.all_to_all(spread, "expert", split_axis=1, concat_axis=0, tiled=True)
-    gate_table = jnp.where(first, jax.nn.sigmoid(first_logit - second_logit)[:, None], 0.0)
-    gate_table = gate_table + jnp.where(
-        second, jax.nn.sigmoid(second_logit - first_logit)[:, None], 0.0
-    )
-    token_out = mixed + jnp.einsum("te,etd->td", gate_table, back, precision=highest_precision)
-    pooled_local = jnp.dot(pool_matrix, token_out, precision=highest_precision)
-    pooled = lax.psum_scatter(pooled_local, "expert", scatter_dimension=1, tiled=True)
-    squares = lax.psum(jnp.sum(pooled * pooled, axis=-1), "expert")
-    summary = (pooled * lax.rsqrt(squares / width + EPSILON)[:, None] * summary_gain).astype(
-        jnp.bfloat16
-    )
-    everyone = lax.all_gather(summary, "dp", axis=0, tiled=True)
+    pooled_cols = lax.psum_scatter(pooled_part, "expert", scatter_dimension=1, tiled=True)
+    pooled_cols = lax.psum(pooled_cols, "dp")
+    squares = lax.psum(jnp.sum(pooled_cols * pooled_cols, axis=-1), "expert")
+    everyone = (
+        pooled_cols * lax.rsqrt(squares / width + EPSILON)[:, None] * summary_gain
+    ).astype(jnp.bfloat16)
+    summary = lax.dynamic_slice_in_dim(everyone, dp_index * span_local, span_local)
     heads_local = slice_width // HD
     mine = summary.reshape(span_local, heads_local, HD)
     others = everyone.reshape(everyone.shape[0], heads_local, HD)

time: 636 us -> 460 us (0.72)
  waiting for transfers between devices: 490 us -> 339 us
  matrix products: 39.8 us -> 27.4 us
  blocking collectives: 63 us -> 53.9 us
    reduce_scatter x1, waiting for transfers between devices: 236 us -> 28.6 us  [shards(): lax.psum_scatter(pooled_part, 'expert', scatter_dimension=1, tiled=True)]
    psum x0 -> x1, waiting for transfers between devices: none -> 148 us  [shards(): pooled_cols = lax.psum(pooled_cols, 'dp')]
    all_gather x1, waiting for transfers between devices: 88.6 us -> 43.6 us  [shards(): gathered = lax.all_gather(compact, 'dp', axis=0, tiled=True)]
    unnamed x6 -> x5, waiting for transfers between devices: 31.8 us -> 0.75 us
    all_to_all x1 -> x0, waiting for transfers between devices: 14.1 us -> none  [shards(): lax.all_to_all(spread, 'expert', split_axis=1, concat_axis=0, tiled=True)]
    dot_general x5, matrix products: 28 us -> 16.9 us  [the longest x1 7.05 us: shards(): jnp.einsum('ned,edf->nf', gathered, w_gate, preferred_element_type=jnp.fl...]
  transfers between devices with their start and end apart: 8 -> 7, of which waited for: 7 -> 6; matrix products, arithmetic and copies ran while one was open for 1% -> 2% of each run, Pallas kernels for 0% -> 0%
where the time goes in v1:
time: 460 us; the launch traced here: 456 us
  waiting for transfers between devices  339 us (74%)
  blocking collectives  53.9 us (12%)
  matrix products  27.4 us (6%)
  between operations  14.1 us (3%)
  starting transfers between devices  12 us (3%)
  other arithmetic  7.17 us (2%)
    psum x1, waiting for transfers between devices, shards(): pooled_cols = lax.psum(pooled_cols, 'dp')  148 us
    all_gather x1, waiting for transfers between devices, shards(): lax.all_gather(out_weight, 'dp', axis=1, tiled=True)  84.1 us
    all_gather x1, blocking collectives, shards(): gathered_weight = lax.all_gather(pool_weight, 'dp', axis=0, tiled=True)  43.9 us
    all_gather x1, waiting for transfers between devices, shards(): gathered = lax.all_gather(compact, 'dp', axis=0, tiled=True)  43.6 us
    reduce_scatter x1, waiting for transfers between devices, shards(): lax.psum_scatter(pooled_part, 'expert', scatter_dimension=1, tiled=True)  28.6 us
    reduce_scatter x1, waiting for transfers between devices, shards(): lax.psum_scatter(head_terms, 'expert', scatter_dimension=0, tiled=True)  27 us
    psum x1, blocking collectives, shards(): squares = lax.psum(jnp.sum(pooled_cols * pooled_cols, axis=-1), 'expert')  10 us
  transfers between devices with their start and end apart: 7, of which 6 were waited for; matrix products, arithmetic and copies ran while one was open for 2% of the time, Pallas kernels for 0%

profile of v1, /device:TPU:2, one launch (start us, length us, event | category | flops | bytes accessed | tf_op | source)
XLA Modules:
  0.0 455.8 jit_solution(10144320645197838944)
XLA Ops:
  7.2 0.7 all-gather.4.cloned.1.call-update
  8.0 0.9 reshape.501
  9.2 1.0 fusion.60
  10.6 0.9 fusion.40
  11.5 0.4 fusion.22
  12.0 84.1 %all-gather.4.cloned.1.call-done = bf16[512,4096]{1,0:T(8,128)(2,1)} async-done(((bf16[512,128]{1,0:T(8,128)(2,1)}), bf16[512,4096]{1,0:T(8,128)(2,1)}) %all-gather.4.cloned.1.call-update) | async-done | bytes 4194320 | tf_op jit(solution)/shard_map/all_gather | solution.py:84
  96.1 4.0 fusion.35
  100.2 0.6 compare_select_fusion.1
  100.8 4.8 %all-to-all-start = ((s32[8,1,8]{2,1,0:T(1,128)}), s32[8,1,8]{2,1,0:T(1,128)S(1)}, u32[]{:S(2)}, u32[]{:S(2)}) async-start(s32[8,1,8]{2,1,0:T(1,128)} %compare_select_fusion.1), calls=%async_computation | async-start | bytes 8192 | tf_op jit(solution)/shard_map/all_to_all | solution.py:100
  105.6 27.0 %reduce-scatter.3.cloned.1.call-done = f32[8,4096]{1,0:T(8,128)} async-done(((f32[64,4096]{1,0:T(8,128)}), f32[8,4096]{1,0:T(8,128)}) %reduce-scatter.3.cloned.1.call-update) | async-done | bytes 131088 | tf_op jit(solution)/shard_map/reduce_scatter | solution.py:87
  132.6 1.1 fusion.47
  133.7 1.0 multiply_convert_fusion.1
  134.7 0.9 broadcast_select_fusion
  135.6 7.0 %all-to-all-start.1 = ((bf16[8,8,4096]{2,1,0:T(8,128)(2,1)}), bf16[8,8,4096]{2,1,0:T(8,128)(2,1)S(1)}, u32[]{:S(2)}, u32[]{:S(2)}) async-start(bf16[8,8,4096]{2,1,0:T(8,128)(2,1)} %broadcast_select_fusion), calls=%async_computation.2 | async-start | bytes 1048576 | tf_op jit(solution)/shard_map/all_to_all | solution.py:99
  142.6 0.5 broadcast.319
  143.1 0.7 fusion.58
  144.1 7.3 %all-to-all-done.1 = bf16[8,8,4096]{2,1,0:T(8,128)(2,1)S(1)} async-done(((bf16[8,8,4096]{2,1,0:T(8,128)(2,1)}), bf16[8,8,4096]{2,1,0:T(8,128)(2,1)S(1)}, u32[]{:S(2)}, u32[]{:S(2)}) %all-to-all-start.1) | async-done | bytes 524320 | tf_op jit(solution)/shard_map/all_to_all | solution.py:99
  151.5 0.9 convolution_convert_fusion
  152.7 1.1 select_reduce_fusion.2
  153.9 43.9 %all-gather = f32[32,24,2]{1,2,0:T(2,128)S(1)} all-gather(f32[1,24,2]{1,2,0:T(2,128)S(1)} %fusion.56), channel_id=1, replica_groups=mesh['dp'=32,'expert'=8] {'dp'}, dimensions={0}, use_global_device_ids=true | all-gather | bytes 6336 | tf_op jit(solution)/shard_map/all_gather | solution.py:129
  197.8 43.6 %all-gather.6.cloned.1.call-done = bf16[768,1,4096]{2,0,1:T(8,128)(2,1)} async-done(((bf16[24,1,4096]{2,0,1:T(8,128)(2,1)}), bf16[768,1,4096]{2,0,1:T(8,128)(2,1)}) %all-gather.6.cloned.1.call-update) | async-done | bytes 6291472 | tf_op jit(solution)/shard_map/all_gather | solution.py:128
  241.4 7.0 %fusion.3 = f32[768,448]{0,1:T(8,128)S(1)} fusion(bf16[768,1,4096]{2,0,1:T(8,128)(2,1)} %all-gather.6.cloned.1.call-done, bf16[1,4096,448]{1,2,0:T(8,128)(2,1)} %param.26), kind=kOutput, calls=%fused_computation.3 | convolution fusion | flops 2818572288 | bytes 11337728 | tf_op jit(solution)/shard_map/ned,edf->nf/dot_general | solution.py:131
  248.4 3.1 fusion.14
  251.9 0.5 fusion.66
  252.5 5.1 %convolution_add_fusion = f32[64,4096]{1,0:T(8,128)} fusion(f32[64,448]{1,0:T(8,128)S(1)} %reshape.513, bf16[1,448,4096]{2,1,0:T(8,128)(2,1)} %param.28, f32[4096]{0:T(1024)S(1)} %get-tuple-element.2, pred[64]{0:T(512)(128)(4,1)S(1)} %iota_compare_fusion.5), kind=kOutput, calls=%fused_computation.5 | convolution fusion | flops 1409810432 | bytes 4849728 | tf_op jit(solution)/shard_map/dot_general | solution.py:140
  257.8 28.6 %reduce-scatter.5.cloned.1.call-done = f32[64,512]{1,0:T(8,128)} async-done(((f32[64,4096]{1,0:T(8,128)}), f32[64,512]{1,0:T(8,128)}) %reduce-scatter.5.cloned.1.call-update) | async-done | bytes 131088 | tf_op jit(solution)/shard_map/reduce_scatter | solution.py:149
  286.4 147.8 %all-reduce.2.cloned.1.call-done = f32[64,512]{1,0:T(8,128)} async-done(((f32[64,512]{1,0:T(8,128)}), f32[64,512]{1,0:T(8,128)}) %all-reduce.2.cloned.1.call-update) | async-done | bytes 131088 | tf_op jit(solution)/shard_map/psum | solution.py:150
  434.3 1.0 multiply_reduce_fusion
  435.3 10.0 %psum.15 = f32[64]{0:T(128)S(1)} all-reduce(f32[64]{0:T(128)S(1)} %multiply_reduce_fusion), channel_id=1, replica_groups=mesh['dp'=32,'expert'=8] {'expert'}, use_global_device_ids=true, to_apply=%region_16.17 | all-reduce | flops 64 | bytes 512 | tf_op jit(solution)/shard_map/psum | solution.py:151
  445.3 1.0 multiply_convert_fusion
  446.3 1.3 fusion.61
  447.6 1.7 fusion.26
  (63 shorter events, 2.3 us)
Async XLA Ops:
  7.2 1.7 copy-start
  7.2 4.3 copy-start.8
  7.2 88.9 %all-gather.4.cloned.1.call-start = ((), (), s32[]{:S(2)}) async-start(), calls=%async_computation.4 | async-start | bytes 4325376 | tf_op jit(solution)/shard_map/all_gather | solution.py:84
  7.9 124.7 %reduce-scatter.3.cloned.1.call-start = ((), (), s32[]{:S(2)}) async-start(), calls=%async_computation.5 | async-start | bytes 1179648 | tf_op jit(solution)/shard_map/reduce_scatter | solution.py:87
  11.9 88.3 %copy-start.5 = (s32[8,2]{0,1:T(2,128)S(1)}, s32[8,2]{0,1:T(2,128)}, u32[]{:S(2)}) copy-start(s32[8,2]{0,1:T(2,128)} %param.25) | copy-start | bytes 196
  11.9 120.7 %copy-start.1 = (bf16[8,4096]{1,0:T(8,128)(2,1)S(1)}, bf16[8,4096]{1,0:T(8,128)(2,1)}, u32[]{:S(2)}) copy-start(bf16[8,4096]{1,0:T(8,128)(2,1)} %param.16) | copy-start | bytes 196612
  11.9 121.8 %copy-start.2 = (f32[4096]{0:T(1024)S(1)}, f32[4096]{0:T(1024)}, u32[]{:S(2)}) copy-start(f32[4096]{0:T(1024)} %param.23) | copy-start | bytes 49156
  96.1 56.6 %copy-start.9 = (bf16[4096,8]{0,1:T(8,128)(2,1)S(1)}, bf16[4096,8]{0,1:T(8,128)(2,1)}, u32[]{:S(2)}) copy-start(bf16[4096,8]{0,1:T(8,128)(2,1)} %param.24) | copy-start | bytes 196612
  100.8 34.8 %all-to-all-start = ((s32[8,1,8]{2,1,0:T(1,128)}), s32[8,1,8]{2,1,0:T(1,128)S(1)}, u32[]{:S(2)}, u32[]{:S(2)}) async-start(s32[8,1,8]{2,1,0:T(1,128)} %compare_select_fusion.1), calls=%async_computation | async-start | bytes 8192 | tf_op jit(solution)/shard_map/all_to_all | solution.py:100
  135.6 15.9 %all-to-all-start.1 = ((bf16[8,8,4096]{2,1,0:T(8,128)(2,1)}), bf16[8,8,4096]{2,1,0:T(8,128)(2,1)S(1)}, u32[]{:S(2)}, u32[]{:S(2)}) async-start(bf16[8,8,4096]{2,1,0:T(8,128)(2,1)} %broadcast_select_fusion), calls=%async_computation.2 | async-start | bytes 1048576 | tf_op jit(solution)/shard_map/all_to_all | solution.py:99
  142.6 98.8 %all-gather.6.cloned.1.call-start = ((), (), s32[]{:S(2)}) async-start(), calls=%async_computation.6 | async-start | bytes 6488064 | tf_op jit(solution)/shard_map/all_gather | solution.py:128
  152.4 134.0 %reduce-scatter.5.cloned.1.call-start = ((), (), s32[]{:S(2)}) async-start(), calls=%async_computation.7 | async-start | bytes 1179648 | tf_op jit(solution)/shard_map/reduce_scatter | solution.py:149
  241.4 7.1 %copy-start.6 = (bf16[768,1,4096]{2,0,1:T(8,128)(2,1)S(1)}, bf16[768,1,4096]{2,0,1:T(8,128)(2,1)}, u32[]{:S(2)}) copy-start(bf16[768,1,4096]{2,0,1:T(8,128)(2,1)} %all-gather.6.cloned.1.call-done) | copy-start | bytes 18874372
  241.4 7.1 %copy-start.7 = (bf16[1,4096,448]{1,2,0:T(8,128)(2,1)S(1)}, bf16[1,4096,448]{1,2,0:T(8,128)(2,1)}, u32[]{:S(2)}) copy-start(bf16[1,4096,448]{1,2,0:T(8,128)(2,1)} %param.27) | copy-start | bytes 11010052
  251.8 5.8 %copy-start.10 = (s32[64]{0:T(128)S(1)}, s32[64]{0:T(128)}, u32[]{:S(2)}) copy-start(s32[64]{0:T(128)} %param.31) | copy-start | bytes 772
  251.8 34.6 %copy-start.11 = (f32[4]{0:T(128)S(1)}, f32[4]{0:T(128)}, u32[]{:S(2)}) copy-start(f32[4]{0:T(128)} %param.30) | copy-start | bytes 52
  251.9 193.4 %copy-start.3 = (f32[512]{0:T(512)S(1)}, f32[512]{0:T(512)}, u32[]{:S(2)}) copy-start(f32[512]{0:T(512)} %param.29) | copy-start | bytes 6148
  257.6 176.6 %all-reduce.2.cloned.1.call-start = ((), (), s32[]{:S(2)}) async-start(), calls=%async_computation.8 | async-start | bytes 262144 | tf_op jit(solution)/shard_map/psum | solution.py:150
  446.3 3.0 copy-start.4
Sparse Core Ops, SparseCore 0:
  10.5 85.6 all-gather.3
  100.3 32.2 reduce-scatter.2
  152.5 88.8 all-gather.5
  257.7 28.6 reduce-scatter.4
  289.7 144.5 all-reduce.1

commit v2 on v1

--- a/solution.py
+++ b/solution.py
@@ -50,6 +50,14 @@
         "ckgts,cskd->ctkgd", fresh_weights, fresh_values, preferred_element_type=jnp.float32
     )
     return context.astype(jnp.bfloat16).reshape(span_count * window, kv_local * group * HD)
+
+
+def doubling_sum(x, axis, count):
+    step = 1
+    while step < count:
+        x = x + lax.ppermute(x, axis, [(a, a ^ step) for a in range(count)])
+        step *= 2
+    return x
 
 
 def shards(
@@ -147,8 +155,8 @@
         (jnp.arange(span_count) == own_span)[:, None], mixed_sum[None, :], 0.0
     )
     pooled_cols = lax.psum_scatter(pooled_part, "expert", scatter_dimension=1, tiled=True)
-    pooled_cols = lax.psum(pooled_cols, "dp")
-    squares = lax.psum(jnp.sum(pooled_cols * pooled_cols, axis=-1), "expert")
+    pooled_cols = doubling_sum(pooled_cols, "dp", n_dp)
+    squares = doubling_sum(jnp.sum(pooled_cols * pooled_cols, axis=-1), "expert", expert_count)
     everyone = (
         pooled_cols * lax.rsqrt(squares / width + EPSILON)[:, None] * summary_gain
     ).astype(jnp.bfloat16)

time: 460 us -> 347 us (0.75)
  waiting for transfers between devices: 339 us -> 222 us
  starting transfers between devices: 12 us -> 29.7 us
  blocking collectives: 53.9 us -> 43.9 us
    psum x1 -> x0, waiting for transfers between devices: 148 us -> none  [shards(): pooled_cols = lax.psum(pooled_cols, 'dp')]
    ppermute x0 -> x8, waiting for transfers between devices: none -> 30.7 us  [doubling_sum(): x = x + lax.ppermute(x, axis, [(a, a ^ step) for a in range(count)])]
    ppermute x0 -> x8, starting transfers between devices: none -> 17.8 us  [doubling_sum(): x = x + lax.ppermute(x, axis, [(a, a ^ step) for a in range(count)])]
    psum x1 -> x0, blocking collectives: 10 us -> none  [shards(): squares = lax.psum(jnp.sum(pooled_cols * pooled_cols, axis=-1), 'expert')]
  transfers between devices with their start and end apart: 7 -> 14, of which waited for: 6 -> 13; matrix products, arithmetic and copies ran while one was open for 2% -> 3% of each run, Pallas kernels for 0% -> 0%
where the time goes in v2:
time: 347 us; the launch traced here: 344 us
  waiting for transfers between devices  222 us (64%)
  blocking collectives  43.9 us (13%)
  starting transfers between devices  29.7 us (9%)
  matrix products  25.6 us (7%)
  between operations  14.1 us (4%)
  other arithmetic  6.35 us (2%)
    all_gather x1, waiting for transfers between devices, shards(): lax.all_gather(out_weight, 'dp', axis=1, tiled=True)  84.1 us
    all_gather x1, blocking collectives, shards(): gathered_weight = lax.all_gather(pool_weight, 'dp', axis=0, tiled=True)  43.9 us
    all_gather x1, waiting for transfers between devices, shards(): gathered = lax.all_gather(compact, 'dp', axis=0, tiled=True)  43.6 us
    ppermute x8, waiting for transfers between devices, doubling_sum(): x = x + lax.ppermute(x, axis, [(a, a ^ step) for a in range(count)])  30.7 us
    reduce_scatter x1, waiting for transfers between devices, shards(): lax.psum_scatter(pooled_part, 'expert', scatter_dimension=1, tiled=True)  28.8 us
    reduce_scatter x1, waiting for transfers between devices, shards(): lax.psum_scatter(head_terms, 'expert', scatter_dimension=0, tiled=True)  27 us
    ppermute x8, starting transfers between devices, doubling_sum(): x = x + lax.ppermute(x, axis, [(a, a ^ step) for a in range(count)])  17.8 us
    all_to_all x1, waiting for transfers between devices, shards(): lax.all_to_all(outgoing, 'expert', split_axis=0, concat_axis=1, tiled=True)  7.32 us
  transfers between devices with their start and end apart: 14, of which 13 were waited for; matrix products, arithmetic and copies ran while one was open for 3% of the time, Pallas kernels for 0%

profile of v2, /device:TPU:2, one launch (start us, length us, event | category | flops | bytes accessed | tf_op | source)
XLA Modules:
  0.0 344.1 jit_solution(10607632594380871506)
XLA Ops:
  9.2 1.0 fusion.60
  10.6 0.9 fusion.40
  12.0 84.1 %all-gather.4.cloned.1.call-done = bf16[512,4096]{1,0:T(8,128)(2,1)} async-done(((bf16[512,128]{1,0:T(8,128)(2,1)}), bf16[512,4096]{1,0:T(8,128)(2,1)}) %all-gather.4.cloned.1.call-update) | async-done | bytes 4194320 | tf_op jit(solution)/shard_map/all_gather | solution.py:92
  96.1 4.0 %fusion.35 = f32[64,4096]{1,0:T(8,128)} fusion(bf16[512,4096]{1,0:T(8,128)(2,1)} %all-gather.4.cloned.1.call-done, bf16[8,8,4,128]{3,2,1,0:T(4,128)(2,1)S(1)} %bitcast.123), kind=kOutput, calls=%fused_computation.44 | convolution fusion | flops 268435456 | bytes 5308416 | tf_op jit(solution)/shard_map/dot_general | solution.py:90
  100.8 4.8 %all-to-all-start = ((s32[8,1,8]{2,1,0:T(1,128)}), s32[8,1,8]{2,1,0:T(1,128)S(1)}, u32[]{:S(2)}, u32[]{:S(2)}) async-start(s32[8,1,8]{2,1,0:T(1,128)} %compare_select_fusion.1), calls=%async_computation | async-start | bytes 8192 | tf_op jit(solution)/shard_map/all_to_all | solution.py:108
  105.6 27.0 %reduce-scatter.3.cloned.1.call-done = f32[8,4096]{1,0:T(8,128)} async-done(((f32[64,4096]{1,0:T(8,128)}), f32[8,4096]{1,0:T(8,128)}) %reduce-scatter.3.cloned.1.call-update) | async-done | bytes 131088 | tf_op jit(solution)/shard_map/reduce_scatter | solution.py:95
  132.6 1.1 fusion.47
  133.7 1.0 multiply_convert_fusion.1
  135.6 7.0 %all-to-all-start.1 = ((bf16[8,8,4096]{2,1,0:T(8,128)(2,1)}), bf16[8,8,4096]{2,1,0:T(8,128)(2,1)S(1)}, u32[]{:S(2)}, u32[]{:S(2)}) async-start(bf16[8,8,4096]{2,1,0:T(8,128)(2,1)} %broadcast_select_fusion), calls=%async_computation.2 | async-start | bytes 1048576 | tf_op jit(solution)/shard_map/all_to_all | solution.py:107
  144.1 7.3 %all-to-all-done.1 = bf16[8,8,4096]{2,1,0:T(8,128)(2,1)S(1)} async-done(((bf16[8,8,4096]{2,1,0:T(8,128)(2,1)}), bf16[8,8,4096]{2,1,0:T(8,128)(2,1)S(1)}, u32[]{:S(2)}, u32[]{:S(2)}) %all-to-all-start.1) | async-done | bytes 524320 | tf_op jit(solution)/shard_map/all_to_all | solution.py:107
  152.7 1.1 select_reduce_fusion.2
  153.9 43.9 %all-gather = f32[32,24,2]{1,2,0:T(2,128)S(1)} all-gather(f32[1,24,2]{1,2,0:T(2,128)S(1)} %fusion.56), channel_id=1, replica_groups=mesh['dp'=32,'expert'=8] {'dp'}, dimensions={0}, use_global_device_ids=true | all-gather | bytes 6336 | tf_op jit(solution)/shard_map/all_gather | solution.py:137
  197.8 43.6 %all-gather.6.cloned.1.call-done = bf16[768,1,4096]{2,0,1:T(8,128)(2,1)} async-done(((bf16[24,1,4096]{2,0,1:T(8,128)(2,1)}), bf16[768,1,4096]{2,0,1:T(8,128)(2,1)}) %all-gather.6.cloned.1.call-update) | async-done | bytes 6291472 | tf_op jit(solution)/shard_map/all_gather | solution.py:136
  241.4 7.0 %fusion.3 = f32[768,448]{0,1:T(8,128)S(1)} fusion(bf16[768,1,4096]{2,0,1:T(8,128)(2,1)} %all-gather.6.cloned.1.call-done, bf16[1,4096,448]{1,2,0:T(8,128)(2,1)} %param.26), kind=kOutput, calls=%fused_computation.3 | convolution fusion | flops 2818572288 | bytes 11337728 | tf_op jit(solution)/shard_map/ned,edf->nf/dot_general | solution.py:139
  248.5 3.1 fusion.14
  252.5 5.1 %convolution_add_fusion = f32[64,4096]{1,0:T(8,128)} fusion(f32[64,448]{1,0:T(8,128)S(1)} %reshape.513, bf16[1,448,4096]{2,1,0:T(8,128)(2,1)} %param.28, f32[4096]{0:T(1024)S(1)} %get-tuple-element.2, pred[64]{0:T(512)(128)(4,1)S(1)} %iota_compare_fusion.5), kind=kOutput, calls=%fused_computation.5 | convolution fusion | flops 1409810432 | bytes 4849728 | tf_op jit(solution)/shard_map/dot_general | solution.py:148
  257.6 28.8 %reduce-scatter.5.cloned.1.call-done = f32[64,512]{1,0:T(8,128)} async-done(((f32[64,4096]{1,0:T(8,128)}), f32[64,512]{1,0:T(8,128)}) %reduce-scatter.5.cloned.1.call-update) | async-done | bytes 131088 | tf_op jit(solution)/shard_map/reduce_scatter | solution.py:157
  286.4 1.5 collective-permute-start
  287.9 3.7 %collective-permute-done = f32[64,512]{1,0:T(8,128)S(1)} collective-permute-done((f32[64,512]{1,0:T(8,128)}, f32[64,512]{1,0:T(8,128)S(1)}, u32[]{:S(2)}, u32[]{:S(2)}) %collective-permute-start) | collective-permute-done | bytes 131104 | tf_op jit(solution)/shard_map/ppermute | solution.py:58
  291.6 0.9 add.102
  292.5 3.3 collective-permute-start.1
  295.8 3.4 collective-permute-done.1
  299.3 1.7 collective-permute-start.2
  301.0 4.7 %collective-permute-done.2 = f32[64,512]{1,0:T(8,128)S(1)} collective-permute-done((f32[64,512]{1,0:T(8,128)S(1)}, f32[64,512]{1,0:T(8,128)S(1)}, u32[]{:S(2)}, u32[]{:S(2)}) %collective-permute-start.2) | collective-permute-done | bytes 131104 | tf_op jit(solution)/shard_map/ppermute | solution.py:58
  305.7 2.5 collective-permute-start.3
  308.2 7.7 %collective-permute-done.3 = f32[64,512]{1,0:T(8,128)S(1)} collective-permute-done((f32[64,512]{1,0:T(8,128)S(1)}, f32[64,512]{1,0:T(8,128)S(1)}, u32[]{:S(2)}, u32[]{:S(2)}) %collective-permute-start.3) | collective-permute-done | bytes 131104 | tf_op jit(solution)/shard_map/ppermute | solution.py:58
  315.9 5.4 %collective-permute-start.4 = (f32[64,512]{1,0:T(8,128)S(1)}, f32[64,512]{1,0:T(8,128)S(1)}, u32[]{:S(2)}, u32[]{:S(2)}) collective-permute-start(f32[64,512]{1,0:T(8,128)S(1)} %add.105), channel_id=1, source_target_pairs={{0,128},{8,136},{16,144},{24,152},{32,160},{40,168},{48,176},{56,1... | collective-permute-start | bytes 393224 | tf_op jit(solution)/shard_map/ppermute | solution.py:58
  321.2 3.6 %collective-permute-done.4 = f32[64,512]{1,0:T(8,128)S(1)} collective-permute-done((f32[64,512]{1,0:T(8,128)S(1)}, f32[64,512]{1,0:T(8,128)S(1)}, u32[]{:S(2)}, u32[]{:S(2)}) %collective-permute-start.4) | collective-permute-done | bytes 131104 | tf_op jit(solution)/shard_map/ppermute | solution.py:58
  325.1 1.1 collective-permute-done.5
  326.2 3.5 %collective-permute-start.6 = (f32[64]{0:T(128)S(1)}, f32[64]{0:T(128)S(1)}, u32[]{:S(2)}, u32[]{:S(2)}) collective-permute-start(f32[64]{0:T(128)S(1)} %add.107), channel_id=1, source_target_pairs={{0,2},{1,3},{2,0},{3,1},{4,6},{5,7},{6,4},{7,5},{8,10},{9,11},{10,... | collective-permute-start | bytes 776 | tf_op jit(solution)/shard_map/ppermute | solution.py:58
  329.7 1.5 collective-permute-done.6
  331.2 5.1 %collective-permute-done.7 = f32[64]{0:T(128)S(1)} collective-permute-done((f32[64]{0:T(128)S(1)}, f32[64]{0:T(128)S(1)}, u32[]{:S(2)}, u32[]{:S(2)}) %collective-permute-start.7) | collective-permute-done | bytes 288 | tf_op jit(solution)/shard_map/ppermute | solution.py:58
  (81 shorter events, 9.8 us)
Async XLA Ops:
  7.2 1.7 copy-start
  7.2 4.3 %copy-start.8 = (bf16[2,1024,128]{2,1,0:T(8,128)(2,1)S(1)}, bf16[2,1024,128]{2,1,0:T(8,128)(2,1)}, u32[]{:S(2)}) copy-start(bf16[2,1024,128]{2,1,0:T(8,128)(2,1)} %param.21) | copy-start | bytes 1572868
  7.2 88.9 %all-gather.4.cloned.1.call-start = ((), (), s32[]{:S(2)}) async-start(), calls=%async_computation.4 | async-start | bytes 4325376 | tf_op jit(solution)/shard_map/all_gather | solution.py:92
  7.9 124.7 %reduce-scatter.3.cloned.1.call-start = ((), (), s32[]{:S(2)}) async-start(), calls=%async_computation.5 | async-start | bytes 1179648 | tf_op jit(solution)/shard_map/reduce_scatter | solution.py:95
  11.9 88.3 %copy-start.5 = (s32[8,2]{0,1:T(2,128)S(1)}, s32[8,2]{0,1:T(2,128)}, u32[]{:S(2)}) copy-start(s32[8,2]{0,1:T(2,128)} %param.25) | copy-start | bytes 196
  11.9 120.7 %copy-start.1 = (bf16[8,4096]{1,0:T(8,128)(2,1)S(1)}, bf16[8,4096]{1,0:T(8,128)(2,1)}, u32[]{:S(2)}) copy-start(bf16[8,4096]{1,0:T(8,128)(2,1)} %param.16) | copy-start | bytes 196612
  11.9 121.8 %copy-start.2 = (f32[4096]{0:T(1024)S(1)}, f32[4096]{0:T(1024)}, u32[]{:S(2)}) copy-start(f32[4096]{0:T(1024)} %param.23) | copy-start | bytes 49156
  96.1 56.6 %copy-start.9 = (bf16[4096,8]{0,1:T(8,128)(2,1)S(1)}, bf16[4096,8]{0,1:T(8,128)(2,1)}, u32[]{:S(2)}) copy-start(bf16[4096,8]{0,1:T(8,128)(2,1)} %param.24) | copy-start | bytes 196612
  100.8 34.8 %all-to-all-start = ((s32[8,1,8]{2,1,0:T(1,128)}), s32[8,1,8]{2,1,0:T(1,128)S(1)}, u32[]{:S(2)}, u32[]{:S(2)}) async-start(s32[8,1,8]{2,1,0:T(1,128)} %compare_select_fusion.1), calls=%async_computation | async-start | bytes 8192 | tf_op jit(solution)/shard_map/all_to_all | solution.py:108
  135.6 15.9 %all-to-all-start.1 = ((bf16[8,8,4096]{2,1,0:T(8,128)(2,1)}), bf16[8,8,4096]{2,1,0:T(8,128)(2,1)S(1)}, u32[]{:S(2)}, u32[]{:S(2)}) async-start(bf16[8,8,4096]{2,1,0:T(8,128)(2,1)} %broadcast_select_fusion), calls=%async_computation.2 | async-start | bytes 1048576 | tf_op jit(solution)/shard_map/all_to_all | solution.py:107
  142.6 98.8 %all-gather.6.cloned.1.call-start = ((), (), s32[]{:S(2)}) async-start(), calls=%async_computation.6 | async-start | bytes 6488064 | tf_op jit(solution)/shard_map/all_gather | solution.py:136
  152.4 134.1 %reduce-scatter.5.cloned.1.call-start = ((), (), s32[]{:S(2)}) async-start(), calls=%async_computation.7 | async-start | bytes 1179648 | tf_op jit(solution)/shard_map/reduce_scatter | solution.py:157
  241.4 7.1 %copy-start.6 = (bf16[768,1,4096]{2,0,1:T(8,128)(2,1)S(1)}, bf16[768,1,4096]{2,0,1:T(8,128)(2,1)}, u32[]{:S(2)}) copy-start(bf16[768,1,4096]{2,0,1:T(8,128)(2,1)} %all-gather.6.cloned.1.call-done) | copy-start | bytes 18874372
  241.4 7.1 %copy-start.7 = (bf16[1,4096,448]{1,2,0:T(8,128)(2,1)S(1)}, bf16[1,4096,448]{1,2,0:T(8,128)(2,1)}, u32[]{:S(2)}) copy-start(bf16[1,4096,448]{1,2,0:T(8,128)(2,1)} %param.27) | copy-start | bytes 11010052
  252.5 72.6 %copy-start.10 = (s32[64]{0:T(128)S(1)}, s32[64]{0:T(128)}, u32[]{:S(2)}) copy-start(s32[64]{0:T(128)} %param.31) | copy-start | bytes 772
  252.5 78.7 %copy-start.11 = (f32[4]{0:T(128)S(1)}, f32[4]{0:T(128)}, u32[]{:S(2)}) copy-start(f32[4]{0:T(128)} %param.30) | copy-start | bytes 52
  252.5 83.8 %copy-start.3 = (f32[512]{0:T(512)S(1)}, f32[512]{0:T(512)}, u32[]{:S(2)}) copy-start(f32[512]{0:T(512)} %param.29) | copy-start | bytes 6148
  286.4 5.2 %collective-permute-start = (f32[64,512]{1,0:T(8,128)}, f32[64,512]{1,0:T(8,128)S(1)}, u32[]{:S(2)}, u32[]{:S(2)}) collective-permute-start(f32[64,512]{1,0:T(8,128)} %reduce-scatter.5.cloned.1.call-done), channel_id=1, source_target_pairs={{0,8},{8,0},{16,24},{24,16},{32,40},{40,32},{48,56},{56,48},{64,72... | collective-permute-start | bytes 393224 | tf_op jit(solution)/shard_map/ppermute | solution.py:58
  292.5 6.7 %collective-permute-start.1 = (f32[64,512]{1,0:T(8,128)S(1)}, f32[64,512]{1,0:T(8,128)S(1)}, u32[]{:S(2)}, u32[]{:S(2)}) collective-permute-start(f32[64,512]{1,0:T(8,128)S(1)} %add.102), channel_id=1, source_target_pairs={{0,16},{8,24},{16,0},{24,8},{32,48},{40,56},{48,32},{56,40},{64,80... | collective-permute-start | bytes 393224 | tf_op jit(solution)/shard_map/ppermute | solution.py:58
  299.3 6.4 %collective-permute-start.2 = (f32[64,512]{1,0:T(8,128)S(1)}, f32[64,512]{1,0:T(8,128)S(1)}, u32[]{:S(2)}, u32[]{:S(2)}) collective-permute-start(f32[64,512]{1,0:T(8,128)S(1)} %add.103), channel_id=1, source_target_pairs={{0,32},{8,40},{16,48},{24,56},{32,0},{40,8},{48,16},{56,24},{64,96... | collective-permute-start | bytes 393224 | tf_op jit(solution)/shard_map/ppermute | solution.py:58
  305.7 10.2 %collective-permute-start.3 = (f32[64,512]{1,0:T(8,128)S(1)}, f32[64,512]{1,0:T(8,128)S(1)}, u32[]{:S(2)}, u32[]{:S(2)}) collective-permute-start(f32[64,512]{1,0:T(8,128)S(1)} %add.104), channel_id=1, source_target_pairs={{0,64},{8,72},{16,80},{24,88},{32,96},{40,104},{48,112},{56,120},{... | collective-permute-start | bytes 393224 | tf_op jit(solution)/shard_map/ppermute | solution.py:58
  315.9 9.0 %collective-permute-start.4 = (f32[64,512]{1,0:T(8,128)S(1)}, f32[64,512]{1,0:T(8,128)S(1)}, u32[]{:S(2)}, u32[]{:S(2)}) collective-permute-start(f32[64,512]{1,0:T(8,128)S(1)} %add.105), channel_id=1, source_target_pairs={{0,128},{8,136},{16,144},{24,152},{32,160},{40,168},{48,176},{56,1... | collective-permute-start | bytes 393224 | tf_op jit(solution)/shard_map/ppermute | solution.py:58
  325.0 1.2 collective-permute-start.5
  326.2 5.0 %collective-permute-start.6 = (f32[64]{0:T(128)S(1)}, f32[64]{0:T(128)S(1)}, u32[]{:S(2)}, u32[]{:S(2)}) collective-permute-start(f32[64]{0:T(128)S(1)} %add.107), channel_id=1, source_target_pairs={{0,2},{1,3},{2,0},{3,1},{4,6},{5,7},{6,4},{7,5},{8,10},{9,11},{10,... | collective-permute-start | bytes 776 | tf_op jit(solution)/shard_map/ppermute | solution.py:58
  331.2 5.1 %collective-permute-start.7 = (f32[64]{0:T(128)S(1)}, f32[64]{0:T(128)S(1)}, u32[]{:S(2)}, u32[]{:S(2)}) collective-permute-start(f32[64]{0:T(128)S(1)} %add.108), channel_id=1, source_target_pairs={{0,4},{1,5},{2,6},{3,7},{4,0},{5,1},{6,2},{7,3},{8,12},{9,13},{10,... | collective-permute-start | bytes 776 | tf_op jit(solution)/shard_map/ppermute | solution.py:58
  336.4 1.2 copy-start.4
Sparse Core Ops, SparseCore 0:
  10.5 85.6 all-gather.3
  100.3 32.2 reduce-scatter.2
  152.5 88.8 all-gather.5
  257.8 28.6 reduce-scatter.4

commit v3 on v2

--- a/solution.py
+++ b/solution.py
@@ -50,6 +50,18 @@
         "ckgts,cskd->ctkgd", fresh_weights, fresh_values, preferred_element_type=jnp.float32
     )
     return context.astype(jnp.bfloat16).reshape(span_count * window, kv_local * group * HD)
+
+
+def a2a_sum(x, axis, dim, count):
+    shape = x.shape
+    split = shape[:dim] + (count, shape[dim] // count) + shape[dim + 1:]
+    received = lax.all_to_all(x.reshape(split), axis, split_axis=dim, concat_axis=dim, tiled=True)
+    return jnp.sum(received, axis=dim)
+
+
+def a2a_gather(x, axis, count):
+    spread = jnp.broadcast_to(x[None], (count,) + x.shape)
+    return lax.all_to_all(spread, axis, split_axis=0, concat_axis=0, tiled=True)
 
 
 def doubling_sum(x, axis, count):
@@ -87,14 +99,12 @@
     slice_width = width // expert_count
     highest_precision = lax.Precision.HIGHEST
     attended = attend(queries, new_keys, new_values, cache_keys, cache_values)
-    head_terms = jnp.dot(
-        attended,
-        lax.all_gather(out_weight, "dp", axis=1, tiled=True),
-        preferred_element_type=jnp.float32,
-    )
-    mixed = residual.astype(jnp.float32) + lax.psum_scatter(
-        head_terms, "expert", scatter_dimension=0, tiled=True
-    )
+    n_dp = lax.axis_size("dp")
+    weight_blocks = a2a_gather(out_weight, "dp", n_dp)
+    head_terms = jnp.einsum(
+        "th,shc->tsc", attended, weight_blocks, preferred_element_type=jnp.float32
+    ).reshape(attended.shape[0], width)
+    mixed = residual.astype(jnp.float32) + a2a_sum(head_terms, "expert", 0, expert_count)
     normed = (
         mixed * lax.rsqrt(jnp.mean(mixed * mixed, axis=-1, keepdims=True) + EPSILON) * ffn_gain
     ).astype(jnp.bfloat16)
@@ -133,9 +143,8 @@
     pool_weight = jnp.where(
         slot_span[:, None] == jnp.arange(span_local)[None, :], slot_gate[:, None], 0.0
     )
-    gathered = lax.all_gather(compact, "dp", axis=0, tiled=True)
-    gathered_weight = lax.all_gather(pool_weight, "dp", axis=0, tiled=True)
-    n_dp = gathered.shape[0] // GROUP_CAP
+    gathered = a2a_gather(compact, "dp", n_dp).reshape((n_dp * GROUP_CAP,) + compact.shape[1:])
+    gathered_weight = a2a_gather(pool_weight, "dp", n_dp)
     gate_proj = jnp.einsum("ned,edf->nf", gathered, w_gate, preferred_element_type=jnp.float32)
     up_proj = jnp.einsum("ned,edf->nf", gathered, w_up, preferred_element_type=jnp.float32)
     hidden = (jax.nn.silu(gate_proj) * up_proj).astype(jnp.bfloat16)
@@ -154,7 +163,7 @@
     pooled_part = pooled_part + jnp.where(
         (jnp.arange(span_count) == own_span)[:, None], mixed_sum[None, :], 0.0
     )
-    pooled_cols = lax.psum_scatter(pooled_part, "expert", scatter_dimension=1, tiled=True)
+    pooled_cols = a2a_sum(pooled_part, "expert", 1, expert_count)
     pooled_cols = doubling_sum(pooled_cols, "dp", n_dp)
     squares = doubling_sum(jnp.sum(pooled_cols * pooled_cols, axis=-1), "expert", expert_count)
     everyone = (

time: 347 us -> 407 us (1.17)
  waiting for transfers between devices: 222 us -> 287 us
  starting transfers between devices: 29.7 us -> 61 us
  blocking collectives: 43.9 us -> 18.6 us
  between operations: 14.1 us -> 1.06 us
  local copies, waits for them, and re-layouts: 2.09 us -> 8.93 us
    all_to_all x0 -> x4, waiting for transfers between devices: none -> 247 us  [the longest x3 233 us: a2a_gather(): return lax.all_to_all(spread, axis, split_axis=0, concat_axis=0, tiled=True)]
    all_gather x2 -> x0, waiting for transfers between devices: 128 us -> none  [the longest x1 84.1 us: shards(): lax.all_gather(out_weight, 'dp', axis=1, tiled=True)]
    reduce_scatter x2 -> x0, waiting for transfers between devices: 55.7 us -> none  [the longest x1 28.8 us: shards(): lax.psum_scatter(pooled_part, 'expert', scatter_dimension=1, tiled=True)]
    all_gather x1 -> x0, blocking collectives: 43.9 us -> none  [shards(): gathered_weight = lax.all_gather(pool_weight, 'dp', axis=0, tiled=True)]
    all_to_all x0 -> x4, starting transfers between devices: none -> 34.9 us  [the longest x3 30.1 us: a2a_gather(): return lax.all_to_all(spread, axis, split_axis=0, concat_axis=0, tiled=True)]
    all_to_all x0 -> x1, blocking collectives: none -> 18.6 us  [a2a_sum(): lax.all_to_all(x.reshape(split), axis, split_axis=dim, concat_axis=dim, t...]
    broadcast_in_dim x0 -> x3, local copies, waits for them, and re-layouts: none -> 6.49 us  [a2a_gather(): spread = jnp.broadcast_to(x[None], (count,) + x.shape)]
  transfers between devices with their start and end apart: 14 -> 14, of which waited for: 13 -> 13; matrix products, arithmetic and copies ran while one was open for 3% -> 5% of each run, Pallas kernels for 0% -> 0%
where the time goes in v3:
time: 407 us; the launch traced here: 405 us
  waiting for transfers between devices  287 us (71%)
  starting transfers between devices  61 us (15%)
  matrix products  24.9 us (6%)
  blocking collectives  18.6 us (5%)
  local copies, waits for them, and re-layouts  8.93 us (2%)
    all_to_all x3, waiting for transfers between devices, a2a_gather(): return lax.all_to_all(spread, axis, split_axis=0, concat_axis=0, tiled=True)  233 us
    ppermute x8, waiting for transfers between devices, doubling_sum(): x = x + lax.ppermute(x, axis, [(a, a ^ step) for a in range(count)])  30.6 us
    all_to_all x3, starting transfers between devices, a2a_gather(): return lax.all_to_all(spread, axis, split_axis=0, concat_axis=0, tiled=True)  30.1 us
    all_to_all x1, blocking collectives, a2a_sum(): lax.all_to_all(x.reshape(split), axis, split_axis=dim, concat_axis=dim, t...  18.6 us
    ppermute x8, starting transfers between devices, doubling_sum(): x = x + lax.ppermute(x, axis, [(a, a ^ step) for a in range(count)])  16.5 us
    all_to_all x1, waiting for transfers between devices, a2a_sum(): lax.all_to_all(x.reshape(split), axis, split_axis=dim, concat_axis=dim, t...  13.9 us
  transfers between devices with their start and end apart: 14, of which 13 were waited for; matrix products, arithmetic and copies ran while one was open for 5% of the time, Pallas kernels for 0%

profile of v3, /device:TPU:2, one launch (start us, length us, event | category | flops | bytes accessed | tf_op | source)
XLA Modules:
  0.0 405.4 jit_solution(1418259613323953156)
XLA Ops:
  1.7 2.4 broadcast_in_dim.192
  4.2 11.7 %all-to-all-start.1 = ((bf16[32,512,128]{1,2,0:T(8,128)(2,1)}), bf16[32,512,128]{1,2,0:T(8,128)(2,1)}, u32[]{:S(2)}, u32[]{:S(2)}) async-start(bf16[32,512,128]{1,2,0:T(8,128)(2,1)} %broadcast_in_dim.192), calls=%async_computation.1 | async-start | bytes 8388608 | tf_op jit(solution)/shard_map/all_to_all | solution.py:64
  17.7 92.5 %all-to-all-done.1 = bf16[32,512,128]{1,2,0:T(8,128)(2,1)} async-done(((bf16[32,512,128]{1,2,0:T(8,128)(2,1)}), bf16[32,512,128]{1,2,0:T(8,128)(2,1)}, u32[]{:S(2)}, u32[]{:S(2)}) %all-to-all-start.1) | async-done | bytes 4194336 | tf_op jit(solution)/shard_map/all_to_all | solution.py:64
  110.2 4.6 %fusion.55 = f32[8,8,4096]{2,1,0:T(8,128)} fusion(bf16[8,8,512]{2,1,0:T(8,128)(2,1)S(1)} %dot_general.49, bf16[4096,512,1]{1,0,2:T(8,128)(2,1)} %bitcast.24), kind=kOutput, calls=%fused_computation.95 | convolution fusion | flops 268435456 | bytes 5308416 | tf_op jit(solution)/shard_map/th,shc->tsc/dot_general | solution.py:104
  114.8 4.8 %all-to-all-start.2 = ((f32[8,8,4096]{2,1,0:T(8,128)}), f32[8,8,4096]{2,1,0:T(8,128)S(1)}, u32[]{:S(2)}, u32[]{:S(2)}) async-start(f32[8,8,4096]{2,1,0:T(8,128)} %fusion.55), calls=%async_computation.2 | async-start | bytes 2097152 | tf_op jit(solution)/shard_map/all_to_all | solution.py:58
  120.2 13.9 %all-to-all-done.2 = f32[8,8,4096]{2,1,0:T(8,128)S(1)} async-done(((f32[8,8,4096]{2,1,0:T(8,128)}), f32[8,8,4096]{2,1,0:T(8,128)S(1)}, u32[]{:S(2)}, u32[]{:S(2)}) %all-to-all-start.2) | async-done | bytes 1048608 | tf_op jit(solution)/shard_map/all_to_all | solution.py:58
  134.1 4.7 %all-to-all-start = ((s32[8,1,8]{2,1,0:T(1,128)}), s32[8,1,8]{2,1,0:T(1,128)S(1)}, u32[]{:S(2)}, u32[]{:S(2)}) async-start(s32[8,1,8]{2,1,0:T(1,128)} %compare_select_fusion.1), calls=%async_computation | async-start | bytes 8192 | tf_op jit(solution)/shard_map/all_to_all | solution.py:118
  140.0 2.6 all-to-all-done
  142.7 4.9 %all-to-all-start.3 = ((bf16[8,8,4096]{2,1,0:T(8,128)(2,1)}), bf16[8,8,4096]{2,1,0:T(8,128)(2,1)S(1)}, u32[]{:S(2)}, u32[]{:S(2)}) async-start(bf16[8,8,4096]{2,1,0:T(8,128)(2,1)} %broadcast_select_fusion), calls=%async_computation.3 | async-start | bytes 1048576 | tf_op jit(solution)/shard_map/all_to_all | solution.py:117
  149.1 7.3 %all-to-all-done.3 = bf16[8,8,4096]{2,1,0:T(8,128)(2,1)S(1)} async-done(((bf16[8,8,4096]{2,1,0:T(8,128)(2,1)}), bf16[8,8,4096]{2,1,0:T(8,128)(2,1)S(1)}, u32[]{:S(2)}, u32[]{:S(2)}) %all-to-all-start.3) | async-done | bytes 524320 | tf_op jit(solution)/shard_map/all_to_all | solution.py:117
  156.6 3.4 broadcast_in_dim.201
  160.0 7.1 %all-to-all-start.5 = ((bf16[32,24,1,4096]{3,1,2,0:T(8,128)(2,1)}), bf16[32,24,1,4096]{3,1,2,0:T(8,128)(2,1)}, u32[]{:S(2)}, u32[]{:S(2)}) async-start(bf16[32,24,1,4096]{3,1,2,0:T(8,128)(2,1)} %broadcast_in_dim.201), calls=%async_computation.5 | async-start | bytes 12582912 | tf_op jit(solution)/shard_map/all_to_all | solution.py:64
  167.7 140.3 %all-to-all-done.5 = bf16[32,24,1,4096]{3,1,2,0:T(8,128)(2,1)} async-done(((bf16[32,24,1,4096]{3,1,2,0:T(8,128)(2,1)}), bf16[32,24,1,4096]{3,1,2,0:T(8,128)(2,1)}, u32[]{:S(2)}, u32[]{:S(2)}) %all-to-all-start.5) | async-done | bytes 6291488 | tf_op jit(solution)/shard_map/all_to_all | solution.py:64
  308.6 11.2 %all-to-all-start.4 = ((f32[32,24,2]{1,2,0:T(2,128)}), f32[32,24,2]{1,2,0:T(2,128)S(1)}, u32[]{:S(2)}, u32[]{:S(2)}) async-start(f32[32,24,2]{1,2,0:T(2,128)} %broadcast_in_dim.200), calls=%async_computation.4 | async-start | bytes 65536 | tf_op jit(solution)/shard_map/all_to_all | solution.py:64
  319.8 7.0 %fusion.5 = f32[768,448]{0,1:T(8,128)S(1)} fusion(bf16[768,4096]{1,0:T(8,128)(2,1)} %bitcast.31, bf16[1,4096,448]{1,2,0:T(8,128)(2,1)} %param.26), kind=kOutput, calls=%fused_computation.7 | convolution fusion | flops 2818572288 | bytes 11337728 | tf_op jit(solution)/shard_map/ned,edf->nf/dot_general | solution.py:148
  326.9 5.9 %fusion.11 = bf16[768,448]{0,1:T(8,128)(2,1)S(1)} fusion(bf16[768,4096]{1,0:T(8,128)(2,1)} %bitcast.31, bf16[1,4096,448]{1,2,0:T(8,128)(2,1)S(1)} %copy-done.8, f32[768,448]{0,1:T(8,128)S(1)} %fusion.5), kind=kOutput, calls=%fused_computation.12 | convolution fusion | flops 2820636672 | bytes 12025856 | tf_op jit(solution)/shard_map/ned,edf->nf/dot_general | solution.py:149
  333.7 4.1 %convolution_add_fusion = f32[64,4096]{1,0:T(8,128)S(1)} fusion(f32[64,448]{1,0:T(8,128)S(1)} %reshape.549, bf16[1,448,4096]{2,1,0:T(8,128)(2,1)} %param.28, f32[4096]{0:T(1024)S(1)} %get-tuple-element.2, pred[64]{0:T(512)(128)(4,1)S(1)} %iota_compare_fusion.5), kind=kOutput, calls=%fused_computation.1 | convolution fusion | flops 1409810432 | bytes 4849728 | tf_op jit(solution)/shard_map/dot_general | solution.py:157
  337.9 18.6 %all_to_all.47 = f32[64,8,512]{2,0,1:T(8,128)S(1)} all-to-all(f32[64,8,512]{2,0,1:T(8,128)S(1)} %bitcast.118), channel_id=1, replica_groups=mesh['dp'=32,'expert'=8] {'expert'}, dimensions={1} | all-to-all | bytes 2097152 | tf_op jit(solution)/shard_map/all_to_all | solution.py:58
  356.6 1.7 collective-permute-start
  358.3 3.3 collective-permute-done
  361.7 3.2 collective-permute-start.1
  364.9 3.4 collective-permute-done.1
  368.3 1.7 collective-permute-start.2
  370.0 4.7 %collective-permute-done.2 = f32[64,512]{1,0:T(8,128)S(1)} collective-permute-done((f32[64,512]{1,0:T(8,128)S(1)}, f32[64,512]{1,0:T(8,128)S(1)}, u32[]{:S(2)}, u32[]{:S(2)}) %collective-permute-start.2) | collective-permute-done | bytes 131104 | tf_op jit(solution)/shard_map/ppermute | solution.py:70
  374.7 2.5 collective-permute-start.3
  377.3 6.5 %collective-permute-done.3 = f32[64,512]{1,0:T(8,128)S(1)} collective-permute-done((f32[64,512]{1,0:T(8,128)S(1)}, f32[64,512]{1,0:T(8,128)S(1)}, u32[]{:S(2)}, u32[]{:S(2)}) %collective-permute-start.3) | collective-permute-done | bytes 131104 | tf_op jit(solution)/shard_map/ppermute | solution.py:70
  383.7 4.5 %collective-permute-start.4 = (f32[64,512]{1,0:T(8,128)S(1)}, f32[64,512]{1,0:T(8,128)S(1)}, u32[]{:S(2)}, u32[]{:S(2)}) collective-permute-start(f32[64,512]{1,0:T(8,128)S(1)} %add.101), channel_id=1, source_target_pairs={{0,128},{8,136},{16,144},{24,152},{32,160},{40,168},{48,176},{56,1... | collective-permute-start | bytes 393224 | tf_op jit(solution)/shard_map/ppermute | solution.py:70
  388.3 5.8 %collective-permute-done.4 = f32[64,512]{1,0:T(8,128)S(1)} collective-permute-done((f32[64,512]{1,0:T(8,128)S(1)}, f32[64,512]{1,0:T(8,128)S(1)}, u32[]{:S(2)}, u32[]{:S(2)}) %collective-permute-start.4) | collective-permute-done | bytes 131104 | tf_op jit(solution)/shard_map/ppermute | solution.py:70
  395.5 1.4 collective-permute-start.6
  396.9 2.1 collective-permute-done.6
  399.0 1.4 collective-permute-start.7
  400.4 3.7 collective-permute-done.7
  (89 shorter events, 11.3 us)
Async XLA Ops:
  0.6 15.4 %copy-start = (bf16[2,1024,128]{2,1,0:T(8,128)(2,1)S(1)}, bf16[2,1024,128]{2,1,0:T(8,128)(2,1)}, u32[]{:S(2)}) copy-start(bf16[2,1024,128]{2,1,0:T(8,128)(2,1)} %param.20) | copy-start | bytes 1572868
  4.2 11.8 %copy-start.2 = (bf16[64,512]{1,0:T(8,128)(2,1)S(1)}, bf16[64,512]{1,0:T(8,128)(2,1)}, u32[]{:S(2)}) copy-start(bf16[64,512]{1,0:T(8,128)(2,1)} %param.17) | copy-start | bytes 196612
  4.2 12.2 %copy-start.3 = (bf16[64,128]{1,0:T(8,128)(2,1)S(1)}, bf16[64,128]{1,0:T(8,128)(2,1)}, u32[]{:S(2)}) copy-start(bf16[64,128]{1,0:T(8,128)(2,1)} %param.18) | copy-start | bytes 49156
  4.2 12.8 %copy-start.11 = (bf16[64,128]{1,0:T(8,128)(2,1)S(1)}, bf16[64,128]{1,0:T(8,128)(2,1)}, u32[]{:S(2)}) copy-start(bf16[64,128]{1,0:T(8,128)(2,1)} %param.19) | copy-start | bytes 49156
  4.2 106.0 %all-to-all-start.1 = ((bf16[32,512,128]{1,2,0:T(8,128)(2,1)}), bf16[32,512,128]{1,2,0:T(8,128)(2,1)}, u32[]{:S(2)}, u32[]{:S(2)}) async-start(bf16[32,512,128]{1,2,0:T(8,128)(2,1)} %broadcast_in_dim.192), calls=%async_computation.1 | async-start | bytes 8388608 | tf_op jit(solution)/shard_map/all_to_all | solution.py:64
  15.9 1.3 copy-start.9
  110.2 9.4 %copy-start.7 = (s32[8,2]{0,1:T(2,128)S(1)}, s32[8,2]{0,1:T(2,128)}, u32[]{:S(2)}) copy-start(s32[8,2]{0,1:T(2,128)} %param.25) | copy-start | bytes 196
  110.2 28.7 %copy-start.1 = (bf16[8,4096]{1,0:T(8,128)(2,1)S(1)}, bf16[8,4096]{1,0:T(8,128)(2,1)}, u32[]{:S(2)}) copy-start(bf16[8,4096]{1,0:T(8,128)(2,1)} %param.16) | copy-start | bytes 196612
  110.2 28.8 %copy-start.4 = (f32[4096]{0:T(1024)S(1)}, f32[4096]{0:T(1024)}, u32[]{:S(2)}) copy-start(f32[4096]{0:T(1024)} %param.23) | copy-start | bytes 49156
  114.8 19.3 %all-to-all-start.2 = ((f32[8,8,4096]{2,1,0:T(8,128)}), f32[8,8,4096]{2,1,0:T(8,128)S(1)}, u32[]{:S(2)}, u32[]{:S(2)}) async-start(f32[8,8,4096]{2,1,0:T(8,128)} %fusion.55), calls=%async_computation.2 | async-start | bytes 2097152 | tf_op jit(solution)/shard_map/all_to_all | solution.py:58
  134.1 8.6 %all-to-all-start = ((s32[8,1,8]{2,1,0:T(1,128)}), s32[8,1,8]{2,1,0:T(1,128)S(1)}, u32[]{:S(2)}, u32[]{:S(2)}) async-start(s32[8,1,8]{2,1,0:T(1,128)} %compare_select_fusion.1), calls=%async_computation | async-start | bytes 8192 | tf_op jit(solution)/shard_map/all_to_all | solution.py:118
  142.7 13.7 %all-to-all-start.3 = ((bf16[8,8,4096]{2,1,0:T(8,128)(2,1)}), bf16[8,8,4096]{2,1,0:T(8,128)(2,1)S(1)}, u32[]{:S(2)}, u32[]{:S(2)}) async-start(bf16[8,8,4096]{2,1,0:T(8,128)(2,1)} %broadcast_select_fusion), calls=%async_computation.3 | async-start | bytes 1048576 | tf_op jit(solution)/shard_map/all_to_all | solution.py:117
  160.0 7.4 %copy-start.10 = (bf16[4096,8]{0,1:T(8,128)(2,1)S(1)}, bf16[4096,8]{0,1:T(8,128)(2,1)}, u32[]{:S(2)}) copy-start(bf16[4096,8]{0,1:T(8,128)(2,1)} %param.24) | copy-start | bytes 196612
  160.0 148.0 %all-to-all-start.5 = ((bf16[32,24,1,4096]{3,1,2,0:T(8,128)(2,1)}), bf16[32,24,1,4096]{3,1,2,0:T(8,128)(2,1)}, u32[]{:S(2)}, u32[]{:S(2)}) async-start(bf16[32,24,1,4096]{3,1,2,0:T(8,128)(2,1)} %broadcast_in_dim.201), calls=%async_computation.5 | async-start | bytes 12582912 | tf_op jit(solution)/shard_map/all_to_all | solution.py:64
  308.6 24.5 %all-to-all-start.4 = ((f32[32,24,2]{1,2,0:T(2,128)}), f32[32,24,2]{1,2,0:T(2,128)S(1)}, u32[]{:S(2)}, u32[]{:S(2)}) async-start(f32[32,24,2]{1,2,0:T(2,128)} %broadcast_in_dim.200), calls=%async_computation.4 | async-start | bytes 65536 | tf_op jit(solution)/shard_map/all_to_all | solution.py:64
  319.8 7.1 %copy-start.8 = (bf16[1,4096,448]{1,2,0:T(8,128)(2,1)S(1)}, bf16[1,4096,448]{1,2,0:T(8,128)(2,1)}, u32[]{:S(2)}) copy-start(bf16[1,4096,448]{1,2,0:T(8,128)(2,1)} %param.27) | copy-start | bytes 11010052
  337.8 56.5 %copy-start.12 = (s32[64]{0:T(128)S(1)}, s32[64]{0:T(128)}, u32[]{:S(2)}) copy-start(s32[64]{0:T(128)} %param.31) | copy-start | bytes 772
  337.8 62.6 %copy-start.13 = (f32[4]{0:T(128)S(1)}, f32[4]{0:T(128)}, u32[]{:S(2)}) copy-start(f32[4]{0:T(128)} %param.30) | copy-start | bytes 52
  337.8 66.3 %copy-start.5 = (f32[512]{0:T(512)S(1)}, f32[512]{0:T(512)}, u32[]{:S(2)}) copy-start(f32[512]{0:T(512)} %param.29) | copy-start | bytes 6148
  356.6 5.1 %collective-permute-start = (f32[64,512]{1,0:T(8,128)S(1)}, f32[64,512]{1,0:T(8,128)S(1)}, u32[]{:S(2)}, u32[]{:S(2)}) collective-permute-start(f32[64,512]{1,0:T(8,128)S(1)} %reduce_sum.117), channel_id=1, source_target_pairs={{0,8},{8,0},{16,24},{24,16},{32,40},{40,32},{48,56},{56,48},{64,72... | collective-permute-start | bytes 393224 | tf_op jit(solution)/shard_map/ppermute | solution.py:70
  361.7 6.6 %collective-permute-start.1 = (f32[64,512]{1,0:T(8,128)S(1)}, f32[64,512]{1,0:T(8,128)S(1)}, u32[]{:S(2)}, u32[]{:S(2)}) collective-permute-start(f32[64,512]{1,0:T(8,128)S(1)} %add.98), channel_id=1, source_target_pairs={{0,16},{8,24},{16,0},{24,8},{32,48},{40,56},{48,32},{56,40},{64,80... | collective-permute-start | bytes 393224 | tf_op jit(solution)/shard_map/ppermute | solution.py:70
  368.3 6.4 %collective-permute-start.2 = (f32[64,512]{1,0:T(8,128)S(1)}, f32[64,512]{1,0:T(8,128)S(1)}, u32[]{:S(2)}, u32[]{:S(2)}) collective-permute-start(f32[64,512]{1,0:T(8,128)S(1)} %add.99), channel_id=1, source_target_pairs={{0,32},{8,40},{16,48},{24,56},{32,0},{40,8},{48,16},{56,24},{64,96... | collective-permute-start | bytes 393224 | tf_op jit(solution)/shard_map/ppermute | solution.py:70
  374.7 9.0 %collective-permute-start.3 = (f32[64,512]{1,0:T(8,128)S(1)}, f32[64,512]{1,0:T(8,128)S(1)}, u32[]{:S(2)}, u32[]{:S(2)}) collective-permute-start(f32[64,512]{1,0:T(8,128)S(1)} %add.100), channel_id=1, source_target_pairs={{0,64},{8,72},{16,80},{24,88},{32,96},{40,104},{48,112},{56,120},{... | collective-permute-start | bytes 393224 | tf_op jit(solution)/shard_map/ppermute | solution.py:70
  383.7 10.4 %collective-permute-start.4 = (f32[64,512]{1,0:T(8,128)S(1)}, f32[64,512]{1,0:T(8,128)S(1)}, u32[]{:S(2)}, u32[]{:S(2)}) collective-permute-start(f32[64,512]{1,0:T(8,128)S(1)} %add.101), channel_id=1, source_target_pairs={{0,128},{8,136},{16,144},{24,152},{32,160},{40,168},{48,176},{56,1... | collective-permute-start | bytes 393224 | tf_op jit(solution)/shard_map/ppermute | solution.py:70
  394.2 1.2 collective-permute-start.5
  395.5 3.6 collective-permute-start.6
  399.0 5.1 %collective-permute-start.7 = (f32[64]{0:T(128)S(1)}, f32[64]{0:T(128)S(1)}, u32[]{:S(2)}, u32[]{:S(2)}) collective-permute-start(f32[64]{0:T(128)S(1)} %add.104), channel_id=1, source_target_pairs={{0,4},{1,5},{2,6},{3,7},{4,0},{5,1},{6,2},{7,3},{8,12},{9,13},{10,... | collective-permute-start | bytes 776 | tf_op jit(solution)/shard_map/ppermute | solution.py:70
  404.2 1.2 copy-start.6

commit v4 on v2

--- a/solution.py
+++ b/solution.py
@@ -14,6 +14,7 @@
 
 
 EPSILON = 1e-05
+DP = ("z", "y")
 
 
 def attend(queries, new_keys, new_values, cache_keys, cache_values):
@@ -50,6 +51,17 @@
         "ckgts,cskd->ctkgd", fresh_weights, fresh_values, preferred_element_type=jnp.float32
     )
     return context.astype(jnp.bfloat16).reshape(span_count * window, kv_local * group * HD)
+
+
+def a2a_sum(x, axis, dim, count):
+    shape = x.shape
+    split = shape[:dim] + (count, shape[dim] // count) + shape[dim + 1:]
+    received = lax.all_to_all(x.reshape(split), axis, split_axis=dim, concat_axis=dim, tiled=True)
+    return jnp.sum(received, axis=dim)
+
+
+def dp_gather(x, axis):
+    return lax.all_gather(lax.all_gather(x, "y", axis=axis, tiled=True), "z", axis=axis, tiled=True)
 
 
 def doubling_sum(x, axis, count):
@@ -79,7 +91,7 @@
     assign,
 ):
     expert_count = lax.axis_size("expert")
-    dp_index = lax.axis_index("dp")
+    dp_index = lax.axis_index(DP)
     column = lax.axis_index("expert")
     span_local = cache_keys.shape[0]
     tok_local = residual.shape[0]
@@ -89,12 +101,10 @@
     attended = attend(queries, new_keys, new_values, cache_keys, cache_values)
     head_terms = jnp.dot(
         attended,
-        lax.all_gather(out_weight, "dp", axis=1, tiled=True),
+        dp_gather(out_weight, 1),
         preferred_element_type=jnp.float32,
     )
-    mixed = residual.astype(jnp.float32) + lax.psum_scatter(
-        head_terms, "expert", scatter_dimension=0, tiled=True
-    )
+    mixed = residual.astype(jnp.float32) + a2a_sum(head_terms, "expert", 0, expert_count)
     normed = (
         mixed * lax.rsqrt(jnp.mean(mixed * mixed, axis=-1, keepdims=True) + EPSILON) * ffn_gain
     ).astype(jnp.bfloat16)
@@ -133,8 +143,8 @@
     pool_weight = jnp.where(
         slot_span[:, None] == jnp.arange(span_local)[None, :], slot_gate[:, None], 0.0
     )
-    gathered = lax.all_gather(compact, "dp", axis=0, tiled=True)
-    gathered_weight = lax.all_gather(pool_weight, "dp", axis=0, tiled=True)
+    gathered = dp_gather(compact, 0)
+    gathered_weight = lax.all_gather(pool_weight, DP, axis=0, tiled=True)
     n_dp = gathered.shape[0] // GROUP_CAP
     gate_proj = jnp.einsum("ned,edf->nf", gathered, w_gate, preferred_element_type=jnp.float32)
     up_proj = jnp.einsum("ned,edf->nf", gathered, w_up, preferred_element_type=jnp.float32)
@@ -154,8 +164,8 @@
     pooled_part = pooled_part + jnp.where(
         (jnp.arange(span_count) == own_span)[:, None], mixed_sum[None, :], 0.0
     )
-    pooled_cols = lax.psum_scatter(pooled_part, "expert", scatter_dimension=1, tiled=True)
-    pooled_cols = doubling_sum(pooled_cols, "dp", n_dp)
+    pooled_cols = a2a_sum(pooled_part, "expert", 1, expert_count)
+    pooled_cols = doubling_sum(pooled_cols, DP, n_dp)
     squares = doubling_sum(jnp.sum(pooled_cols * pooled_cols, axis=-1), "expert", expert_count)
     everyone = (
         pooled_cols * lax.rsqrt(squares / width + EPSILON)[:, None] * summary_gain
@@ -181,27 +191,32 @@
 
 
 def solution(mesh):
+    dp_size, expert_size = mesh.devices.shape
+    y_size = 4
+    split_mesh = jax.sharding.Mesh(
+        mesh.devices.reshape(dp_size // y_size, y_size, expert_size), ("z", "y", "expert")
+    )
     return jax.shard_map(
         shards,
-        mesh=mesh,
+        mesh=split_mesh,
         in_specs=(
-            P(("dp", "expert"), None),
-            P("dp", "expert"),
-            P("dp", "expert"),
-            P("dp", "expert"),
-            P("dp", None, "expert"),
-            P("dp", None, "expert"),
-            P("expert", "dp"),
+            P((*DP, "expert"), None),
+            P(DP, "expert"),
+            P(DP, "expert"),
+            P(DP, "expert"),
+            P(DP, None, "expert"),
+            P(DP, None, "expert"),
+            P("expert", DP),
             P(),
             P(),
-            P(("dp", "expert"), None),
-            P("expert", None, "dp"),
-            P("expert", None, "dp"),
-            P("expert", "dp", None),
+            P((*DP, "expert"), None),
+            P("expert", None, DP),
+            P("expert", None, DP),
+            P("expert", DP, None),
             P("expert"),
             P("expert"),
             P(),
         ),
-        out_specs=(P("dp", "expert"), P("dp", "expert")),
+        out_specs=(P(DP, "expert"), P(DP, "expert")),
         check_vma=False,
     )

time: 347 us -> 303 us (0.87)
  waiting for transfers between devices: 222 us -> 137 us
  blocking collectives: 43.9 us -> 93.8 us
    reduce_scatter x2 -> x0, waiting for transfers between devices: 55.7 us -> none  [the longest x1 28.8 us: shards(): lax.psum_scatter(pooled_part, 'expert', scatter_dimension=1, tiled=True)]
    all_gather x2, waiting for transfers between devices: 128 us -> 82 us  [dp_gather(): lax.all_gather(lax.all_gather(x, 'y', axis=axis, tiled=True), 'z', axis=a...]
    all_gather x1 -> x3, blocking collectives: 43.9 us -> 74.6 us  [the longest x1 44.4 us: shards(): gathered_weight = lax.all_gather(pool_weight, DP, axis=0, tiled=True)]
    all_to_all x0 -> x1, blocking collectives: none -> 19.2 us  [a2a_sum(): lax.all_to_all(x.reshape(split), axis, split_axis=dim, concat_axis=dim, t...]
    all_to_all x0 -> x1, waiting for transfers between devices: none -> 13.9 us  [a2a_sum(): lax.all_to_all(x.reshape(split), axis, split_axis=dim, concat_axis=dim, t...]
    all_to_all x0 -> x1, starting transfers between devices: none -> 4.94 us  [a2a_sum(): lax.all_to_all(x.reshape(split), axis, split_axis=dim, concat_axis=dim, t...]
    ppermute x8, starting transfers between devices: 17.8 us -> 13.9 us  [doubling_sum(): x = x + lax.ppermute(x, axis, [(a, a ^ step) for a in range(count)])]
  transfers between devices with their start and end apart: 14 -> 13, of which waited for: 13 -> 13; matrix products, arithmetic and copies ran while one was open for 3% -> 2% of each run, Pallas kernels for 0% -> 0%
where the time goes in v4:
time: 303 us; the launch traced here: 302 us
  waiting for transfers between devices  137 us (45%)
  blocking collectives  93.8 us (31%)
  starting transfers between devices  28.5 us (9%)
  matrix products  22.3 us (7%)
  between operations  14.4 us (5%)
  other arithmetic  3.76 us (1%)
    all_gather x2, waiting for transfers between devices, dp_gather(): lax.all_gather(lax.all_gather(x, 'y', axis=axis, tiled=True), 'z', axis=a...  82 us
    all_gather x1, blocking collectives, shards(): gathered_weight = lax.all_gather(pool_weight, DP, axis=0, tiled=True)  44.4 us
    ppermute x8, waiting for transfers between devices, doubling_sum(): x = x + lax.ppermute(x, axis, [(a, a ^ step) for a in range(count)])  31.3 us
    all_gather x2, blocking collectives, dp_gather(): lax.all_gather(x, 'y', axis=axis, tiled=True)  30.2 us
    all_to_all x1, blocking collectives, a2a_sum(): lax.all_to_all(x.reshape(split), axis, split_axis=dim, concat_axis=dim, t...  19.2 us
    ppermute x8, starting transfers between devices, doubling_sum(): x = x + lax.ppermute(x, axis, [(a, a ^ step) for a in range(count)])  13.9 us
    all_to_all x1, waiting for transfers between devices, a2a_sum(): lax.all_to_all(x.reshape(split), axis, split_axis=dim, concat_axis=dim, t...  13.9 us
    all_to_all x1, waiting for transfers between devices, shards(): lax.all_to_all(outgoing, 'expert', split_axis=0, concat_axis=1, tiled=True)  7.32 us
  transfers between devices with their start and end apart: 13, of which 13 were waited for; matrix products, arithmetic and copies ran while one was open for 2% of the time, Pallas kernels for 0%

profile of v4, /device:TPU:2, one launch (start us, length us, event | category | flops | bytes accessed | tf_op | source)
XLA Modules:
  0.0 302.0 jit_solution(6907460537318314307)
XLA Ops:
  7.2 15.8 %all_gather.15 = bf16[512,512]{1,0:T(8,128)(2,1)} all-gather(bf16[512,128]{1,0:T(8,128)(2,1)} %param.22), channel_id=1, replica_groups=mesh['z'=8,'y'=4,'expert'=8] {'y'}, dimensions={1}, use_global_device_ids=true | all-gather | bytes 655360 | tf_op jit(solution)/shard_map/all_gather | solution.py:64
  24.4 1.0 fusion.59
  26.4 54.3 %all-gather.4.cloned.1.call-done = bf16[512,4096]{1,0:T(8,128)(2,1)} async-done(((bf16[512,512]{1,0:T(8,128)(2,1)}), bf16[512,4096]{1,0:T(8,128)(2,1)}) %all-gather.4.cloned.1.call-update) | async-done | bytes 4194320 | tf_op jit(solution)/shard_map/all_gather | solution.py:64
  80.7 4.0 %fusion.5 = f32[8,8,4096]{2,1,0:T(8,128)} fusion(bf16[8,8,512]{2,1,0:T(8,128)(2,1)S(1)} %dot_general.45, bf16[512,4096]{1,0:T(8,128)(2,1)} %all-gather.4.cloned.1.call-done), kind=kOutput, calls=%fused_computation.7 | convolution fusion | flops 268435456 | bytes 5308416 | tf_op jit(solution)/shard_map/dot_general | solution.py:102
  84.7 4.9 %all-to-all-start.1 = ((f32[8,8,4096]{2,1,0:T(8,128)}), f32[8,8,4096]{2,1,0:T(8,128)S(1)}, u32[]{:S(2)}, u32[]{:S(2)}) async-start(f32[8,8,4096]{2,1,0:T(8,128)} %fusion.5), calls=%async_computation.1 | async-start | bytes 2097152 | tf_op jit(solution)/shard_map/all_to_all | solution.py:59
  90.3 13.9 %all-to-all-done.1 = f32[8,8,4096]{2,1,0:T(8,128)S(1)} async-done(((f32[8,8,4096]{2,1,0:T(8,128)}), f32[8,8,4096]{2,1,0:T(8,128)S(1)}, u32[]{:S(2)}, u32[]{:S(2)}) %all-to-all-start.1) | async-done | bytes 1048608 | tf_op jit(solution)/shard_map/all_to_all | solution.py:59
  104.1 4.7 %all-to-all-start = ((s32[8,1,8]{2,1,0:T(1,128)}), s32[8,1,8]{2,1,0:T(1,128)S(1)}, u32[]{:S(2)}, u32[]{:S(2)}) async-start(s32[8,1,8]{2,1,0:T(1,128)} %compare_select_fusion.1), calls=%async_computation | async-start | bytes 8192 | tf_op jit(solution)/shard_map/all_to_all | solution.py:118
  109.2 0.9 broadcast_select_fusion
  110.1 2.6 all-to-all-done
  112.7 4.9 %all-to-all-start.2 = ((bf16[8,8,4096]{2,1,0:T(8,128)(2,1)}), bf16[8,8,4096]{2,1,0:T(8,128)(2,1)S(1)}, u32[]{:S(2)}, u32[]{:S(2)}) async-start(bf16[8,8,4096]{2,1,0:T(8,128)(2,1)} %broadcast_select_fusion), calls=%async_computation.2 | async-start | bytes 1048576 | tf_op jit(solution)/shard_map/all_to_all | solution.py:117
  119.1 7.3 %all-to-all-done.2 = bf16[8,8,4096]{2,1,0:T(8,128)(2,1)S(1)} async-done(((bf16[8,8,4096]{2,1,0:T(8,128)(2,1)}), bf16[8,8,4096]{2,1,0:T(8,128)(2,1)S(1)}, u32[]{:S(2)}, u32[]{:S(2)}) %all-to-all-start.2) | async-done | bytes 524320 | tf_op jit(solution)/shard_map/all_to_all | solution.py:117
  126.6 14.4 %all_gather.18 = bf16[96,1,4096]{2,0,1:T(8,128)(2,1)} all-gather(bf16[24,1,4096]{2,0,1:T(8,128)(2,1)S(1)} %bitcast.127), channel_id=1, replica_groups=mesh['z'=8,'y'=4,'expert'=8] {'y'}, dimensions={0}, use_global_device_ids=true | all-gather | bytes 983040 | tf_op jit(solution)/shard_map/all_gather | solution.py:64
  141.6 44.4 %all-gather = f32[32,24,2]{1,2,0:T(2,128)S(1)} all-gather(f32[1,24,2]{1,2,0:T(2,128)S(1)} %fusion.55), channel_id=1, replica_groups=mesh['z'=8,'y'=4,'expert'=8] {'z','y'}, dimensions={0}, use_global_device_ids=true | all-gather | bytes 6336 | tf_op jit(solution)/shard_map/all_gather | solution.py:147
  186.0 27.7 %all-gather.6.cloned.1.call-done = bf16[768,1,4096]{2,0,1:T(8,128)(2,1)} async-done(((bf16[96,1,4096]{2,0,1:T(8,128)(2,1)}), bf16[768,1,4096]{2,0,1:T(8,128)(2,1)}) %all-gather.6.cloned.1.call-update) | async-done | bytes 6291472 | tf_op jit(solution)/shard_map/all_gather | solution.py:64
  213.7 7.0 %fusion.3 = f32[768,448]{0,1:T(8,128)S(1)} fusion(bf16[768,1,4096]{2,0,1:T(8,128)(2,1)} %all-gather.6.cloned.1.call-done, bf16[1,4096,448]{1,2,0:T(8,128)(2,1)} %param.26), kind=kOutput, calls=%fused_computation.3 | convolution fusion | flops 2818572288 | bytes 11337728 | tf_op jit(solution)/shard_map/ned,edf->nf/dot_general | solution.py:149
  220.8 3.1 %fusion.16 = bf16[768,448]{0,1:T(8,128)(2,1)S(1)} fusion(bf16[1,4096,448]{1,2,0:T(8,128)(2,1)S(1)} %copy-done.7, bf16[768,1,4096]{2,0,1:T(8,128)(2,1)S(1)} %copy-done.6, f32[768,448]{0,1:T(8,128)S(1)} %fusion.3), kind=kOutput, calls=%fused_computation.15 | convolution fusion | flops 2820636672 | bytes 12025856 | tf_op jit(solution)/shard_map/ned,edf->nf/dot_general | solution.py:150
  224.8 4.1 %convolution_add_fusion = f32[64,4096]{1,0:T(8,128)S(1)} fusion(f32[64,448]{1,0:T(8,128)S(1)} %reshape.516, bf16[1,448,4096]{2,1,0:T(8,128)(2,1)} %param.28, f32[4096]{0:T(1024)S(1)} %get-tuple-element.2, pred[64]{0:T(512)(128)(4,1)S(1)} %iota_compare_fusion.5), kind=kOutput, calls=%fused_computation.5 | convolution fusion | flops 1409810432 | bytes 4849728 | tf_op jit(solution)/shard_map/dot_general | solution.py:158
  229.0 19.2 %all_to_all.32 = f32[64,8,512]{2,0,1:T(8,128)S(1)} all-to-all(f32[64,8,512]{2,0,1:T(8,128)S(1)} %bitcast.125), channel_id=1, replica_groups=mesh['z'=8,'y'=4,'expert'=8] {'expert'}, dimensions={1} | all-to-all | bytes 2097152 | tf_op jit(solution)/shard_map/all_to_all | solution.py:59
  248.3 1.7 collective-permute-start
  250.0 3.5 %collective-permute-done = f32[64,512]{1,0:T(8,128)S(1)} collective-permute-done((f32[64,512]{1,0:T(8,128)S(1)}, f32[64,512]{1,0:T(8,128)S(1)}, u32[]{:S(2)}, u32[]{:S(2)}) %collective-permute-start) | collective-permute-done | bytes 131104 | tf_op jit(solution)/shard_map/ppermute | solution.py:70
  253.6 3.1 %collective-permute-start.1 = (f32[64,512]{1,0:T(8,128)S(1)}, f32[64,512]{1,0:T(8,128)S(1)}, u32[]{:S(2)}, u32[]{:S(2)}) collective-permute-start(f32[64,512]{1,0:T(8,128)S(1)} %add.102), channel_id=1, source_target_pairs={{0,16},{8,24},{16,0},{24,8},{32,48},{40,56},{48,32},{56,40},{64,80... | collective-permute-start | bytes 393224 | tf_op jit(solution)/shard_map/ppermute | solution.py:70
  256.6 3.5 %collective-permute-done.1 = f32[64,512]{1,0:T(8,128)S(1)} collective-permute-done((f32[64,512]{1,0:T(8,128)S(1)}, f32[64,512]{1,0:T(8,128)S(1)}, u32[]{:S(2)}, u32[]{:S(2)}) %collective-permute-start.1) | collective-permute-done | bytes 131104 | tf_op jit(solution)/shard_map/ppermute | solution.py:70
  260.2 5.6 %collective-permute-done.2 = f32[64,512]{1,0:T(8,128)S(1)} collective-permute-done((f32[64,512]{1,0:T(8,128)S(1)}, f32[64,512]{1,0:T(8,128)S(1)}, u32[]{:S(2)}, u32[]{:S(2)}) %collective-permute-start.2) | collective-permute-done | bytes 131104 | tf_op jit(solution)/shard_map/ppermute | solution.py:70
  265.9 1.9 collective-permute-start.3
  267.8 6.4 %collective-permute-done.3 = f32[64,512]{1,0:T(8,128)S(1)} collective-permute-done((f32[64,512]{1,0:T(8,128)S(1)}, f32[64,512]{1,0:T(8,128)S(1)}, u32[]{:S(2)}, u32[]{:S(2)}) %collective-permute-start.3) | collective-permute-done | bytes 131104 | tf_op jit(solution)/shard_map/ppermute | solution.py:70
  274.2 4.3 %collective-permute-start.4 = (f32[64,512]{1,0:T(8,128)S(1)}, f32[64,512]{1,0:T(8,128)S(1)}, u32[]{:S(2)}, u32[]{:S(2)}) collective-permute-start(f32[64,512]{1,0:T(8,128)S(1)} %add.105), channel_id=1, source_target_pairs={{0,128},{8,136},{16,144},{24,152},{32,160},{40,168},{48,176},{56,1... | collective-permute-start | bytes 393224 | tf_op jit(solution)/shard_map/ppermute | solution.py:70
  278.4 5.4 %collective-permute-done.4 = f32[64,512]{1,0:T(8,128)S(1)} collective-permute-done((f32[64,512]{1,0:T(8,128)S(1)}, f32[64,512]{1,0:T(8,128)S(1)}, u32[]{:S(2)}, u32[]{:S(2)}) %collective-permute-start.4) | collective-permute-done | bytes 131104 | tf_op jit(solution)/shard_map/ppermute | solution.py:70
  284.2 1.1 collective-permute-done.5
  285.2 1.4 collective-permute-start.6
  286.7 2.1 collective-permute-done.6
  288.8 1.4 collective-permute-start.7
  290.2 3.7 %collective-permute-done.7 = f32[64]{0:T(128)S(1)} collective-permute-done((f32[64]{0:T(128)S(1)}, f32[64]{0:T(128)S(1)}, u32[]{:S(2)}, u32[]{:S(2)}) %collective-permute-start.7) | collective-permute-done | bytes 288 | tf_op jit(solution)/shard_map/ppermute | solution.py:70
  (86 shorter events, 8.4 us)
Async XLA Ops:
  7.2 16.8 %copy-start = (bf16[2,1024,128]{2,1,0:T(8,128)(2,1)S(1)}, bf16[2,1024,128]{2,1,0:T(8,128)(2,1)}, u32[]{:S(2)}) copy-start(bf16[2,1024,128]{2,1,0:T(8,128)(2,1)} %param.20) | copy-start | bytes 1572868
  7.2 18.5 %copy-start.10 = (bf16[64,128]{1,0:T(8,128)(2,1)S(1)}, bf16[64,128]{1,0:T(8,128)(2,1)}, u32[]{:S(2)}) copy-start(bf16[64,128]{1,0:T(8,128)(2,1)} %param.19) | copy-start | bytes 49156
  7.2 18.7 %copy-start.8 = (bf16[2,1024,128]{2,1,0:T(8,128)(2,1)S(1)}, bf16[2,1024,128]{2,1,0:T(8,128)(2,1)}, u32[]{:S(2)}) copy-start(bf16[2,1024,128]{2,1,0:T(8,128)(2,1)} %param.21) | copy-start | bytes 1572868
  7.2 73.5 %all-gather.4.cloned.1.call-start = ((), (), s32[]{:S(2)}) async-start(), calls=%async_computation.4 | async-start | bytes 4718592 | tf_op jit(solution)/shard_map/all_gather | solution.py:64
  26.4 63.3 %copy-start.5 = (s32[8,2]{0,1:T(2,128)S(1)}, s32[8,2]{0,1:T(2,128)}, u32[]{:S(2)}) copy-start(s32[8,2]{0,1:T(2,128)} %param.25) | copy-start | bytes 196
  26.4 82.5 %copy-start.1 = (bf16[8,4096]{1,0:T(8,128)(2,1)S(1)}, bf16[8,4096]{1,0:T(8,128)(2,1)}, u32[]{:S(2)}) copy-start(bf16[8,4096]{1,0:T(8,128)(2,1)} %param.16) | copy-start | bytes 196612
  26.4 82.6 %copy-start.2 = (f32[4096]{0:T(1024)S(1)}, f32[4096]{0:T(1024)}, u32[]{:S(2)}) copy-start(f32[4096]{0:T(1024)} %param.23) | copy-start | bytes 49156
  84.7 56.6 %copy-start.9 = (bf16[4096,8]{0,1:T(8,128)(2,1)S(1)}, bf16[4096,8]{0,1:T(8,128)(2,1)}, u32[]{:S(2)}) copy-start(bf16[4096,8]{0,1:T(8,128)(2,1)} %param.24) | copy-start | bytes 196612
  84.7 19.4 %all-to-all-start.1 = ((f32[8,8,4096]{2,1,0:T(8,128)}), f32[8,8,4096]{2,1,0:T(8,128)S(1)}, u32[]{:S(2)}, u32[]{:S(2)}) async-start(f32[8,8,4096]{2,1,0:T(8,128)} %fusion.5), calls=%async_computation.1 | async-start | bytes 2097152 | tf_op jit(solution)/shard_map/all_to_all | solution.py:59
  104.1 8.6 %all-to-all-start = ((s32[8,1,8]{2,1,0:T(1,128)}), s32[8,1,8]{2,1,0:T(1,128)S(1)}, u32[]{:S(2)}, u32[]{:S(2)}) async-start(s32[8,1,8]{2,1,0:T(1,128)} %compare_select_fusion.1), calls=%async_computation | async-start | bytes 8192 | tf_op jit(solution)/shard_map/all_to_all | solution.py:118
  112.7 13.7 %all-to-all-start.2 = ((bf16[8,8,4096]{2,1,0:T(8,128)(2,1)}), bf16[8,8,4096]{2,1,0:T(8,128)(2,1)S(1)}, u32[]{:S(2)}, u32[]{:S(2)}) async-start(bf16[8,8,4096]{2,1,0:T(8,128)(2,1)} %broadcast_select_fusion), calls=%async_computation.2 | async-start | bytes 1048576 | tf_op jit(solution)/shard_map/all_to_all | solution.py:117
  117.5 96.1 %all-gather.6.cloned.1.call-start = ((), (), s32[]{:S(2)}) async-start(), calls=%async_computation.5 | async-start | bytes 7077888 | tf_op jit(solution)/shard_map/all_gather | solution.py:64
  213.7 7.1 %copy-start.6 = (bf16[768,1,4096]{2,0,1:T(8,128)(2,1)S(1)}, bf16[768,1,4096]{2,0,1:T(8,128)(2,1)}, u32[]{:S(2)}) copy-start(bf16[768,1,4096]{2,0,1:T(8,128)(2,1)} %all-gather.6.cloned.1.call-done) | copy-start | bytes 18874372
  213.7 7.1 %copy-start.7 = (bf16[1,4096,448]{1,2,0:T(8,128)(2,1)S(1)}, bf16[1,4096,448]{1,2,0:T(8,128)(2,1)}, u32[]{:S(2)}) copy-start(bf16[1,4096,448]{1,2,0:T(8,128)(2,1)} %param.27) | copy-start | bytes 11010052
  228.9 55.2 %copy-start.11 = (s32[64]{0:T(128)S(1)}, s32[64]{0:T(128)}, u32[]{:S(2)}) copy-start(s32[64]{0:T(128)} %param.31) | copy-start | bytes 772
  228.9 61.3 %copy-start.12 = (f32[4]{0:T(128)S(1)}, f32[4]{0:T(128)}, u32[]{:S(2)}) copy-start(f32[4]{0:T(128)} %param.30) | copy-start | bytes 52
  228.9 65.0 %copy-start.3 = (f32[512]{0:T(512)S(1)}, f32[512]{0:T(512)}, u32[]{:S(2)}) copy-start(f32[512]{0:T(512)} %param.29) | copy-start | bytes 6148
  248.3 5.2 %collective-permute-start = (f32[64,512]{1,0:T(8,128)S(1)}, f32[64,512]{1,0:T(8,128)S(1)}, u32[]{:S(2)}, u32[]{:S(2)}) collective-permute-start(f32[64,512]{1,0:T(8,128)S(1)} %reduce_sum.117), channel_id=1, source_target_pairs={{0,8},{8,0},{16,24},{24,16},{32,40},{40,32},{48,56},{56,48},{64,72... | collective-permute-start | bytes 393224 | tf_op jit(solution)/shard_map/ppermute | solution.py:70
  253.6 6.6 %collective-permute-start.1 = (f32[64,512]{1,0:T(8,128)S(1)}, f32[64,512]{1,0:T(8,128)S(1)}, u32[]{:S(2)}, u32[]{:S(2)}) collective-permute-start(f32[64,512]{1,0:T(8,128)S(1)} %add.102), channel_id=1, source_target_pairs={{0,16},{8,24},{16,0},{24,8},{32,48},{40,56},{48,32},{56,40},{64,80... | collective-permute-start | bytes 393224 | tf_op jit(solution)/shard_map/ppermute | solution.py:70
  260.1 5.7 %collective-permute-start.2 = (f32[64,512]{1,0:T(8,128)S(1)}, f32[64,512]{1,0:T(8,128)S(1)}, u32[]{:S(2)}, u32[]{:S(2)}) collective-permute-start(f32[64,512]{1,0:T(8,128)S(1)} %add.103), channel_id=1, source_target_pairs={{0,32},{8,40},{16,48},{24,56},{32,0},{40,8},{48,16},{56,24},{64,96... | collective-permute-start | bytes 393224 | tf_op jit(solution)/shard_map/ppermute | solution.py:70
  265.9 8.2 %collective-permute-start.3 = (f32[64,512]{1,0:T(8,128)S(1)}, f32[64,512]{1,0:T(8,128)S(1)}, u32[]{:S(2)}, u32[]{:S(2)}) collective-permute-start(f32[64,512]{1,0:T(8,128)S(1)} %add.104), channel_id=1, source_target_pairs={{0,64},{8,72},{16,80},{24,88},{32,96},{40,104},{48,112},{56,120},{... | collective-permute-start | bytes 393224 | tf_op jit(solution)/shard_map/ppermute | solution.py:70
  274.2 9.7 %collective-permute-start.4 = (f32[64,512]{1,0:T(8,128)S(1)}, f32[64,512]{1,0:T(8,128)S(1)}, u32[]{:S(2)}, u32[]{:S(2)}) collective-permute-start(f32[64,512]{1,0:T(8,128)S(1)} %add.105), channel_id=1, source_target_pairs={{0,128},{8,136},{16,144},{24,152},{32,160},{40,168},{48,176},{56,1... | collective-permute-start | bytes 393224 | tf_op jit(solution)/shard_map/ppermute | solution.py:70
  284.0 1.2 collective-permute-start.5
  285.2 3.6 %collective-permute-start.6 = (f32[64]{0:T(128)S(1)}, f32[64]{0:T(128)S(1)}, u32[]{:S(2)}, u32[]{:S(2)}) collective-permute-start(f32[64]{0:T(128)S(1)} %add.107), channel_id=1, source_target_pairs={{0,2},{1,3},{2,0},{3,1},{4,6},{5,7},{6,4},{7,5},{8,10},{9,11},{10,... | collective-permute-start | bytes 776 | tf_op jit(solution)/shard_map/ppermute | solution.py:70
  288.8 5.1 %collective-permute-start.7 = (f32[64]{0:T(128)S(1)}, f32[64]{0:T(128)S(1)}, u32[]{:S(2)}, u32[]{:S(2)}) collective-permute-start(f32[64]{0:T(128)S(1)} %add.108), channel_id=1, source_target_pairs={{0,4},{1,5},{2,6},{3,7},{4,0},{5,1},{6,2},{7,3},{8,12},{9,13},{10,... | collective-permute-start | bytes 776 | tf_op jit(solution)/shard_map/ppermute | solution.py:70
  294.0 1.2 copy-start.4
Sparse Core Ops, SparseCore 0:
  23.2 57.4 all-gather.3
  141.2 72.4 all-gather.5

commit v5 on v4

--- a/solution.py
+++ b/solution.py
@@ -58,6 +58,11 @@
     split = shape[:dim] + (count, shape[dim] // count) + shape[dim + 1:]
     received = lax.all_to_all(x.reshape(split), axis, split_axis=dim, concat_axis=dim, tiled=True)
     return jnp.sum(received, axis=dim)
+
+
+def a2a_gather(x, axis, count):
+    spread = jnp.broadcast_to(x[None], (count,) + x.shape)
+    return lax.all_to_all(spread, axis, split_axis=0, concat_axis=0, tiled=True)
 
 
 def dp_gather(x, axis):
@@ -112,11 +117,15 @@
     first = routes[:, 0:1] == expert_ids[None, :]
     second = routes[:, 1:2] == expert_ids[None, :]
     partner = jnp.where(first, routes[:, 1:2], jnp.where(second, routes[:, 0:1], -1))
-    outgoing = jnp.where((partner >= 0).T[:, :, None], normed[None, :, :], 0)
-    arrived_rows, arrived_partner = (
-        lax.all_to_all(outgoing, "expert", split_axis=0, concat_axis=1, tiled=True),
-        lax.all_to_all(partner.T, "expert", split_axis=0, concat_axis=1, tiled=True),
-    )
+    tag_width = 128
+    tag = jnp.broadcast_to(((partner + 1).T)[:, :, None], partner.T.shape + (tag_width,))
+    outgoing = jnp.concatenate(
+        [jnp.where((partner >= 0).T[:, :, None], normed[None, :, :], 0), tag.astype(jnp.bfloat16)],
+        axis=2,
+    )
+    arrived = lax.all_to_all(outgoing, "expert", split_axis=0, concat_axis=1, tiled=True)
+    arrived_rows = arrived[:, :, :width]
+    arrived_partner = arrived[:, :, width].astype(jnp.int32) - 1
     present = (arrived_partner >= 0).astype(jnp.int32)
     position = jnp.cumsum(present, axis=1) - 1
     picker = (present[:, None, :] > 0) & (
@@ -165,12 +174,12 @@
         (jnp.arange(span_count) == own_span)[:, None], mixed_sum[None, :], 0.0
     )
     pooled_cols = a2a_sum(pooled_part, "expert", 1, expert_count)
-    pooled_cols = doubling_sum(pooled_cols, DP, n_dp)
-    squares = doubling_sum(jnp.sum(pooled_cols * pooled_cols, axis=-1), "expert", expert_count)
-    everyone = (
-        pooled_cols * lax.rsqrt(squares / width + EPSILON)[:, None] * summary_gain
+    own_cols = a2a_sum(pooled_cols, DP, 0, n_dp)
+    squares = doubling_sum(jnp.sum(own_cols * own_cols, axis=-1), "expert", expert_count)
+    summary = (
+        own_cols * lax.rsqrt(squares / width + EPSILON)[:, None] * summary_gain
     ).astype(jnp.bfloat16)
-    summary = lax.dynamic_slice_in_dim(everyone, dp_index * span_local, span_local)
+    everyone = a2a_gather(summary, DP, n_dp).reshape(n_dp * span_local, slice_width)
     heads_local = slice_width // HD
     mine = summary.reshape(span_local, heads_local, HD)
     others = everyone.reshape(everyone.shape[0], heads_local, HD)

time: 303 us -> 292 us (0.964)
  blocking collectives: 93.8 us -> 107 us
  waiting for transfers between devices: 137 us -> 124 us
  starting transfers between devices: 28.5 us -> 18.7 us
    ppermute x8 -> x3, waiting for transfers between devices: 31.3 us -> 7.02 us  [doubling_sum(): x = x + lax.ppermute(x, axis, [(a, a ^ step) for a in range(count)])]
    all_to_all x0 -> x1, blocking collectives: none -> 12.9 us  [shards(): lax.all_to_all(outgoing, 'expert', split_axis=0, concat_axis=1, tiled=True)]
    ppermute x8 -> x3, starting transfers between devices: 13.9 us -> 2.85 us  [doubling_sum(): x = x + lax.ppermute(x, axis, [(a, a ^ step) for a in range(count)])]
    all_to_all x1 -> x2, waiting for transfers between devices: 13.9 us -> 24.8 us  [a2a_sum(): lax.all_to_all(x.reshape(split), axis, split_axis=dim, concat_axis=dim, t...]
    all_to_all x1 -> x2, starting transfers between devices: 4.94 us -> 12 us  [a2a_sum(): lax.all_to_all(x.reshape(split), axis, split_axis=dim, concat_axis=dim, t...]
    all_to_all x2 -> x1, starting transfers between devices: 9.56 us -> 3.85 us  [a2a_gather(): return lax.all_to_all(spread, axis, split_axis=0, concat_axis=0, tiled=True)]
    all_to_all x2 -> x1, waiting for transfers between devices: 9.95 us -> 10 us  [a2a_gather(): return lax.all_to_all(spread, axis, split_axis=0, concat_axis=0, tiled=True)]
  transfers between devices with their start and end apart: 13 -> 8, of which waited for: 13 -> 8; matrix products, arithmetic and copies ran while one was open for 2% -> 1% of each run, Pallas kernels for 0% -> 0%
where the time goes in v5:
time: 292 us; the launch traced here: 291 us
  waiting for transfers between devices  124 us (42%)
  blocking collectives  107 us (37%)
  matrix products  22.3 us (8%)
  starting transfers between devices  18.7 us (6%)
  between operations  14.5 us (5%)
  local copies, waits for them, and re-layouts  3.03 us (1%)
    all_gather x2, waiting for transfers between devices, dp_gather(): lax.all_gather(lax.all_gather(x, 'y', axis=axis, tiled=True), 'z', axis=a...  82 us
    all_gather x1, blocking collectives, shards(): gathered_weight = lax.all_gather(pool_weight, DP, axis=0, tiled=True)  44.5 us
    all_gather x2, blocking collectives, dp_gather(): lax.all_gather(x, 'y', axis=axis, tiled=True)  30.3 us
    all_to_all x2, waiting for transfers between devices, a2a_sum(): lax.all_to_all(x.reshape(split), axis, split_axis=dim, concat_axis=dim, t...  24.8 us
    all_to_all x1, blocking collectives, a2a_sum(): lax.all_to_all(x.reshape(split), axis, split_axis=dim, concat_axis=dim, t...  19.2 us
    all_to_all x1, blocking collectives, shards(): lax.all_to_all(outgoing, 'expert', split_axis=0, concat_axis=1, tiled=True)  12.9 us
    all_to_all x2, starting transfers between devices, a2a_sum(): lax.all_to_all(x.reshape(split), axis, split_axis=dim, concat_axis=dim, t...  12 us
    all_to_all x1, waiting for transfers between devices, a2a_gather(): return lax.all_to_all(spread, axis, split_axis=0, concat_axis=0, tiled=True)  10 us
  transfers between devices with their start and end apart: 8, of which 8 were waited for; matrix products, arithmetic and copies ran while one was open for 1% of the time, Pallas kernels for 0%

profile of v5, /device:TPU:2, one launch (start us, length us, event | category | flops | bytes accessed | tf_op | source)
XLA Modules:
  0.0 291.1 jit_solution(1806218389037574153)
XLA Ops:
  7.2 15.8 %all_gather.15 = bf16[512,512]{1,0:T(8,128)(2,1)} all-gather(bf16[512,128]{1,0:T(8,128)(2,1)} %param.22), channel_id=1, replica_groups=mesh['z'=8,'y'=4,'expert'=8] {'y'}, dimensions={1}, use_global_device_ids=true | all-gather | bytes 655360 | tf_op jit(solution)/shard_map/all_gather | solution.py:69
  23.1 0.9 reshape.471
  24.0 0.4 fusion.59
  24.4 1.0 fusion.60
  25.4 0.3 fusion.29
  25.9 0.4 fusion.24
  26.4 54.3 %all-gather.4.cloned.1.call-done = bf16[512,4096]{1,0:T(8,128)(2,1)} async-done(((bf16[512,512]{1,0:T(8,128)(2,1)}), bf16[512,4096]{1,0:T(8,128)(2,1)}) %all-gather.4.cloned.1.call-update) | async-done | bytes 4194320 | tf_op jit(solution)/shard_map/all_gather | solution.py:69
  80.7 4.0 %fusion.5 = f32[8,8,4096]{2,1,0:T(8,128)} fusion(bf16[8,8,512]{2,1,0:T(8,128)(2,1)S(1)} %dot_general.45, bf16[512,4096]{1,0:T(8,128)(2,1)} %all-gather.4.cloned.1.call-done), kind=kOutput, calls=%fused_computation.7 | convolution fusion | flops 268435456 | bytes 5308416 | tf_op jit(solution)/shard_map/dot_general | solution.py:107
  84.7 4.8 %all-to-all-start = ((f32[8,8,4096]{2,1,0:T(8,128)}), f32[8,8,4096]{2,1,0:T(8,128)S(1)}, u32[]{:S(2)}, u32[]{:S(2)}) async-start(f32[8,8,4096]{2,1,0:T(8,128)} %fusion.5), calls=%async_computation | async-start | bytes 2097152 | tf_op jit(solution)/shard_map/all_to_all | solution.py:59
  89.6 14.4 %all-to-all-done = f32[8,8,4096]{2,1,0:T(8,128)S(1)} async-done(((f32[8,8,4096]{2,1,0:T(8,128)}), f32[8,8,4096]{2,1,0:T(8,128)S(1)}, u32[]{:S(2)}, u32[]{:S(2)}) %all-to-all-start) | async-done | bytes 1048608 | tf_op jit(solution)/shard_map/all_to_all | solution.py:59
  104.6 12.9 %all_to_all.32 = bf16[8,8,4224]{2,1,0:T(8,128)(2,1)S(1)} all-to-all(bf16[8,8,4224]{2,1,0:T(8,128)(2,1)S(1)} %pad_maximum_fusion), channel_id=1, replica_groups=mesh['z'=8,'y'=4,'expert'=8] {'expert'}, dimensions={0} | all-to-all | bytes 1081344 | tf_op jit(solution)/shard_map/all_to_all | solution.py:126
  118.1 14.5 %all_gather.18 = bf16[96,1,4096]{2,0,1:T(8,128)(2,1)} all-gather(bf16[24,1,4096]{2,0,1:T(8,128)(2,1)S(1)} %bitcast.124), channel_id=1, replica_groups=mesh['z'=8,'y'=4,'expert'=8] {'y'}, dimensions={0}, use_global_device_ids=true | all-gather | bytes 983040 | tf_op jit(solution)/shard_map/all_gather | solution.py:69
  133.1 44.5 %all-gather = f32[32,24,2]{1,2,0:T(2,128)S(1)} all-gather(f32[1,24,2]{1,2,0:T(2,128)S(1)} %fusion.57), channel_id=1, replica_groups=mesh['z'=8,'y'=4,'expert'=8] {'z','y'}, dimensions={0}, use_global_device_ids=true | all-gather | bytes 6336 | tf_op jit(solution)/shard_map/all_gather | solution.py:156
  177.6 27.7 %all-gather.6.cloned.1.call-done = bf16[768,1,4096]{2,0,1:T(8,128)(2,1)} async-done(((bf16[96,1,4096]{2,0,1:T(8,128)(2,1)}), bf16[768,1,4096]{2,0,1:T(8,128)(2,1)}) %all-gather.6.cloned.1.call-update) | async-done | bytes 6291472 | tf_op jit(solution)/shard_map/all_gather | solution.py:69
  205.3 7.0 %fusion.3 = f32[768,448]{0,1:T(8,128)S(1)} fusion(bf16[768,1,4096]{2,0,1:T(8,128)(2,1)} %all-gather.6.cloned.1.call-done, bf16[1,4096,448]{1,2,0:T(8,128)(2,1)} %param.26), kind=kOutput, calls=%fused_computation.3 | convolution fusion | flops 2818572288 | bytes 11337728 | tf_op jit(solution)/shard_map/ned,edf->nf/dot_general | solution.py:158
  212.4 3.1 %fusion.16 = bf16[768,448]{0,1:T(8,128)(2,1)S(1)} fusion(bf16[1,4096,448]{1,2,0:T(8,128)(2,1)S(1)} %copy-done.7, bf16[768,1,4096]{2,0,1:T(8,128)(2,1)S(1)} %copy-done.6, f32[768,448]{0,1:T(8,128)S(1)} %fusion.3), kind=kOutput, calls=%fused_computation.15 | convolution fusion | flops 2820636672 | bytes 12025856 | tf_op jit(solution)/shard_map/ned,edf->nf/dot_general | solution.py:159
  215.8 0.5 fusion.66
  216.5 4.1 %convolution_add_fusion = f32[64,4096]{1,0:T(8,128)S(1)} fusion(f32[64,448]{1,0:T(8,128)S(1)} %reshape.482, bf16[1,448,4096]{2,1,0:T(8,128)(2,1)} %param.28, f32[4096]{0:T(1024)S(1)} %get-tuple-element.2, pred[64]{0:T(512)(128)(4,1)S(1)} %iota_compare_fusion.5), kind=kOutput, calls=%fused_computation.5 | convolution fusion | flops 1409810432 | bytes 4849728 | tf_op jit(solution)/shard_map/dot_general | solution.py:167
  220.7 19.2 %all_to_all.33 = f32[64,8,512]{2,0,1:T(8,128)S(1)} all-to-all(f32[64,8,512]{2,0,1:T(8,128)S(1)} %bitcast.119), channel_id=1, replica_groups=mesh['z'=8,'y'=4,'expert'=8] {'expert'}, dimensions={1} | all-to-all | bytes 2097152 | tf_op jit(solution)/shard_map/all_to_all | solution.py:59
  240.0 0.7 reshape.484
  240.7 7.2 %all-to-all-start.3 = ((f32[32,2,512]{2,1,0:T(2,128)}), f32[32,2,512]{2,1,0:T(2,128)S(1)}, u32[]{:S(2)}, u32[]{:S(2)}) async-start(f32[32,2,512]{2,1,0:T(2,128)} %reshape.484), calls=%async_computation.3 | async-start | bytes 262144 | tf_op jit(solution)/shard_map/all_to_all | solution.py:59
  248.0 10.4 %all-to-all-done.3 = f32[32,2,512]{2,1,0:T(2,128)S(1)} async-done(((f32[32,2,512]{2,1,0:T(2,128)}), f32[32,2,512]{2,1,0:T(2,128)S(1)}, u32[]{:S(2)}, u32[]{:S(2)}) %all-to-all-start.3) | async-done | bytes 131104 | tf_op jit(solution)/shard_map/all_to_all | solution.py:59
  258.6 1.1 collective-permute-done
  259.8 1.4 collective-permute-start.1
  261.2 2.2 collective-permute-done.1
  263.4 1.4 collective-permute-start.2
  264.8 3.7 %collective-permute-done.2 = f32[2]{0:T(128)S(1)} collective-permute-done((f32[2]{0:T(128)S(1)}, f32[2]{0:T(128)S(1)}, u32[]{:S(2)}, u32[]{:S(2)}) %collective-permute-start.2) | collective-permute-done | bytes 40 | tf_op jit(solution)/shard_map/ppermute | solution.py:75
  268.5 0.7 broadcast_in_dim.191
  269.2 3.9 %all-to-all-start.4 = ((bf16[32,2,512]{2,1,0:T(2,128)(2,1)}), bf16[32,2,512]{2,1,0:T(2,128)(2,1)S(1)}, u32[]{:S(2)}, u32[]{:S(2)}) async-start(bf16[32,2,512]{2,1,0:T(2,128)(2,1)} %broadcast_in_dim.191), calls=%async_computation.4 | async-start | bytes 131072 | tf_op jit(solution)/shard_map/all_to_all | solution.py:65
  273.1 10.0 %all-to-all-done.4 = bf16[32,2,512]{2,1,0:T(2,128)(2,1)S(1)} async-done(((bf16[32,2,512]{2,1,0:T(2,128)(2,1)}), bf16[32,2,512]{2,1,0:T(2,128)(2,1)S(1)}, u32[]{:S(2)}, u32[]{:S(2)}) %all-to-all-start.4) | async-done | bytes 65568 | tf_op jit(solution)/shard_map/all_to_all | solution.py:65
  283.1 0.4 fusion.61
  283.5 0.8 fusion.28
  (76 shorter events, 3.1 us)
Async XLA Ops:
  7.2 16.8 %copy-start = (bf16[2,1024,128]{2,1,0:T(8,128)(2,1)S(1)}, bf16[2,1024,128]{2,1,0:T(8,128)(2,1)}, u32[]{:S(2)}) copy-start(bf16[2,1024,128]{2,1,0:T(8,128)(2,1)} %param.20) | copy-start | bytes 1572868
  7.2 18.5 %copy-start.10 = (bf16[64,128]{1,0:T(8,128)(2,1)S(1)}, bf16[64,128]{1,0:T(8,128)(2,1)}, u32[]{:S(2)}) copy-start(bf16[64,128]{1,0:T(8,128)(2,1)} %param.19) | copy-start | bytes 49156
  7.2 18.7 %copy-start.8 = (bf16[2,1024,128]{2,1,0:T(8,128)(2,1)S(1)}, bf16[2,1024,128]{2,1,0:T(8,128)(2,1)}, u32[]{:S(2)}) copy-start(bf16[2,1024,128]{2,1,0:T(8,128)(2,1)} %param.21) | copy-start | bytes 1572868
  7.2 73.5 %all-gather.4.cloned.1.call-start = ((), (), s32[]{:S(2)}) async-start(), calls=%async_computation.5 | async-start | bytes 4718592 | tf_op jit(solution)/shard_map/all_gather | solution.py:69
  26.4 63.1 %copy-start.5 = (s32[8,2]{0,1:T(2,128)S(1)}, s32[8,2]{0,1:T(2,128)}, u32[]{:S(2)}) copy-start(s32[8,2]{0,1:T(2,128)} %param.25) | copy-start | bytes 196
  26.4 77.6 %copy-start.1 = (bf16[8,4096]{1,0:T(8,128)(2,1)S(1)}, bf16[8,4096]{1,0:T(8,128)(2,1)}, u32[]{:S(2)}) copy-start(bf16[8,4096]{1,0:T(8,128)(2,1)} %param.16) | copy-start | bytes 196612
  26.4 77.8 %copy-start.2 = (f32[4096]{0:T(1024)S(1)}, f32[4096]{0:T(1024)}, u32[]{:S(2)}) copy-start(f32[4096]{0:T(1024)} %param.23) | copy-start | bytes 49156
  84.7 19.3 %all-to-all-start = ((f32[8,8,4096]{2,1,0:T(8,128)}), f32[8,8,4096]{2,1,0:T(8,128)S(1)}, u32[]{:S(2)}, u32[]{:S(2)}) async-start(f32[8,8,4096]{2,1,0:T(8,128)} %fusion.5), calls=%async_computation | async-start | bytes 2097152 | tf_op jit(solution)/shard_map/all_to_all | solution.py:59
  89.5 43.4 %copy-start.9 = (bf16[4096,8]{0,1:T(8,128)(2,1)S(1)}, bf16[4096,8]{0,1:T(8,128)(2,1)}, u32[]{:S(2)}) copy-start(bf16[4096,8]{0,1:T(8,128)(2,1)} %param.24) | copy-start | bytes 196612
  89.5 115.8 %all-gather.6.cloned.1.call-start = ((), (), s32[]{:S(2)}) async-start(), calls=%async_computation.6 | async-start | bytes 7077888 | tf_op jit(solution)/shard_map/all_gather | solution.py:69
  205.3 7.1 %copy-start.6 = (bf16[768,1,4096]{2,0,1:T(8,128)(2,1)S(1)}, bf16[768,1,4096]{2,0,1:T(8,128)(2,1)}, u32[]{:S(2)}) copy-start(bf16[768,1,4096]{2,0,1:T(8,128)(2,1)} %all-gather.6.cloned.1.call-done) | copy-start | bytes 18874372
  205.3 7.1 %copy-start.7 = (bf16[1,4096,448]{1,2,0:T(8,128)(2,1)S(1)}, bf16[1,4096,448]{1,2,0:T(8,128)(2,1)}, u32[]{:S(2)}) copy-start(bf16[1,4096,448]{1,2,0:T(8,128)(2,1)} %param.27) | copy-start | bytes 11010052
  220.5 27.3 %copy-start.11 = (s32[64]{0:T(128)S(1)}, s32[64]{0:T(128)}, u32[]{:S(2)}) copy-start(s32[64]{0:T(128)} %param.31) | copy-start | bytes 772
  220.6 47.9 %copy-start.4 = (f32[512]{0:T(512)S(1)}, f32[512]{0:T(512)}, u32[]{:S(2)}) copy-start(f32[512]{0:T(512)} %param.29) | copy-start | bytes 6148
  220.6 52.5 %copy-start.12 = (f32[4]{0:T(128)S(1)}, f32[4]{0:T(128)}, u32[]{:S(2)}) copy-start(f32[4]{0:T(128)} %param.30) | copy-start | bytes 52
  240.7 17.7 %all-to-all-start.3 = ((f32[32,2,512]{2,1,0:T(2,128)}), f32[32,2,512]{2,1,0:T(2,128)S(1)}, u32[]{:S(2)}, u32[]{:S(2)}) async-start(f32[32,2,512]{2,1,0:T(2,128)} %reshape.484), calls=%async_computation.3 | async-start | bytes 262144 | tf_op jit(solution)/shard_map/all_to_all | solution.py:59
  258.6 1.2 collective-permute-start
  259.8 3.6 %collective-permute-start.1 = (f32[2]{0:T(128)S(1)}, f32[2]{0:T(128)S(1)}, u32[]{:S(2)}, u32[]{:S(2)}) collective-permute-start(f32[2]{0:T(128)S(1)} %add.117), channel_id=1, source_target_pairs={{0,2},{1,3},{2,0},{3,1},{4,6},{5,7},{6,4},{7,5},{8,10},{9,11},{10,... | collective-permute-start | bytes 32 | tf_op jit(solution)/shard_map/ppermute | solution.py:75
  263.4 5.1 %collective-permute-start.2 = (f32[2]{0:T(128)S(1)}, f32[2]{0:T(128)S(1)}, u32[]{:S(2)}, u32[]{:S(2)}) collective-permute-start(f32[2]{0:T(128)S(1)} %add.118), channel_id=1, source_target_pairs={{0,4},{1,5},{2,6},{3,7},{4,0},{5,1},{6,2},{7,3},{8,12},{9,13},{10,... | collective-permute-start | bytes 32 | tf_op jit(solution)/shard_map/ppermute | solution.py:75
  268.5 15.8 %copy-start.3 = (bf16[2,512]{1,0:T(2,128)(2,1)}, bf16[2,512]{1,0:T(2,128)(2,1)S(1)}, u32[]{:S(2)}) copy-start(bf16[2,512]{1,0:T(2,128)(2,1)S(1)} %multiply_convert_fusion.1) | copy-start | bytes 6148
  269.2 13.9 %all-to-all-start.4 = ((bf16[32,2,512]{2,1,0:T(2,128)(2,1)}), bf16[32,2,512]{2,1,0:T(2,128)(2,1)S(1)}, u32[]{:S(2)}, u32[]{:S(2)}) async-start(bf16[32,2,512]{2,1,0:T(2,128)(2,1)} %broadcast_in_dim.191), calls=%async_computation.4 | async-start | bytes 131072 | tf_op jit(solution)/shard_map/all_to_all | solution.py:65
Sparse Core Ops, SparseCore 0:
  23.2 57.4 all-gather.3
  132.7 72.5 all-gather.5

commit v6 on v5

--- a/solution.py
+++ b/solution.py
@@ -104,12 +104,18 @@
     slice_width = width // expert_count
     highest_precision = lax.Precision.HIGHEST
     attended = attend(queries, new_keys, new_values, cache_keys, cache_values)
-    head_terms = jnp.dot(
-        attended,
-        dp_gather(out_weight, 1),
-        preferred_element_type=jnp.float32,
-    )
-    mixed = residual.astype(jnp.float32) + a2a_sum(head_terms, "expert", 0, expert_count)
+    y_count = lax.axis_size("y")
+    z_count = lax.axis_size("z")
+    attended_row = lax.all_gather(attended, "y", axis=0, tiled=True)
+    weight_row = lax.all_gather(out_weight, "z", axis=1, tiled=True)
+    col_block = out_weight.shape[1]
+    head_terms = jnp.dot(attended_row, weight_row, preferred_element_type=jnp.float32)
+    head_terms = head_terms.reshape(y_count, expert_count, tok_local, z_count * col_block)
+    head_terms = head_terms.transpose(1, 0, 2, 3)
+    token_cols = a2a_sum(head_terms, "expert", 0, expert_count)[0]
+    token_cols = lax.all_to_all(token_cols, "y", split_axis=0, concat_axis=0, tiled=True)
+    token_cols = token_cols.reshape(y_count, tok_local, z_count, col_block).transpose(1, 2, 0, 3)
+    mixed = residual.astype(jnp.float32) + token_cols.reshape(tok_local, width)
     normed = (
         mixed * lax.rsqrt(jnp.mean(mixed * mixed, axis=-1, keepdims=True) + EPSILON) * ffn_gain
     ).astype(jnp.bfloat16)

time: 292 us -> 272 us (0.932)
  waiting for transfers between devices: 124 us -> 103 us
  starting transfers between devices: 18.7 us -> 23.1 us
  blocking collectives: 107 us -> 104 us
    all_gather x2 -> x1, waiting for transfers between devices: 82 us -> 26.9 us  [dp_gather(): lax.all_gather(lax.all_gather(x, 'y', axis=axis, tiled=True), 'z', axis=a...]
    all_gather x0 -> x1, waiting for transfers between devices: none -> 27.3 us  [shards(): weight_row = lax.all_gather(out_weight, 'z', axis=1, tiled=True)]
    all_gather x2 -> x1, blocking collectives: 30.3 us -> 14.7 us  [dp_gather(): lax.all_gather(x, 'y', axis=axis, tiled=True)]
    all_gather x0 -> x1, blocking collectives: none -> 12.8 us  [shards(): attended_row = lax.all_gather(attended, 'y', axis=0, tiled=True)]
    all_to_all x0 -> x1, waiting for transfers between devices: none -> 5.96 us  [shards(): lax.all_to_all(token_cols, 'y', split_axis=0, concat_axis=0, tiled=True)]
    all_to_all x0 -> x1, starting transfers between devices: none -> 4.42 us  [shards(): lax.all_to_all(token_cols, 'y', split_axis=0, concat_axis=0, tiled=True)]
  transfers between devices with their start and end apart: 8 -> 9, of which waited for: 8 -> 9; matrix products, arithmetic and copies ran while one was open for 1% -> 2% of each run, Pallas kernels for 0% -> 0%
where the time goes in v6:
time: 272 us; the launch traced here: 271 us
  blocking collectives  104 us (38%)
  waiting for transfers between devices  103 us (38%)
  starting transfers between devices  23.1 us (8%)
  matrix products  20.6 us (8%)
  between operations  14.5 us (5%)
  local copies, waits for them, and re-layouts  4.27 us (2%)
    all_gather x1, blocking collectives, shards(): gathered_weight = lax.all_gather(pool_weight, DP, axis=0, tiled=True)  44 us
    all_gather x1, waiting for transfers between devices, shards(): weight_row = lax.all_gather(out_weight, 'z', axis=1, tiled=True)  27.3 us
    all_gather x1, waiting for transfers between devices, dp_gather(): lax.all_gather(lax.all_gather(x, 'y', axis=axis, tiled=True), 'z', axis=a...  26.9 us
    all_to_all x2, waiting for transfers between devices, a2a_sum(): lax.all_to_all(x.reshape(split), axis, split_axis=dim, concat_axis=dim, t...  24.8 us
    all_to_all x1, blocking collectives, a2a_sum(): lax.all_to_all(x.reshape(split), axis, split_axis=dim, concat_axis=dim, t...  19.2 us
    all_gather x1, blocking collectives, dp_gather(): lax.all_gather(x, 'y', axis=axis, tiled=True)  14.7 us
    all_to_all x1, blocking collectives, shards(): lax.all_to_all(outgoing, 'expert', split_axis=0, concat_axis=1, tiled=True)  12.9 us
    all_gather x1, blocking collectives, shards(): attended_row = lax.all_gather(attended, 'y', axis=0, tiled=True)  12.8 us
  transfers between devices with their start and end apart: 9, of which 9 were waited for; matrix products, arithmetic and copies ran while one was open for 2% of the time, Pallas kernels for 0%

profile of v6, /device:TPU:2, one launch (start us, length us, event | category | flops | bytes accessed | tf_op | source)
XLA Modules:
  0.0 271.3 jit_solution(14118267845998968763)
XLA Ops:
  7.2 0.7 all-gather.4.cloned.1.call-update
  7.9 0.9 reshape.484
  9.2 1.0 fusion.58
  10.5 0.9 fusion.34
  11.9 12.8 %all_gather.15 = bf16[256,512]{1,0:T(8,128)(2,1)S(1)} all-gather(bf16[64,512]{1,0:T(8,128)(2,1)S(1)} %bitcast.145), channel_id=1, replica_groups=mesh['z'=8,'y'=4,'expert'=8] {'y'}, dimensions={0}, use_global_device_ids=true | all-gather | bytes 327680 | tf_op jit(solution)/shard_map/all_gather | solution.py:109
  24.7 27.3 %all-gather.4.cloned.1.call-done = bf16[512,1024]{1,0:T(8,128)(2,1)} async-done(((bf16[512,128]{1,0:T(8,128)(2,1)}), bf16[512,1024]{1,0:T(8,128)(2,1)}) %all-gather.4.cloned.1.call-update) | async-done | bytes 1048592 | tf_op jit(solution)/shard_map/all_gather | solution.py:110
  52.0 1.7 fusion.64
  53.7 1.1 copy.109
  54.8 4.8 %all-to-all-start = ((f32[8,1,4,8,1024]{4,3,2,1,0:T(8,128)}), f32[8,1,4,8,1024]{4,3,2,1,0:T(8,128)S(1)}, u32[]{:S(2)}, u32[]{:S(2)}) async-start(f32[8,1,4,8,1024]{4,3,2,1,0:T(8,128)} %bitcast.131), calls=%async_computation | async-start | bytes 2097152 | tf_op jit(solution)/shard_map/all_to_all | solution.py:59
  59.6 14.5 %all-to-all-done = f32[8,1,4,8,1024]{4,3,2,1,0:T(8,128)S(1)} async-done(((f32[8,1,4,8,1024]{4,3,2,1,0:T(8,128)}), f32[8,1,4,8,1024]{4,3,2,1,0:T(8,128)S(1)}, u32[]{:S(2)}, u32[]{:S(2)}) %all-to-all-start) | async-done | bytes 1048608 | tf_op jit(solution)/shard_map/all_to_all | solution.py:59
  74.1 0.7 reduce_sum.121
  74.8 4.4 %all-to-all-start.1 = ((f32[4,8,1024]{2,1,0:T(8,128)}), f32[4,8,1024]{2,1,0:T(8,128)S(1)}, u32[]{:S(2)}, u32[]{:S(2)}) async-start(f32[4,8,1024]{2,1,0:T(8,128)} %reduce_sum.121), calls=%async_computation.1 | async-start | bytes 262144 | tf_op jit(solution)/shard_map/all_to_all | solution.py:116
  79.2 6.0 %all-to-all-done.1 = f32[4,8,1024]{2,1,0:T(8,128)S(1)} async-done(((f32[4,8,1024]{2,1,0:T(8,128)}), f32[4,8,1024]{2,1,0:T(8,128)S(1)}, u32[]{:S(2)}, u32[]{:S(2)}) %all-to-all-start.1) | async-done | bytes 131104 | tf_op jit(solution)/shard_map/all_to_all | solution.py:116
  85.9 12.9 %all_to_all.37 = bf16[8,8,4224]{2,1,0:T(8,128)(2,1)S(1)} all-to-all(bf16[8,8,4224]{2,1,0:T(8,128)(2,1)S(1)} %pad_maximum_fusion), channel_id=1, replica_groups=mesh['z'=8,'y'=4,'expert'=8] {'expert'}, dimensions={0} | all-to-all | bytes 1081344 | tf_op jit(solution)/shard_map/all_to_all | solution.py:132
  99.4 14.7 %all_gather.18 = bf16[96,1,4096]{2,0,1:T(8,128)(2,1)} all-gather(bf16[24,1,4096]{2,0,1:T(8,128)(2,1)S(1)} %bitcast.142), channel_id=1, replica_groups=mesh['z'=8,'y'=4,'expert'=8] {'y'}, dimensions={0}, use_global_device_ids=true | all-gather | bytes 983040 | tf_op jit(solution)/shard_map/all_gather | solution.py:69
  114.6 44.0 %all-gather = f32[32,24,2]{1,2,0:T(2,128)S(1)} all-gather(f32[1,24,2]{1,2,0:T(2,128)S(1)} %fusion.55), channel_id=1, replica_groups=mesh['z'=8,'y'=4,'expert'=8] {'z','y'}, dimensions={0}, use_global_device_ids=true | all-gather | bytes 6336 | tf_op jit(solution)/shard_map/all_gather | solution.py:162
  158.6 26.9 %all-gather.6.cloned.1.call-done = bf16[768,1,4096]{2,0,1:T(8,128)(2,1)} async-done(((bf16[96,1,4096]{2,0,1:T(8,128)(2,1)}), bf16[768,1,4096]{2,0,1:T(8,128)(2,1)}) %all-gather.6.cloned.1.call-update) | async-done | bytes 6291472 | tf_op jit(solution)/shard_map/all_gather | solution.py:69
  185.6 7.0 %fusion.3 = f32[768,448]{0,1:T(8,128)S(1)} fusion(bf16[768,1,4096]{2,0,1:T(8,128)(2,1)} %all-gather.6.cloned.1.call-done, bf16[1,4096,448]{1,2,0:T(8,128)(2,1)} %param.26), kind=kOutput, calls=%fused_computation.3 | convolution fusion | flops 2818572288 | bytes 11337728 | tf_op jit(solution)/shard_map/ned,edf->nf/dot_general | solution.py:164
  192.6 3.1 %fusion.14 = bf16[768,448]{0,1:T(8,128)(2,1)S(1)} fusion(bf16[1,4096,448]{1,2,0:T(8,128)(2,1)S(1)} %copy-done.7, bf16[768,1,4096]{2,0,1:T(8,128)(2,1)S(1)} %copy-done.6, f32[768,448]{0,1:T(8,128)S(1)} %fusion.3), kind=kOutput, calls=%fused_computation.13 | convolution fusion | flops 2820636672 | bytes 12025856 | tf_op jit(solution)/shard_map/ned,edf->nf/dot_general | solution.py:165
  196.7 4.1 %convolution_add_fusion = f32[64,4096]{1,0:T(8,128)S(1)} fusion(f32[64,448]{1,0:T(8,128)S(1)} %reshape.500, bf16[1,448,4096]{2,1,0:T(8,128)(2,1)} %param.28, f32[4096]{0:T(1024)S(1)} %get-tuple-element.2, pred[64]{0:T(512)(128)(4,1)S(1)} %iota_compare_fusion.5), kind=kOutput, calls=%fused_computation.5 | convolution fusion | flops 1409810432 | bytes 4849728 | tf_op jit(solution)/shard_map/dot_general | solution.py:173
  200.9 19.2 %all_to_all.38 = f32[64,8,512]{2,0,1:T(8,128)S(1)} all-to-all(f32[64,8,512]{2,0,1:T(8,128)S(1)} %bitcast.137), channel_id=1, replica_groups=mesh['z'=8,'y'=4,'expert'=8] {'expert'}, dimensions={1} | all-to-all | bytes 2097152 | tf_op jit(solution)/shard_map/all_to_all | solution.py:59
  220.2 0.7 reshape.502
  220.9 7.1 %all-to-all-start.4 = ((f32[32,2,512]{2,1,0:T(2,128)}), f32[32,2,512]{2,1,0:T(2,128)S(1)}, u32[]{:S(2)}, u32[]{:S(2)}) async-start(f32[32,2,512]{2,1,0:T(2,128)} %reshape.502), calls=%async_computation.4 | async-start | bytes 262144 | tf_op jit(solution)/shard_map/all_to_all | solution.py:59
  228.2 10.4 %all-to-all-done.4 = f32[32,2,512]{2,1,0:T(2,128)S(1)} async-done(((f32[32,2,512]{2,1,0:T(2,128)}), f32[32,2,512]{2,1,0:T(2,128)S(1)}, u32[]{:S(2)}, u32[]{:S(2)}) %all-to-all-start.4) | async-done | bytes 131104 | tf_op jit(solution)/shard_map/all_to_all | solution.py:59
  238.9 1.1 collective-permute-done
  240.0 1.4 collective-permute-start.1
  241.4 2.2 collective-permute-done.1
  243.6 1.4 collective-permute-start.2
  245.0 3.7 %collective-permute-done.2 = f32[2]{0:T(128)S(1)} collective-permute-done((f32[2]{0:T(128)S(1)}, f32[2]{0:T(128)S(1)}, u32[]{:S(2)}, u32[]{:S(2)}) %collective-permute-start.2) | collective-permute-done | bytes 40 | tf_op jit(solution)/shard_map/ppermute | solution.py:75
  249.4 3.9 %all-to-all-start.5 = ((bf16[32,2,512]{2,1,0:T(2,128)(2,1)}), bf16[32,2,512]{2,1,0:T(2,128)(2,1)S(1)}, u32[]{:S(2)}, u32[]{:S(2)}) async-start(bf16[32,2,512]{2,1,0:T(2,128)(2,1)} %broadcast_in_dim.191), calls=%async_computation.5 | async-start | bytes 131072 | tf_op jit(solution)/shard_map/all_to_all | solution.py:65
  253.3 10.0 %all-to-all-done.5 = bf16[32,2,512]{2,1,0:T(2,128)(2,1)S(1)} async-done(((bf16[32,2,512]{2,1,0:T(2,128)(2,1)}), bf16[32,2,512]{2,1,0:T(2,128)(2,1)S(1)}, u32[]{:S(2)}, u32[]{:S(2)}) %all-to-all-start.5) | async-done | bytes 65568 | tf_op jit(solution)/shard_map/all_to_all | solution.py:65
  263.7 0.8 fusion.26
  (80 shorter events, 5.6 us)
Async XLA Ops:
  7.2 1.6 copy-start
  7.2 4.3 %copy-start.8 = (bf16[2,1024,128]{2,1,0:T(8,128)(2,1)S(1)}, bf16[2,1024,128]{2,1,0:T(8,128)(2,1)}, u32[]{:S(2)}) copy-start(bf16[2,1024,128]{2,1,0:T(8,128)(2,1)} %param.21) | copy-start | bytes 1572868
  7.2 44.8 %all-gather.4.cloned.1.call-start = ((), (), s32[]{:S(2)}) async-start(), calls=%async_computation.6 | async-start | bytes 1179648 | tf_op jit(solution)/shard_map/all_gather | solution.py:110
  11.9 47.7 %copy-start.5 = (s32[8,2]{0,1:T(2,128)S(1)}, s32[8,2]{0,1:T(2,128)}, u32[]{:S(2)}) copy-start(s32[8,2]{0,1:T(2,128)} %param.25) | copy-start | bytes 196
  53.7 31.7 %copy-start.1 = (bf16[8,4096]{1,0:T(8,128)(2,1)S(1)}, bf16[8,4096]{1,0:T(8,128)(2,1)}, u32[]{:S(2)}) copy-start(bf16[8,4096]{1,0:T(8,128)(2,1)} %param.16) | copy-start | bytes 196612
  53.7 31.9 %copy-start.2 = (f32[4096]{0:T(1024)S(1)}, f32[4096]{0:T(1024)}, u32[]{:S(2)}) copy-start(f32[4096]{0:T(1024)} %param.23) | copy-start | bytes 49156
  54.8 19.3 %all-to-all-start = ((f32[8,1,4,8,1024]{4,3,2,1,0:T(8,128)}), f32[8,1,4,8,1024]{4,3,2,1,0:T(8,128)S(1)}, u32[]{:S(2)}, u32[]{:S(2)}) async-start(f32[8,1,4,8,1024]{4,3,2,1,0:T(8,128)} %bitcast.131), calls=%async_computation | async-start | bytes 2097152 | tf_op jit(solution)/shard_map/all_to_all | solution.py:59
  74.8 39.6 %copy-start.9 = (bf16[4096,8]{0,1:T(8,128)(2,1)S(1)}, bf16[4096,8]{0,1:T(8,128)(2,1)}, u32[]{:S(2)}) copy-start(bf16[4096,8]{0,1:T(8,128)(2,1)} %param.24) | copy-start | bytes 196612
  74.8 10.4 %all-to-all-start.1 = ((f32[4,8,1024]{2,1,0:T(8,128)}), f32[4,8,1024]{2,1,0:T(8,128)S(1)}, u32[]{:S(2)}, u32[]{:S(2)}) async-start(f32[4,8,1024]{2,1,0:T(8,128)} %reduce_sum.121), calls=%async_computation.1 | async-start | bytes 262144 | tf_op jit(solution)/shard_map/all_to_all | solution.py:116
  79.2 106.4 %all-gather.6.cloned.1.call-start = ((), (), s32[]{:S(2)}) async-start(), calls=%async_computation.7 | async-start | bytes 7077888 | tf_op jit(solution)/shard_map/all_gather | solution.py:69
  185.6 7.1 %copy-start.6 = (bf16[768,1,4096]{2,0,1:T(8,128)(2,1)S(1)}, bf16[768,1,4096]{2,0,1:T(8,128)(2,1)}, u32[]{:S(2)}) copy-start(bf16[768,1,4096]{2,0,1:T(8,128)(2,1)} %all-gather.6.cloned.1.call-done) | copy-start | bytes 18874372
  185.6 7.1 %copy-start.7 = (bf16[1,4096,448]{1,2,0:T(8,128)(2,1)S(1)}, bf16[1,4096,448]{1,2,0:T(8,128)(2,1)}, u32[]{:S(2)}) copy-start(bf16[1,4096,448]{1,2,0:T(8,128)(2,1)} %param.27) | copy-start | bytes 11010052
  200.8 27.3 %copy-start.10 = (s32[64]{0:T(128)S(1)}, s32[64]{0:T(128)}, u32[]{:S(2)}) copy-start(s32[64]{0:T(128)} %param.31) | copy-start | bytes 772
  200.8 47.9 %copy-start.4 = (f32[512]{0:T(512)S(1)}, f32[512]{0:T(512)}, u32[]{:S(2)}) copy-start(f32[512]{0:T(512)} %param.29) | copy-start | bytes 6148
  200.8 52.5 %copy-start.11 = (f32[4]{0:T(128)S(1)}, f32[4]{0:T(128)}, u32[]{:S(2)}) copy-start(f32[4]{0:T(128)} %param.30) | copy-start | bytes 52
  220.9 17.7 %all-to-all-start.4 = ((f32[32,2,512]{2,1,0:T(2,128)}), f32[32,2,512]{2,1,0:T(2,128)S(1)}, u32[]{:S(2)}, u32[]{:S(2)}) async-start(f32[32,2,512]{2,1,0:T(2,128)} %reshape.502), calls=%async_computation.4 | async-start | bytes 262144 | tf_op jit(solution)/shard_map/all_to_all | solution.py:59
  238.8 1.2 collective-permute-start
  240.0 3.6 %collective-permute-start.1 = (f32[2]{0:T(128)S(1)}, f32[2]{0:T(128)S(1)}, u32[]{:S(2)}, u32[]{:S(2)}) collective-permute-start(f32[2]{0:T(128)S(1)} %add.117), channel_id=1, source_target_pairs={{0,2},{1,3},{2,0},{3,1},{4,6},{5,7},{6,4},{7,5},{8,10},{9,11},{10,... | collective-permute-start | bytes 32 | tf_op jit(solution)/shard_map/ppermute | solution.py:75
  243.6 5.1 %collective-permute-start.2 = (f32[2]{0:T(128)S(1)}, f32[2]{0:T(128)S(1)}, u32[]{:S(2)}, u32[]{:S(2)}) collective-permute-start(f32[2]{0:T(128)S(1)} %add.118), channel_id=1, source_target_pairs={{0,4},{1,5},{2,6},{3,7},{4,0},{5,1},{6,2},{7,3},{8,12},{9,13},{10,... | collective-permute-start | bytes 32 | tf_op jit(solution)/shard_map/ppermute | solution.py:75
  248.7 15.8 %copy-start.3 = (bf16[2,512]{1,0:T(2,128)(2,1)}, bf16[2,512]{1,0:T(2,128)(2,1)S(1)}, u32[]{:S(2)}) copy-start(bf16[2,512]{1,0:T(2,128)(2,1)S(1)} %multiply_convert_fusion.1) | copy-start | bytes 6148
  249.4 13.9 %all-to-all-start.5 = ((bf16[32,2,512]{2,1,0:T(2,128)(2,1)}), bf16[32,2,512]{2,1,0:T(2,128)(2,1)S(1)}, u32[]{:S(2)}, u32[]{:S(2)}) async-start(bf16[32,2,512]{2,1,0:T(2,128)(2,1)} %broadcast_in_dim.191), calls=%async_computation.5 | async-start | bytes 131072 | tf_op jit(solution)/shard_map/all_to_all | solution.py:65
Sparse Core Ops, SparseCore 0:
  9.7 42.2 all-gather.3
  114.2 71.2 all-gather.5

commit v7 on v6

--- a/solution.py
+++ b/solution.py
@@ -107,9 +107,11 @@
     y_count = lax.axis_size("y")
     z_count = lax.axis_size("z")
     attended_row = lax.all_gather(attended, "y", axis=0, tiled=True)
-    weight_row = lax.all_gather(out_weight, "z", axis=1, tiled=True)
+    weight_row = a2a_gather(out_weight, "z", z_count)
     col_block = out_weight.shape[1]
-    head_terms = jnp.dot(attended_row, weight_row, preferred_element_type=jnp.float32)
+    head_terms = jnp.einsum(
+        "th,zhc->tzc", attended_row, weight_row, preferred_element_type=jnp.float32
+    )
     head_terms = head_terms.reshape(y_count, expert_count, tok_local, z_count * col_block)
     head_terms = head_terms.transpose(1, 0, 2, 3)
     token_cols = a2a_sum(head_terms, "expert", 0, expert_count)[0]

time: 272 us -> 263 us (0.967)
  waiting for transfers between devices: 103 us -> 87 us
  starting transfers between devices: 23.1 us -> 31.8 us
  local copies, waits for them, and re-layouts: 4.27 us -> 7.12 us
    all_gather x1 -> x0, waiting for transfers between devices: 27.3 us -> none  [shards(): weight_row = lax.all_gather(out_weight, 'z', axis=1, tiled=True)]
    all_to_all x1 -> x2, waiting for transfers between devices: 10 us -> 23.4 us  [a2a_gather(): return lax.all_to_all(spread, axis, split_axis=0, concat_axis=0, tiled=True)]
    all_to_all x1 -> x2, starting transfers between devices: 3.85 us -> 12.3 us  [a2a_gather(): return lax.all_to_all(spread, axis, split_axis=0, concat_axis=0, tiled=True)]
  transfers between devices with their start and end apart: 9 -> 9, of which waited for: 9 -> 9; matrix products, arithmetic and copies ran while one was open for 2% -> 1% of each run, Pallas kernels for 0% -> 0%
where the time goes in v7:
time: 263 us
  blocking collectives  102 us (39%)
  waiting for transfers between devices  87 us (33%)
  starting transfers between devices  31.8 us (12%)
  matrix products  18 us (7%)
  between operations  14.5 us (6%)
  local copies, waits for them, and re-layouts  7.12 us (3%)
    all_gather x1, blocking collectives, shards(): gathered_weight = lax.all_gather(pool_weight, DP, axis=0, tiled=True)  42.2 us
    all_gather x1, waiting for transfers between devices, dp_gather(): lax.all_gather(lax.all_gather(x, 'y', axis=axis, tiled=True), 'z', axis=a...  25.8 us
    all_to_all x2, waiting for transfers between devices, a2a_sum(): lax.all_to_all(x.reshape(split), axis, split_axis=dim, concat_axis=dim, t...  24.8 us
    all_to_all x2, waiting for transfers between devices, a2a_gather(): return lax.all_to_all(spread, axis, split_axis=0, concat_axis=0, tiled=True)  23.4 us
    all_to_all x1, blocking collectives, a2a_sum(): lax.all_to_all(x.reshape(split), axis, split_axis=dim, concat_axis=dim, t...  19.2 us
    all_gather x1, blocking collectives, dp_gather(): lax.all_gather(x, 'y', axis=axis, tiled=True)  14.7 us
    all_to_all x1, blocking collectives, shards(): lax.all_to_all(outgoing, 'expert', split_axis=0, concat_axis=1, tiled=True)  12.9 us
    all_gather x1, blocking collectives, shards(): attended_row = lax.all_gather(attended, 'y', axis=0, tiled=True)  12.8 us
  transfers between devices with their start and end apart: 9, of which 9 were waited for; matrix products, arithmetic and copies ran while one was open for 1% of the time, Pallas kernels for 0%

profile of v7, /device:TPU:2, one launch (start us, length us, event | category | flops | bytes accessed | tf_op | source)
XLA Modules:
  0.0 262.7 jit_solution(15683637962642243952)
XLA Ops:
  7.2 2.1 broadcast_in_dim.183
  9.3 8.5 %all-to-all-start = ((bf16[8,512,128]{2,1,0:T(8,128)(2,1)}), bf16[8,512,128]{2,1,0:T(8,128)(2,1)S(1)}, u32[]{:S(2)}, u32[]{:S(2)}) async-start(bf16[8,512,128]{2,1,0:T(8,128)(2,1)} %broadcast_in_dim.183), calls=%async_computation | async-start | bytes 2097152 | tf_op jit(solution)/shard_map/all_to_all | solution.py:65
  17.8 0.9 reshape.485
  20.4 12.8 %all_gather.12 = bf16[256,512]{1,0:T(8,128)(2,1)S(1)} all-gather(bf16[64,512]{1,0:T(8,128)(2,1)S(1)} %bitcast.144), channel_id=1, replica_groups=mesh['z'=8,'y'=4,'expert'=8] {'y'}, dimensions={0}, use_global_device_ids=true | all-gather | bytes 327680 | tf_op jit(solution)/shard_map/all_gather | solution.py:109
  33.2 13.4 %all-to-all-done = bf16[8,512,128]{2,1,0:T(8,128)(2,1)S(1)} async-done(((bf16[8,512,128]{2,1,0:T(8,128)(2,1)}), bf16[8,512,128]{2,1,0:T(8,128)(2,1)S(1)}, u32[]{:S(2)}, u32[]{:S(2)}) %all-to-all-start) | async-done | bytes 1048608 | tf_op jit(solution)/shard_map/all_to_all | solution.py:65
  47.0 0.6 copy.76
  47.8 1.1 copy.77
  48.8 4.8 %all-to-all-start.1 = ((f32[8,1,4,8,1024]{4,3,2,1,0:T(8,128)}), f32[8,1,4,8,1024]{4,3,2,1,0:T(8,128)S(1)}, u32[]{:S(2)}, u32[]{:S(2)}) async-start(f32[8,1,4,8,1024]{4,3,2,1,0:T(8,128)} %copy.77), calls=%async_computation.1 | async-start | bytes 2097152 | tf_op jit(solution)/shard_map/all_to_all | solution.py:59
  53.7 14.5 %all-to-all-done.1 = f32[8,1,4,8,1024]{4,3,2,1,0:T(8,128)S(1)} async-done(((f32[8,1,4,8,1024]{4,3,2,1,0:T(8,128)}), f32[8,1,4,8,1024]{4,3,2,1,0:T(8,128)S(1)}, u32[]{:S(2)}, u32[]{:S(2)}) %all-to-all-start.1) | async-done | bytes 1048608 | tf_op jit(solution)/shard_map/all_to_all | solution.py:59
  68.2 0.7 reduce_sum.121
  68.9 4.6 %all-to-all-start.2 = ((f32[4,8,1024]{2,1,0:T(8,128)}), f32[4,8,1024]{2,1,0:T(8,128)S(1)}, u32[]{:S(2)}, u32[]{:S(2)}) async-start(f32[4,8,1024]{2,1,0:T(8,128)} %reduce_sum.121), calls=%async_computation.2 | async-start | bytes 262144 | tf_op jit(solution)/shard_map/all_to_all | solution.py:118
  73.5 6.0 %all-to-all-done.2 = f32[4,8,1024]{2,1,0:T(8,128)S(1)} async-done(((f32[4,8,1024]{2,1,0:T(8,128)}), f32[4,8,1024]{2,1,0:T(8,128)S(1)}, u32[]{:S(2)}, u32[]{:S(2)}) %all-to-all-start.2) | async-done | bytes 131104 | tf_op jit(solution)/shard_map/all_to_all | solution.py:118
  80.1 12.9 %all_to_all.42 = bf16[8,8,4224]{2,1,0:T(8,128)(2,1)S(1)} all-to-all(bf16[8,8,4224]{2,1,0:T(8,128)(2,1)S(1)} %pad_maximum_fusion), channel_id=1, replica_groups=mesh['z'=8,'y'=4,'expert'=8] {'expert'}, dimensions={0} | all-to-all | bytes 1081344 | tf_op jit(solution)/shard_map/all_to_all | solution.py:134
  93.6 14.7 %all_gather.14 = bf16[96,1,4096]{2,0,1:T(8,128)(2,1)} all-gather(bf16[24,1,4096]{2,0,1:T(8,128)(2,1)S(1)} %bitcast.141), channel_id=1, replica_groups=mesh['z'=8,'y'=4,'expert'=8] {'y'}, dimensions={0}, use_global_device_ids=true | all-gather | bytes 983040 | tf_op jit(solution)/shard_map/all_gather | solution.py:69
  108.9 42.2 %all-gather = f32[32,24,2]{1,2,0:T(2,128)S(1)} all-gather(f32[1,24,2]{1,2,0:T(2,128)S(1)} %fusion.57), channel_id=1, replica_groups=mesh['z'=8,'y'=4,'expert'=8] {'z','y'}, dimensions={0}, use_global_device_ids=true | all-gather | bytes 6336 | tf_op jit(solution)/shard_map/all_gather | solution.py:164
  151.1 25.8 %all-gather.3.cloned.1.call-done = bf16[768,1,4096]{2,0,1:T(8,128)(2,1)} async-done(((bf16[96,1,4096]{2,0,1:T(8,128)(2,1)}), bf16[768,1,4096]{2,0,1:T(8,128)(2,1)}) %all-gather.3.cloned.1.call-update) | async-done | bytes 6291472 | tf_op jit(solution)/shard_map/all_gather | solution.py:69
  176.9 7.0 %fusion.3 = f32[768,448]{0,1:T(8,128)S(1)} fusion(bf16[768,1,4096]{2,0,1:T(8,128)(2,1)} %all-gather.3.cloned.1.call-done, bf16[1,4096,448]{1,2,0:T(8,128)(2,1)} %param.26), kind=kOutput, calls=%fused_computation.3 | convolution fusion | flops 2818572288 | bytes 11337728 | tf_op jit(solution)/shard_map/ned,edf->nf/dot_general | solution.py:166
  184.0 3.1 %fusion.14 = bf16[768,448]{0,1:T(8,128)(2,1)S(1)} fusion(bf16[1,4096,448]{1,2,0:T(8,128)(2,1)S(1)} %copy-done.8, bf16[768,1,4096]{2,0,1:T(8,128)(2,1)S(1)} %copy-done.7, f32[768,448]{0,1:T(8,128)S(1)} %fusion.3), kind=kOutput, calls=%fused_computation.13 | convolution fusion | flops 2820636672 | bytes 12025856 | tf_op jit(solution)/shard_map/ned,edf->nf/dot_general | solution.py:167
  188.0 4.1 %convolution_add_fusion = f32[64,4096]{1,0:T(8,128)S(1)} fusion(f32[64,448]{1,0:T(8,128)S(1)} %reshape.501, bf16[1,448,4096]{2,1,0:T(8,128)(2,1)} %param.28, f32[4096]{0:T(1024)S(1)} %get-tuple-element.2, pred[64]{0:T(512)(128)(4,1)S(1)} %iota_compare_fusion.5), kind=kOutput, calls=%fused_computation.5 | convolution fusion | flops 1409810432 | bytes 4849728 | tf_op jit(solution)/shard_map/dot_general | solution.py:175
  192.2 19.2 %all_to_all.43 = f32[64,8,512]{2,0,1:T(8,128)S(1)} all-to-all(f32[64,8,512]{2,0,1:T(8,128)S(1)} %bitcast.136), channel_id=1, replica_groups=mesh['z'=8,'y'=4,'expert'=8] {'expert'}, dimensions={1} | all-to-all | bytes 2097152 | tf_op jit(solution)/shard_map/all_to_all | solution.py:59
  211.5 0.7 reshape.503
  212.2 7.2 %all-to-all-start.5 = ((f32[32,2,512]{2,1,0:T(2,128)}), f32[32,2,512]{2,1,0:T(2,128)S(1)}, u32[]{:S(2)}, u32[]{:S(2)}) async-start(f32[32,2,512]{2,1,0:T(2,128)} %reshape.503), calls=%async_computation.5 | async-start | bytes 262144 | tf_op jit(solution)/shard_map/all_to_all | solution.py:59
  219.6 10.4 %all-to-all-done.5 = f32[32,2,512]{2,1,0:T(2,128)S(1)} async-done(((f32[32,2,512]{2,1,0:T(2,128)}), f32[32,2,512]{2,1,0:T(2,128)S(1)}, u32[]{:S(2)}, u32[]{:S(2)}) %all-to-all-start.5) | async-done | bytes 131104 | tf_op jit(solution)/shard_map/all_to_all | solution.py:59
  230.2 1.1 collective-permute-done
  231.4 1.4 collective-permute-start.1
  232.7 2.2 collective-permute-done.1
  234.9 1.4 collective-permute-start.2
  236.3 3.7 %collective-permute-done.2 = f32[2]{0:T(128)S(1)} collective-permute-done((f32[2]{0:T(128)S(1)}, f32[2]{0:T(128)S(1)}, u32[]{:S(2)}, u32[]{:S(2)}) %collective-permute-start.2) | collective-permute-done | bytes 40 | tf_op jit(solution)/shard_map/ppermute | solution.py:75
  240.1 0.7 broadcast_in_dim.198
  240.7 3.9 %all-to-all-start.6 = ((bf16[32,2,512]{2,1,0:T(2,128)(2,1)}), bf16[32,2,512]{2,1,0:T(2,128)(2,1)S(1)}, u32[]{:S(2)}, u32[]{:S(2)}) async-start(bf16[32,2,512]{2,1,0:T(2,128)(2,1)} %broadcast_in_dim.198), calls=%async_computation.6 | async-start | bytes 131072 | tf_op jit(solution)/shard_map/all_to_all | solution.py:65
  244.6 10.0 %all-to-all-done.6 = bf16[32,2,512]{2,1,0:T(2,128)(2,1)S(1)} async-done(((bf16[32,2,512]{2,1,0:T(2,128)(2,1)}), bf16[32,2,512]{2,1,0:T(2,128)(2,1)S(1)}, u32[]{:S(2)}, u32[]{:S(2)}) %all-to-all-start.6) | async-done | bytes 65568 | tf_op jit(solution)/shard_map/all_to_all | solution.py:65
  255.0 0.8 fusion.26
  (86 shorter events, 5.9 us)
Async XLA Ops:
  7.2 11.5 %copy-start = (bf16[2,1024,128]{2,1,0:T(8,128)(2,1)S(1)}, bf16[2,1024,128]{2,1,0:T(8,128)(2,1)}, u32[]{:S(2)}) copy-start(bf16[2,1024,128]{2,1,0:T(8,128)(2,1)} %param.20) | copy-start | bytes 1572868
  7.2 11.9 %copy-start.2 = (bf16[64,128]{1,0:T(8,128)(2,1)S(1)}, bf16[64,128]{1,0:T(8,128)(2,1)}, u32[]{:S(2)}) copy-start(bf16[64,128]{1,0:T(8,128)(2,1)} %param.18) | copy-start | bytes 49156
  7.2 12.5 %copy-start.11 = (bf16[64,128]{1,0:T(8,128)(2,1)S(1)}, bf16[64,128]{1,0:T(8,128)(2,1)}, u32[]{:S(2)}) copy-start(bf16[64,128]{1,0:T(8,128)(2,1)} %param.19) | copy-start | bytes 49156
  7.2 12.7 %copy-start.9 = (bf16[2,1024,128]{2,1,0:T(8,128)(2,1)S(1)}, bf16[2,1024,128]{2,1,0:T(8,128)(2,1)}, u32[]{:S(2)}) copy-start(bf16[2,1024,128]{2,1,0:T(8,128)(2,1)} %param.21) | copy-start | bytes 1572868
  9.3 37.2 %all-to-all-start = ((bf16[8,512,128]{2,1,0:T(8,128)(2,1)}), bf16[8,512,128]{2,1,0:T(8,128)(2,1)S(1)}, u32[]{:S(2)}, u32[]{:S(2)}) async-start(bf16[8,512,128]{2,1,0:T(8,128)(2,1)} %broadcast_in_dim.183), calls=%async_computation | async-start | bytes 2097152 | tf_op jit(solution)/shard_map/all_to_all | solution.py:65
  47.6 6.1 %copy-start.6 = (s32[8,2]{0,1:T(2,128)S(1)}, s32[8,2]{0,1:T(2,128)}, u32[]{:S(2)}) copy-start(s32[8,2]{0,1:T(2,128)} %param.25) | copy-start | bytes 196
  47.8 31.9 %copy-start.1 = (bf16[8,4096]{1,0:T(8,128)(2,1)S(1)}, bf16[8,4096]{1,0:T(8,128)(2,1)}, u32[]{:S(2)}) copy-start(bf16[8,4096]{1,0:T(8,128)(2,1)} %param.16) | copy-start | bytes 196612
  47.8 32.0 %copy-start.3 = (f32[4096]{0:T(1024)S(1)}, f32[4096]{0:T(1024)}, u32[]{:S(2)}) copy-start(f32[4096]{0:T(1024)} %param.23) | copy-start | bytes 49156
  48.8 19.3 %all-to-all-start.1 = ((f32[8,1,4,8,1024]{4,3,2,1,0:T(8,128)}), f32[8,1,4,8,1024]{4,3,2,1,0:T(8,128)S(1)}, u32[]{:S(2)}, u32[]{:S(2)}) async-start(f32[8,1,4,8,1024]{4,3,2,1,0:T(8,128)} %copy.77), calls=%async_computation.1 | async-start | bytes 2097152 | tf_op jit(solution)/shard_map/all_to_all | solution.py:59
  68.9 39.8 %copy-start.10 = (bf16[4096,8]{0,1:T(8,128)(2,1)S(1)}, bf16[4096,8]{0,1:T(8,128)(2,1)}, u32[]{:S(2)}) copy-start(bf16[4096,8]{0,1:T(8,128)(2,1)} %param.24) | copy-start | bytes 196612
  68.9 10.6 %all-to-all-start.2 = ((f32[4,8,1024]{2,1,0:T(8,128)}), f32[4,8,1024]{2,1,0:T(8,128)S(1)}, u32[]{:S(2)}, u32[]{:S(2)}) async-start(f32[4,8,1024]{2,1,0:T(8,128)} %reduce_sum.121), calls=%async_computation.2 | async-start | bytes 262144 | tf_op jit(solution)/shard_map/all_to_all | solution.py:118
  73.4 103.4 %all-gather.3.cloned.1.call-start = ((), (), s32[]{:S(2)}) async-start(), calls=%async_computation.7 | async-start | bytes 7077888 | tf_op jit(solution)/shard_map/all_gather | solution.py:69
  176.9 7.1 %copy-start.7 = (bf16[768,1,4096]{2,0,1:T(8,128)(2,1)S(1)}, bf16[768,1,4096]{2,0,1:T(8,128)(2,1)}, u32[]{:S(2)}) copy-start(bf16[768,1,4096]{2,0,1:T(8,128)(2,1)} %all-gather.3.cloned.1.call-done) | copy-start | bytes 18874372
  176.9 7.1 %copy-start.8 = (bf16[1,4096,448]{1,2,0:T(8,128)(2,1)S(1)}, bf16[1,4096,448]{1,2,0:T(8,128)(2,1)}, u32[]{:S(2)}) copy-start(bf16[1,4096,448]{1,2,0:T(8,128)(2,1)} %param.27) | copy-start | bytes 11010052
  192.1 27.3 %copy-start.12 = (s32[64]{0:T(128)S(1)}, s32[64]{0:T(128)}, u32[]{:S(2)}) copy-start(s32[64]{0:T(128)} %param.31) | copy-start | bytes 772
  192.1 47.9 %copy-start.5 = (f32[512]{0:T(512)S(1)}, f32[512]{0:T(512)}, u32[]{:S(2)}) copy-start(f32[512]{0:T(512)} %param.29) | copy-start | bytes 6148
  192.1 52.5 %copy-start.13 = (f32[4]{0:T(128)S(1)}, f32[4]{0:T(128)}, u32[]{:S(2)}) copy-start(f32[4]{0:T(128)} %param.30) | copy-start | bytes 52
  212.2 17.7 %all-to-all-start.5 = ((f32[32,2,512]{2,1,0:T(2,128)}), f32[32,2,512]{2,1,0:T(2,128)S(1)}, u32[]{:S(2)}, u32[]{:S(2)}) async-start(f32[32,2,512]{2,1,0:T(2,128)} %reshape.503), calls=%async_computation.5 | async-start | bytes 262144 | tf_op jit(solution)/shard_map/all_to_all | solution.py:59
  230.1 1.2 collective-permute-start
  231.4 3.6 %collective-permute-start.1 = (f32[2]{0:T(128)S(1)}, f32[2]{0:T(128)S(1)}, u32[]{:S(2)}, u32[]{:S(2)}) collective-permute-start(f32[2]{0:T(128)S(1)} %add.117), channel_id=1, source_target_pairs={{0,2},{1,3},{2,0},{3,1},{4,6},{5,7},{6,4},{7,5},{8,10},{9,11},{10,... | collective-permute-start | bytes 32 | tf_op jit(solution)/shard_map/ppermute | solution.py:75
  234.9 5.1 %collective-permute-start.2 = (f32[2]{0:T(128)S(1)}, f32[2]{0:T(128)S(1)}, u32[]{:S(2)}, u32[]{:S(2)}) collective-permute-start(f32[2]{0:T(128)S(1)} %add.118), channel_id=1, source_target_pairs={{0,4},{1,5},{2,6},{3,7},{4,0},{5,1},{6,2},{7,3},{8,12},{9,13},{10,... | collective-permute-start | bytes 32 | tf_op jit(solution)/shard_map/ppermute | solution.py:75
  240.1 15.8 %copy-start.4 = (bf16[2,512]{1,0:T(2,128)(2,1)}, bf16[2,512]{1,0:T(2,128)(2,1)S(1)}, u32[]{:S(2)}) copy-start(bf16[2,512]{1,0:T(2,128)(2,1)S(1)} %multiply_convert_fusion.1) | copy-start | bytes 6148
  240.7 13.9 %all-to-all-start.6 = ((bf16[32,2,512]{2,1,0:T(2,128)(2,1)}), bf16[32,2,512]{2,1,0:T(2,128)(2,1)S(1)}, u32[]{:S(2)}, u32[]{:S(2)}) async-start(bf16[32,2,512]{2,1,0:T(2,128)(2,1)} %broadcast_in_dim.198), calls=%async_computation.6 | async-start | bytes 131072 | tf_op jit(solution)/shard_map/all_to_all | solution.py:65
Sparse Core Ops, SparseCore 0:
  108.5 68.3 all-gather.2

commit v8 on v7

--- a/solution.py
+++ b/solution.py
@@ -102,7 +102,7 @@
     tok_local = residual.shape[0]
     width = residual.shape[1]
     slice_width = width // expert_count
-    highest_precision = lax.Precision.HIGHEST
+    f32_precision = lax.Precision.HIGH
     attended = attend(queries, new_keys, new_values, cache_keys, cache_values)
     y_count = lax.axis_size("y")
     z_count = lax.axis_size("z")
@@ -112,10 +112,13 @@
     head_terms = jnp.einsum(
         "th,zhc->tzc", attended_row, weight_row, preferred_element_type=jnp.float32
     )
-    head_terms = head_terms.reshape(y_count, expert_count, tok_local, z_count * col_block)
-    head_terms = head_terms.transpose(1, 0, 2, 3)
-    token_cols = a2a_sum(head_terms, "expert", 0, expert_count)[0]
-    token_cols = lax.all_to_all(token_cols, "y", split_axis=0, concat_axis=0, tiled=True)
+    head_terms = head_terms.reshape(y_count * expert_count, tok_local, z_count * col_block)
+    token_cols = lax.all_to_all(
+        head_terms, ("y", "expert"), split_axis=0, concat_axis=0, tiled=True
+    )
+    token_cols = jnp.sum(
+        token_cols.reshape(y_count, expert_count, tok_local, z_count * col_block), axis=1
+    )
     token_cols = token_cols.reshape(y_count, tok_local, z_count, col_block).transpose(1, 2, 0, 3)
     mixed = residual.astype(jnp.float32) + token_cols.reshape(tok_local, width)
     normed = (
@@ -170,10 +173,10 @@
         "iks,ikf->isf",
         gathered_weight.reshape(n_dp, GROUP_CAP, span_local),
         hidden.reshape(n_dp, GROUP_CAP, -1).astype(jnp.float32),
-        precision=highest_precision,
+        precision=f32_precision,
     ).reshape(n_dp * span_local, -1)
     pooled_part = jnp.dot(
-        span_hidden, w_down[0].astype(jnp.float32), precision=highest_precision
+        span_hidden, w_down[0].astype(jnp.float32), precision=f32_precision
     )
     own_span = dp_index * span_local + (column * tok_local) // WIN
     span_count = n_dp * span_local

time: 263 us -> 256 us (0.973)
  waiting for transfers between devices: 87 us -> 82.7 us
    all_to_all x2 -> x1, waiting for transfers between devices: 24.8 us -> 10.4 us  [a2a_sum(): lax.all_to_all(x.reshape(split), axis, split_axis=dim, concat_axis=dim, t...]
    all_to_all x1, waiting for transfers between devices: 5.96 us -> 15.9 us  [shards(): lax.all_to_all(head_terms, ('y', 'expert'), split_axis=0, concat_axis=0,...]
    all_to_all x2 -> x1, starting transfers between devices: 12 us -> 7.15 us  [a2a_sum(): lax.all_to_all(x.reshape(split), axis, split_axis=dim, concat_axis=dim, t...]
    all_to_all x1, starting transfers between devices: 4.59 us -> 7.62 us  [shards(): lax.all_to_all(head_terms, ('y', 'expert'), split_axis=0, concat_axis=0,...]
  transfers between devices with their start and end apart: 9 -> 8, of which waited for: 9 -> 8; matrix products, arithmetic and copies ran while one was open for 1% -> 1% of each run, Pallas kernels for 0% -> 0%
where the time goes in v8:
time: 256 us; the launch traced here: 255 us
  blocking collectives  102 us (40%)
  waiting for transfers between devices  82.7 us (32%)
  starting transfers between devices  30 us (12%)
  matrix products  17.2 us (7%)
  between operations  14.5 us (6%)
  local copies, waits for them, and re-layouts  7.05 us (3%)
    all_gather x1, blocking collectives, shards(): gathered_weight = lax.all_gather(pool_weight, DP, axis=0, tiled=True)  42 us
    all_gather x1, waiting for transfers between devices, dp_gather(): lax.all_gather(lax.all_gather(x, 'y', axis=axis, tiled=True), 'z', axis=a...  26 us
    all_to_all x2, waiting for transfers between devices, a2a_gather(): return lax.all_to_all(spread, axis, split_axis=0, concat_axis=0, tiled=True)  23.4 us
    all_to_all x1, blocking collectives, a2a_sum(): lax.all_to_all(x.reshape(split), axis, split_axis=dim, concat_axis=dim, t...  19.4 us
    all_to_all x1, waiting for transfers between devices, shards(): lax.all_to_all(head_terms, ('y', 'expert'), split_axis=0, concat_axis=0,...  15.9 us
    all_gather x1, blocking collectives, dp_gather(): lax.all_gather(x, 'y', axis=axis, tiled=True)  14.7 us
    all_to_all x1, blocking collectives, shards(): lax.all_to_all(outgoing, 'expert', split_axis=0, concat_axis=1, tiled=True)  13 us
    all_gather x1, blocking collectives, shards(): attended_row = lax.all_gather(attended, 'y', axis=0, tiled=True)  12.8 us
  transfers between devices with their start and end apart: 8, of which 8 were waited for; matrix products, arithmetic and copies ran while one was open for 1% of the time, Pallas kernels for 0%

profile of v8, /device:TPU:2, one launch (start us, length us, event | category | flops | bytes accessed | tf_op | source)
XLA Modules:
  0.0 255.2 jit_solution(8812249323611625722)
XLA Ops:
  7.2 2.1 broadcast_in_dim.183
  9.3 8.5 %all-to-all-start = ((bf16[8,512,128]{2,1,0:T(8,128)(2,1)}), bf16[8,512,128]{2,1,0:T(8,128)(2,1)S(1)}, u32[]{:S(2)}, u32[]{:S(2)}) async-start(bf16[8,512,128]{2,1,0:T(8,128)(2,1)} %broadcast_in_dim.183), calls=%async_computation | async-start | bytes 2097152 | tf_op jit(solution)/shard_map/all_to_all | solution.py:65
  17.8 0.9 reshape.483
  19.9 0.4 fusion.22
  20.4 12.8 %all_gather.12 = bf16[256,512]{1,0:T(8,128)(2,1)S(1)} all-gather(bf16[64,512]{1,0:T(8,128)(2,1)S(1)} %bitcast.142), channel_id=1, replica_groups=mesh['z'=8,'y'=4,'expert'=8] {'y'}, dimensions={0}, use_global_device_ids=true | all-gather | bytes 327680 | tf_op jit(solution)/shard_map/all_gather | solution.py:109
  33.2 13.4 %all-to-all-done = bf16[8,512,128]{2,1,0:T(8,128)(2,1)S(1)} async-done(((bf16[8,512,128]{2,1,0:T(8,128)(2,1)}), bf16[8,512,128]{2,1,0:T(8,128)(2,1)S(1)}, u32[]{:S(2)}, u32[]{:S(2)}) %all-to-all-start) | async-done | bytes 1048608 | tf_op jit(solution)/shard_map/all_to_all | solution.py:65
  46.5 0.4 fusion.31
  47.0 0.6 copy.74
  47.6 1.1 reshape.489
  48.8 7.6 %all-to-all-start.1 = ((f32[32,8,1024]{2,1,0:T(8,128)}), f32[32,8,1024]{2,1,0:T(8,128)S(1)}, u32[]{:S(2)}, u32[]{:S(2)}) async-start(f32[32,8,1024]{2,1,0:T(8,128)} %reshape.489), calls=%async_computation.1 | async-start | bytes 2097152 | tf_op jit(solution)/shard_map/all_to_all | solution.py:116
  56.5 15.9 %all-to-all-done.1 = f32[32,8,1024]{2,1,0:T(8,128)S(1)} async-done(((f32[32,8,1024]{2,1,0:T(8,128)}), f32[32,8,1024]{2,1,0:T(8,128)S(1)}, u32[]{:S(2)}, u32[]{:S(2)}) %all-to-all-start.1) | async-done | bytes 1048608 | tf_op jit(solution)/shard_map/all_to_all | solution.py:116
  73.2 13.0 %all_to_all.37 = bf16[8,8,4224]{2,1,0:T(8,128)(2,1)S(1)} all-to-all(bf16[8,8,4224]{2,1,0:T(8,128)(2,1)S(1)} %pad_maximum_fusion), channel_id=1, replica_groups=mesh['z'=8,'y'=4,'expert'=8] {'expert'}, dimensions={0} | all-to-all | bytes 1081344 | tf_op jit(solution)/shard_map/all_to_all | solution.py:137
  86.7 14.7 %all_gather.14 = bf16[96,1,4096]{2,0,1:T(8,128)(2,1)} all-gather(bf16[24,1,4096]{2,0,1:T(8,128)(2,1)S(1)} %bitcast.139), channel_id=1, replica_groups=mesh['z'=8,'y'=4,'expert'=8] {'y'}, dimensions={0}, use_global_device_ids=true | all-gather | bytes 983040 | tf_op jit(solution)/shard_map/all_gather | solution.py:69
  102.0 42.0 %all-gather = f32[32,24,2]{1,2,0:T(2,128)S(1)} all-gather(f32[1,24,2]{1,2,0:T(2,128)S(1)} %fusion.57), channel_id=1, replica_groups=mesh['z'=8,'y'=4,'expert'=8] {'z','y'}, dimensions={0}, use_global_device_ids=true | all-gather | bytes 6336 | tf_op jit(solution)/shard_map/all_gather | solution.py:167
  144.0 26.0 %all-gather.3.cloned.1.call-done = bf16[768,1,4096]{2,0,1:T(8,128)(2,1)} async-done(((bf16[96,1,4096]{2,0,1:T(8,128)(2,1)}), bf16[768,1,4096]{2,0,1:T(8,128)(2,1)}) %all-gather.3.cloned.1.call-update) | async-done | bytes 6291472 | tf_op jit(solution)/shard_map/all_gather | solution.py:69
  170.0 7.0 %fusion.3 = f32[768,448]{0,1:T(8,128)S(1)} fusion(bf16[768,1,4096]{2,0,1:T(8,128)(2,1)} %all-gather.3.cloned.1.call-done, bf16[1,4096,448]{1,2,0:T(8,128)(2,1)} %param.26), kind=kOutput, calls=%fused_computation.3 | convolution fusion | flops 2818572288 | bytes 11337728 | tf_op jit(solution)/shard_map/ned,edf->nf/dot_general | solution.py:169
  177.1 3.1 %fusion.14 = bf16[768,448]{0,1:T(8,128)(2,1)S(1)} fusion(bf16[1,4096,448]{1,2,0:T(8,128)(2,1)S(1)} %copy-done.8, bf16[768,1,4096]{2,0,1:T(8,128)(2,1)S(1)} %copy-done.7, f32[768,448]{0,1:T(8,128)S(1)} %fusion.3), kind=kOutput, calls=%fused_computation.13 | convolution fusion | flops 2820636672 | bytes 12025856 | tf_op jit(solution)/shard_map/ned,edf->nf/dot_general | solution.py:170
  180.4 0.4 fusion.66
  181.0 3.4 %convolution_add_fusion = f32[64,4096]{1,0:T(8,128)S(1)} fusion(f32[64,448]{1,0:T(8,128)S(1)} %reshape.499, bf16[1,448,4096]{2,1,0:T(8,128)(2,1)} %param.28, f32[4096]{0:T(1024)S(1)} %get-tuple-element.2, pred[64]{0:T(512)(128)(4,1)S(1)} %iota_compare_fusion.5), kind=kOutput, calls=%fused_computation.5 | convolution fusion | flops 705167360 | bytes 4849728 | tf_op jit(solution)/shard_map/dot_general | solution.py:178
  184.5 19.4 %all_to_all.38 = f32[64,8,512]{2,0,1:T(8,128)S(1)} all-to-all(f32[64,8,512]{2,0,1:T(8,128)S(1)} %bitcast.134), channel_id=1, replica_groups=mesh['z'=8,'y'=4,'expert'=8] {'expert'}, dimensions={1} | all-to-all | bytes 2097152 | tf_op jit(solution)/shard_map/all_to_all | solution.py:59
  204.0 0.7 reshape.501
  204.7 7.2 %all-to-all-start.4 = ((f32[32,2,512]{2,1,0:T(2,128)}), f32[32,2,512]{2,1,0:T(2,128)S(1)}, u32[]{:S(2)}, u32[]{:S(2)}) async-start(f32[32,2,512]{2,1,0:T(2,128)} %reshape.501), calls=%async_computation.4 | async-start | bytes 262144 | tf_op jit(solution)/shard_map/all_to_all | solution.py:59
  212.0 10.4 %all-to-all-done.4 = f32[32,2,512]{2,1,0:T(2,128)S(1)} async-done(((f32[32,2,512]{2,1,0:T(2,128)}), f32[32,2,512]{2,1,0:T(2,128)S(1)}, u32[]{:S(2)}, u32[]{:S(2)}) %all-to-all-start.4) | async-done | bytes 131104 | tf_op jit(solution)/shard_map/all_to_all | solution.py:59
  222.7 1.1 collective-permute-done
  223.8 1.4 collective-permute-start.1
  225.2 2.2 collective-permute-done.1
  227.4 1.4 collective-permute-start.2
  228.8 3.7 %collective-permute-done.2 = f32[2]{0:T(128)S(1)} collective-permute-done((f32[2]{0:T(128)S(1)}, f32[2]{0:T(128)S(1)}, u32[]{:S(2)}, u32[]{:S(2)}) %collective-permute-start.2) | collective-permute-done | bytes 40 | tf_op jit(solution)/shard_map/ppermute | solution.py:75
  232.6 0.7 broadcast_in_dim.198
  233.2 3.9 %all-to-all-start.5 = ((bf16[32,2,512]{2,1,0:T(2,128)(2,1)}), bf16[32,2,512]{2,1,0:T(2,128)(2,1)S(1)}, u32[]{:S(2)}, u32[]{:S(2)}) async-start(bf16[32,2,512]{2,1,0:T(2,128)(2,1)} %broadcast_in_dim.198), calls=%async_computation.5 | async-start | bytes 131072 | tf_op jit(solution)/shard_map/all_to_all | solution.py:65
  237.1 10.0 %all-to-all-done.5 = bf16[32,2,512]{2,1,0:T(2,128)(2,1)S(1)} async-done(((bf16[32,2,512]{2,1,0:T(2,128)(2,1)}), bf16[32,2,512]{2,1,0:T(2,128)(2,1)S(1)}, u32[]{:S(2)}, u32[]{:S(2)}) %all-to-all-start.5) | async-done | bytes 65568 | tf_op jit(solution)/shard_map/all_to_all | solution.py:65
  247.5 0.8 fusion.26
  (83 shorter events, 4.5 us)
Async XLA Ops:
  7.2 11.5 %copy-start = (bf16[2,1024,128]{2,1,0:T(8,128)(2,1)S(1)}, bf16[2,1024,128]{2,1,0:T(8,128)(2,1)}, u32[]{:S(2)}) copy-start(bf16[2,1024,128]{2,1,0:T(8,128)(2,1)} %param.20) | copy-start | bytes 1572868
  7.2 11.9 %copy-start.2 = (bf16[64,128]{1,0:T(8,128)(2,1)S(1)}, bf16[64,128]{1,0:T(8,128)(2,1)}, u32[]{:S(2)}) copy-start(bf16[64,128]{1,0:T(8,128)(2,1)} %param.18) | copy-start | bytes 49156
  7.2 12.5 %copy-start.11 = (bf16[64,128]{1,0:T(8,128)(2,1)S(1)}, bf16[64,128]{1,0:T(8,128)(2,1)}, u32[]{:S(2)}) copy-start(bf16[64,128]{1,0:T(8,128)(2,1)} %param.19) | copy-start | bytes 49156
  7.2 12.7 %copy-start.9 = (bf16[2,1024,128]{2,1,0:T(8,128)(2,1)S(1)}, bf16[2,1024,128]{2,1,0:T(8,128)(2,1)}, u32[]{:S(2)}) copy-start(bf16[2,1024,128]{2,1,0:T(8,128)(2,1)} %param.21) | copy-start | bytes 1572868
  9.3 37.2 %all-to-all-start = ((bf16[8,512,128]{2,1,0:T(8,128)(2,1)}), bf16[8,512,128]{2,1,0:T(8,128)(2,1)S(1)}, u32[]{:S(2)}, u32[]{:S(2)}) async-start(bf16[8,512,128]{2,1,0:T(8,128)(2,1)} %broadcast_in_dim.183), calls=%async_computation | async-start | bytes 2097152 | tf_op jit(solution)/shard_map/all_to_all | solution.py:65
  47.0 9.5 %copy-start.6 = (s32[8,2]{0,1:T(2,128)S(1)}, s32[8,2]{0,1:T(2,128)}, u32[]{:S(2)}) copy-start(s32[8,2]{0,1:T(2,128)} %param.25) | copy-start | bytes 196
  47.0 25.7 %copy-start.1 = (bf16[8,4096]{1,0:T(8,128)(2,1)S(1)}, bf16[8,4096]{1,0:T(8,128)(2,1)}, u32[]{:S(2)}) copy-start(bf16[8,4096]{1,0:T(8,128)(2,1)} %param.16) | copy-start | bytes 196612
  47.6 25.2 %copy-start.3 = (f32[4096]{0:T(1024)S(1)}, f32[4096]{0:T(1024)}, u32[]{:S(2)}) copy-start(f32[4096]{0:T(1024)} %param.23) | copy-start | bytes 49156
  48.8 23.6 %all-to-all-start.1 = ((f32[32,8,1024]{2,1,0:T(8,128)}), f32[32,8,1024]{2,1,0:T(8,128)S(1)}, u32[]{:S(2)}, u32[]{:S(2)}) async-start(f32[32,8,1024]{2,1,0:T(8,128)} %reshape.489), calls=%async_computation.1 | async-start | bytes 2097152 | tf_op jit(solution)/shard_map/all_to_all | solution.py:116
  56.4 113.6 %all-gather.3.cloned.1.call-start = ((), (), s32[]{:S(2)}) async-start(), calls=%async_computation.6 | async-start | bytes 7077888 | tf_op jit(solution)/shard_map/all_gather | solution.py:69
  72.4 29.3 %copy-start.10 = (bf16[4096,8]{0,1:T(8,128)(2,1)S(1)}, bf16[4096,8]{0,1:T(8,128)(2,1)}, u32[]{:S(2)}) copy-start(bf16[4096,8]{0,1:T(8,128)(2,1)} %param.24) | copy-start | bytes 196612
  170.0 7.1 %copy-start.7 = (bf16[768,1,4096]{2,0,1:T(8,128)(2,1)S(1)}, bf16[768,1,4096]{2,0,1:T(8,128)(2,1)}, u32[]{:S(2)}) copy-start(bf16[768,1,4096]{2,0,1:T(8,128)(2,1)} %all-gather.3.cloned.1.call-done) | copy-start | bytes 18874372
  170.0 7.1 %copy-start.8 = (bf16[1,4096,448]{1,2,0:T(8,128)(2,1)S(1)}, bf16[1,4096,448]{1,2,0:T(8,128)(2,1)}, u32[]{:S(2)}) copy-start(bf16[1,4096,448]{1,2,0:T(8,128)(2,1)} %param.27) | copy-start | bytes 11010052
  184.4 27.5 %copy-start.12 = (s32[64]{0:T(128)S(1)}, s32[64]{0:T(128)}, u32[]{:S(2)}) copy-start(s32[64]{0:T(128)} %param.31) | copy-start | bytes 772
  184.4 48.1 %copy-start.5 = (f32[512]{0:T(512)S(1)}, f32[512]{0:T(512)}, u32[]{:S(2)}) copy-start(f32[512]{0:T(512)} %param.29) | copy-start | bytes 6148
  184.4 52.7 %copy-start.13 = (f32[4]{0:T(128)S(1)}, f32[4]{0:T(128)}, u32[]{:S(2)}) copy-start(f32[4]{0:T(128)} %param.30) | copy-start | bytes 52
  204.7 17.7 %all-to-all-start.4 = ((f32[32,2,512]{2,1,0:T(2,128)}), f32[32,2,512]{2,1,0:T(2,128)S(1)}, u32[]{:S(2)}, u32[]{:S(2)}) async-start(f32[32,2,512]{2,1,0:T(2,128)} %reshape.501), calls=%async_computation.4 | async-start | bytes 262144 | tf_op jit(solution)/shard_map/all_to_all | solution.py:59
  222.6 1.2 collective-permute-start
  223.8 3.6 %collective-permute-start.1 = (f32[2]{0:T(128)S(1)}, f32[2]{0:T(128)S(1)}, u32[]{:S(2)}, u32[]{:S(2)}) collective-permute-start(f32[2]{0:T(128)S(1)} %add.117), channel_id=1, source_target_pairs={{0,2},{1,3},{2,0},{3,1},{4,6},{5,7},{6,4},{7,5},{8,10},{9,11},{10,... | collective-permute-start | bytes 32 | tf_op jit(solution)/shard_map/ppermute | solution.py:75
  227.4 5.1 %collective-permute-start.2 = (f32[2]{0:T(128)S(1)}, f32[2]{0:T(128)S(1)}, u32[]{:S(2)}, u32[]{:S(2)}) collective-permute-start(f32[2]{0:T(128)S(1)} %add.118), channel_id=1, source_target_pairs={{0,4},{1,5},{2,6},{3,7},{4,0},{5,1},{6,2},{7,3},{8,12},{9,13},{10,... | collective-permute-start | bytes 32 | tf_op jit(solution)/shard_map/ppermute | solution.py:75
  232.6 15.8 %copy-start.4 = (bf16[2,512]{1,0:T(2,128)(2,1)}, bf16[2,512]{1,0:T(2,128)(2,1)S(1)}, u32[]{:S(2)}) copy-start(bf16[2,512]{1,0:T(2,128)(2,1)S(1)} %multiply_convert_fusion.1) | copy-start | bytes 6148
  233.2 13.9 %all-to-all-start.5 = ((bf16[32,2,512]{2,1,0:T(2,128)(2,1)}), bf16[32,2,512]{2,1,0:T(2,128)(2,1)S(1)}, u32[]{:S(2)}, u32[]{:S(2)}) async-start(bf16[32,2,512]{2,1,0:T(2,128)(2,1)} %broadcast_in_dim.198), calls=%async_computation.5 | async-start | bytes 131072 | tf_op jit(solution)/shard_map/all_to_all | solution.py:65
Sparse Core Ops, SparseCore 0:
  101.6 68.3 all-gather.2

commit v9 on v8

--- a/solution.py
+++ b/solution.py
@@ -66,7 +66,10 @@
 
 
 def dp_gather(x, axis):
-    return lax.all_gather(lax.all_gather(x, "y", axis=axis, tiled=True), "z", axis=axis, tiled=True)
+    assert axis == 0
+    row = a2a_gather(x, "y", lax.axis_size("y"))
+    row = row.reshape((row.shape[0] * row.shape[1],) + row.shape[2:])
+    return lax.all_gather(row, "z", axis=0, tiled=True)
 
 
 def doubling_sum(x, axis, count):
@@ -184,8 +187,14 @@
     pooled_part = pooled_part + jnp.where(
         (jnp.arange(span_count) == own_span)[:, None], mixed_sum[None, :], 0.0
     )
-    pooled_cols = a2a_sum(pooled_part, "expert", 1, expert_count)
-    own_cols = a2a_sum(pooled_cols, DP, 0, n_dp)
+    pooled_part = pooled_part.reshape(n_dp, span_local, expert_count, slice_width)
+    pooled_part = pooled_part.transpose(0, 2, 1, 3).reshape(
+        n_dp * expert_count, span_local, slice_width
+    )
+    own_cols = jnp.sum(
+        lax.all_to_all(pooled_part, (*DP, "expert"), split_axis=0, concat_axis=0, tiled=True),
+        axis=0,
+    )
     squares = doubling_sum(jnp.sum(own_cols * own_cols, axis=-1), "expert", expert_count)
     summary = (
         own_cols * lax.rsqrt(squares / width + EPSILON)[:, None] * summary_gain

time: 256 us -> 263 us (1.027)
  blocking collectives: 102 us -> 84.4 us
  waiting for transfers between devices: 82.7 us -> 100 us
  starting transfers between devices: 30 us -> 35.7 us
    all_to_all x1, waiting for transfers between devices: 10.4 us -> 30.3 us  [shards(): lax.all_to_all(pooled_part, (*DP, 'expert'), split_axis=0, concat_axis=0,...]
    all_gather x1 -> x0, blocking collectives: 14.7 us -> none  [dp_gather(): lax.all_gather(x, 'y', axis=axis, tiled=True)]
    all_to_all x1, blocking collectives: 19.4 us -> 15.9 us  [a2a_gather(): return lax.all_to_all(spread, axis, split_axis=0, concat_axis=0, tiled=True)]
    all_to_all x1, starting transfers between devices: 7.15 us -> 10.3 us  [shards(): lax.all_to_all(pooled_part, (*DP, 'expert'), split_axis=0, concat_axis=0,...]
where the time goes in v9:
time: 263 us
  waiting for transfers between devices  100 us (38%)
  blocking collectives  84.4 us (32%)
  starting transfers between devices  35.7 us (14%)
  matrix products  17.2 us (7%)
  between operations  14.5 us (6%)
  local copies, waits for them, and re-layouts  8.8 us (3%)
    all_gather x1, blocking collectives, shards(): gathered_weight = lax.all_gather(pool_weight, DP, axis=0, tiled=True)  42.7 us
    all_to_all x1, waiting for transfers between devices, shards(): lax.all_to_all(pooled_part, (*DP, 'expert'), split_axis=0, concat_axis=0,...  30.3 us
    all_gather x1, waiting for transfers between devices, dp_gather(): return lax.all_gather(row, 'z', axis=0, tiled=True)  25 us
    all_to_all x2, waiting for transfers between devices, a2a_gather(): return lax.all_to_all(spread, axis, split_axis=0, concat_axis=0, tiled=True)  23.3 us
    all_to_all x1, waiting for transfers between devices, shards(): lax.all_to_all(head_terms, ('y', 'expert'), split_axis=0, concat_axis=0,...  15.9 us
    all_to_all x1, blocking collectives, a2a_gather(): return lax.all_to_all(spread, axis, split_axis=0, concat_axis=0, tiled=True)  15.9 us
    all_to_all x2, starting transfers between devices, a2a_gather(): return lax.all_to_all(spread, axis, split_axis=0, concat_axis=0, tiled=True)  13.3 us
    all_to_all x1, blocking collectives, shards(): lax.all_to_all(outgoing, 'expert', split_axis=0, concat_axis=1, tiled=True)  13 us
  transfers between devices with their start and end apart: 8, of which 8 were waited for; matrix products, arithmetic and copies ran while one was open for 1% of the time, Pallas kernels for 0%

profile of v9, /device:TPU:2, one launch (start us, length us, event | category | flops | bytes accessed | tf_op | source)
XLA Modules:
  0.0 262.7 jit_solution(2250280884062045787)
XLA Ops:
  7.2 2.1 broadcast_in_dim.189
  9.3 8.5 %all-to-all-start = ((bf16[8,512,128]{2,1,0:T(8,128)(2,1)}), bf16[8,512,128]{2,1,0:T(8,128)(2,1)S(1)}, u32[]{:S(2)}, u32[]{:S(2)}) async-start(bf16[8,512,128]{2,1,0:T(8,128)(2,1)} %broadcast_in_dim.189), calls=%async_computation | async-start | bytes 2097152 | tf_op jit(solution)/shard_map/all_to_all | solution.py:65
  17.8 0.9 reshape.489
  19.9 0.4 fusion.23
  20.4 12.8 %all_gather.9 = bf16[256,512]{1,0:T(8,128)(2,1)S(1)} all-gather(bf16[64,512]{1,0:T(8,128)(2,1)S(1)} %bitcast.146), channel_id=1, replica_groups=mesh['z'=8,'y'=4,'expert'=8] {'y'}, dimensions={0}, use_global_device_ids=true | all-gather | bytes 327680 | tf_op jit(solution)/shard_map/all_gather | solution.py:112
  33.2 13.4 %all-to-all-done = bf16[8,512,128]{2,1,0:T(8,128)(2,1)S(1)} async-done(((bf16[8,512,128]{2,1,0:T(8,128)(2,1)}), bf16[8,512,128]{2,1,0:T(8,128)(2,1)S(1)}, u32[]{:S(2)}, u32[]{:S(2)}) %all-to-all-start) | async-done | bytes 1048608 | tf_op jit(solution)/shard_map/all_to_all | solution.py:65
  46.5 0.4 fusion.32
  47.0 0.6 copy.65
  47.6 1.1 reshape.495
  48.8 7.6 %all-to-all-start.1 = ((f32[32,8,1024]{2,1,0:T(8,128)}), f32[32,8,1024]{2,1,0:T(8,128)S(1)}, u32[]{:S(2)}, u32[]{:S(2)}) async-start(f32[32,8,1024]{2,1,0:T(8,128)} %reshape.495), calls=%async_computation.1 | async-start | bytes 2097152 | tf_op jit(solution)/shard_map/all_to_all | solution.py:119
  56.5 15.9 %all-to-all-done.1 = f32[32,8,1024]{2,1,0:T(8,128)S(1)} async-done(((f32[32,8,1024]{2,1,0:T(8,128)}), f32[32,8,1024]{2,1,0:T(8,128)S(1)}, u32[]{:S(2)}, u32[]{:S(2)}) %all-to-all-start.1) | async-done | bytes 1048608 | tf_op jit(solution)/shard_map/all_to_all | solution.py:119
  73.2 13.0 %all_to_all.37 = bf16[8,8,4224]{2,1,0:T(8,128)(2,1)S(1)} all-to-all(bf16[8,8,4224]{2,1,0:T(8,128)(2,1)S(1)} %pad_maximum_fusion), channel_id=1, replica_groups=mesh['z'=8,'y'=4,'expert'=8] {'expert'}, dimensions={0} | all-to-all | bytes 1081344 | tf_op jit(solution)/shard_map/all_to_all | solution.py:140
  86.8 15.9 %all_to_all.38 = bf16[4,24,1,4096]{3,1,2,0:T(8,128)(2,1)} all-to-all(bf16[4,24,1,4096]{3,1,2,0:T(8,128)(2,1)S(1)} %broadcast_in_dim.201), channel_id=1, replica_groups=mesh['z'=8,'y'=4,'expert'=8] {'y'}, dimensions={0} | all-to-all | bytes 1572864 | tf_op jit(solution)/shard_map/all_to_all | solution.py:65
  103.2 42.7 %all-gather = f32[32,24,2]{1,2,0:T(2,128)S(1)} all-gather(f32[1,24,2]{1,2,0:T(2,128)S(1)} %fusion.56), channel_id=1, replica_groups=mesh['z'=8,'y'=4,'expert'=8] {'z','y'}, dimensions={0}, use_global_device_ids=true | all-gather | bytes 6336 | tf_op jit(solution)/shard_map/all_gather | solution.py:170
  145.9 25.0 %all-gather.3.cloned.1.call-done = bf16[768,1,4096]{2,0,1:T(8,128)(2,1)} async-done(((bf16[96,1,4096]{2,0,1:T(8,128)(2,1)}), bf16[768,1,4096]{2,0,1:T(8,128)(2,1)}) %all-gather.3.cloned.1.call-update) | async-done | bytes 6291472 | tf_op jit(solution)/shard_map/all_gather | solution.py:72
  170.9 7.0 %fusion.3 = f32[768,448]{0,1:T(8,128)S(1)} fusion(bf16[768,1,4096]{2,0,1:T(8,128)(2,1)} %all-gather.3.cloned.1.call-done, bf16[1,4096,448]{1,2,0:T(8,128)(2,1)} %param.26), kind=kOutput, calls=%fused_computation.3 | convolution fusion | flops 2818572288 | bytes 11337728 | tf_op jit(solution)/shard_map/ned,edf->nf/dot_general | solution.py:172
  178.0 3.1 %fusion.15 = bf16[768,448]{0,1:T(8,128)(2,1)S(1)} fusion(bf16[1,4096,448]{1,2,0:T(8,128)(2,1)S(1)} %copy-done.8, bf16[768,1,4096]{2,0,1:T(8,128)(2,1)S(1)} %copy-done.7, f32[768,448]{0,1:T(8,128)S(1)} %fusion.3), kind=kOutput, calls=%fused_computation.14 | convolution fusion | flops 2820636672 | bytes 12025856 | tf_op jit(solution)/shard_map/ned,edf->nf/dot_general | solution.py:173
  181.4 0.4 fusion.65
  181.9 3.4 %convolution_add_fusion = f32[64,4096]{1,0:T(8,128)S(1)} fusion(f32[64,448]{1,0:T(8,128)S(1)} %reshape.506, bf16[1,448,4096]{2,1,0:T(8,128)(2,1)} %param.28, f32[4096]{0:T(1024)S(1)} %get-tuple-element.2, pred[64]{0:T(512)(128)(4,1)S(1)} %iota_compare_fusion.5), kind=kOutput, calls=%fused_computation.5 | convolution fusion | flops 705167360 | bytes 4849728 | tf_op jit(solution)/shard_map/dot_general | solution.py:181
  185.3 0.6 copy.81
  186.1 1.8 copy.70
  187.9 10.3 %all-to-all-start.4 = ((f32[256,2,512]{2,1,0:T(2,128)}), f32[256,2,512]{2,1,0:T(2,128)S(1)}, u32[]{:S(2)}, u32[]{:S(2)}) async-start(f32[256,2,512]{2,1,0:T(2,128)} %copy.70), calls=%async_computation.4 | async-start | bytes 2097152 | tf_op jit(solution)/shard_map/all_to_all | solution.py:195
  198.4 30.3 %all-to-all-done.4 = f32[256,2,512]{2,1,0:T(2,128)S(1)} async-done(((f32[256,2,512]{2,1,0:T(2,128)}), f32[256,2,512]{2,1,0:T(2,128)S(1)}, u32[]{:S(2)}, u32[]{:S(2)}) %all-to-all-start.4) | async-done | bytes 1048608 | tf_op jit(solution)/shard_map/all_to_all | solution.py:195
  229.3 1.1 collective-permute-done
  230.4 1.4 collective-permute-start.1
  231.8 2.2 collective-permute-done.1
  234.0 2.8 %collective-permute-start.2 = (f32[2]{0:T(128)S(1)}, f32[2]{0:T(128)S(1)}, u32[]{:S(2)}, u32[]{:S(2)}) collective-permute-start(f32[2]{0:T(128)S(1)} %add.118), channel_id=1, source_target_pairs={{0,4},{1,5},{2,6},{3,7},{4,0},{5,1},{6,2},{7,3},{8,12},{9,13},{10,... | collective-permute-start | bytes 32 | tf_op jit(solution)/shard_map/ppermute | solution.py:78
  236.8 2.2 collective-permute-done.2
  239.2 0.7 broadcast_in_dim.205
  239.8 4.8 %all-to-all-start.5 = ((bf16[32,2,512]{2,1,0:T(2,128)(2,1)}), bf16[32,2,512]{2,1,0:T(2,128)(2,1)S(1)}, u32[]{:S(2)}, u32[]{:S(2)}) async-start(bf16[32,2,512]{2,1,0:T(2,128)(2,1)} %broadcast_in_dim.205), calls=%async_computation.5 | async-start | bytes 131072 | tf_op jit(solution)/shard_map/all_to_all | solution.py:65
  244.7 9.9 %all-to-all-done.5 = bf16[32,2,512]{2,1,0:T(2,128)(2,1)S(1)} async-done(((bf16[32,2,512]{2,1,0:T(2,128)(2,1)}), bf16[32,2,512]{2,1,0:T(2,128)(2,1)S(1)}, u32[]{:S(2)}, u32[]{:S(2)}) %all-to-all-start.5) | async-done | bytes 65568 | tf_op jit(solution)/shard_map/all_to_all | solution.py:65
  255.0 0.8 fusion.27
  (83 shorter events, 4.8 us)
Async XLA Ops:
  7.2 11.5 %copy-start = (bf16[2,1024,128]{2,1,0:T(8,128)(2,1)S(1)}, bf16[2,1024,128]{2,1,0:T(8,128)(2,1)}, u32[]{:S(2)}) copy-start(bf16[2,1024,128]{2,1,0:T(8,128)(2,1)} %param.20) | copy-start | bytes 1572868
  7.2 11.9 %copy-start.2 = (bf16[64,128]{1,0:T(8,128)(2,1)S(1)}, bf16[64,128]{1,0:T(8,128)(2,1)}, u32[]{:S(2)}) copy-start(bf16[64,128]{1,0:T(8,128)(2,1)} %param.18) | copy-start | bytes 49156
  7.2 12.5 %copy-start.11 = (bf16[64,128]{1,0:T(8,128)(2,1)S(1)}, bf16[64,128]{1,0:T(8,128)(2,1)}, u32[]{:S(2)}) copy-start(bf16[64,128]{1,0:T(8,128)(2,1)} %param.19) | copy-start | bytes 49156
  7.2 12.7 %copy-start.9 = (bf16[2,1024,128]{2,1,0:T(8,128)(2,1)S(1)}, bf16[2,1024,128]{2,1,0:T(8,128)(2,1)}, u32[]{:S(2)}) copy-start(bf16[2,1024,128]{2,1,0:T(8,128)(2,1)} %param.21) | copy-start | bytes 1572868
  9.3 37.2 %all-to-all-start = ((bf16[8,512,128]{2,1,0:T(8,128)(2,1)}), bf16[8,512,128]{2,1,0:T(8,128)(2,1)S(1)}, u32[]{:S(2)}, u32[]{:S(2)}) async-start(bf16[8,512,128]{2,1,0:T(8,128)(2,1)} %broadcast_in_dim.189), calls=%async_computation | async-start | bytes 2097152 | tf_op jit(solution)/shard_map/all_to_all | solution.py:65
  47.0 9.5 %copy-start.6 = (s32[8,2]{0,1:T(2,128)S(1)}, s32[8,2]{0,1:T(2,128)}, u32[]{:S(2)}) copy-start(s32[8,2]{0,1:T(2,128)} %param.25) | copy-start | bytes 196
  47.0 25.7 %copy-start.1 = (bf16[8,4096]{1,0:T(8,128)(2,1)S(1)}, bf16[8,4096]{1,0:T(8,128)(2,1)}, u32[]{:S(2)}) copy-start(bf16[8,4096]{1,0:T(8,128)(2,1)} %param.16) | copy-start | bytes 196612
  47.6 25.2 %copy-start.3 = (f32[4096]{0:T(1024)S(1)}, f32[4096]{0:T(1024)}, u32[]{:S(2)}) copy-start(f32[4096]{0:T(1024)} %param.23) | copy-start | bytes 49156
  48.8 23.6 %all-to-all-start.1 = ((f32[32,8,1024]{2,1,0:T(8,128)}), f32[32,8,1024]{2,1,0:T(8,128)S(1)}, u32[]{:S(2)}, u32[]{:S(2)}) async-start(f32[32,8,1024]{2,1,0:T(8,128)} %reshape.495), calls=%async_computation.1 | async-start | bytes 2097152 | tf_op jit(solution)/shard_map/all_to_all | solution.py:119
  56.4 114.5 %all-gather.3.cloned.1.call-start = ((), (), s32[]{:S(2)}) async-start(), calls=%async_computation.6 | async-start | bytes 7077888 | tf_op jit(solution)/shard_map/all_gather | solution.py:72
  72.8 30.1 %copy-start.10 = (bf16[4096,8]{0,1:T(8,128)(2,1)S(1)}, bf16[4096,8]{0,1:T(8,128)(2,1)}, u32[]{:S(2)}) copy-start(bf16[4096,8]{0,1:T(8,128)(2,1)} %param.24) | copy-start | bytes 196612
  170.9 7.1 %copy-start.7 = (bf16[768,1,4096]{2,0,1:T(8,128)(2,1)S(1)}, bf16[768,1,4096]{2,0,1:T(8,128)(2,1)}, u32[]{:S(2)}) copy-start(bf16[768,1,4096]{2,0,1:T(8,128)(2,1)} %all-gather.3.cloned.1.call-done) | copy-start | bytes 18874372
  170.9 7.1 %copy-start.8 = (bf16[1,4096,448]{1,2,0:T(8,128)(2,1)S(1)}, bf16[1,4096,448]{1,2,0:T(8,128)(2,1)}, u32[]{:S(2)}) copy-start(bf16[1,4096,448]{1,2,0:T(8,128)(2,1)} %param.27) | copy-start | bytes 11010052
  186.0 12.3 %copy-start.12 = (s32[64]{0:T(128)S(1)}, s32[64]{0:T(128)}, u32[]{:S(2)}) copy-start(s32[64]{0:T(128)} %param.31) | copy-start | bytes 772
  186.0 53.1 %copy-start.5 = (f32[512]{0:T(512)S(1)}, f32[512]{0:T(512)}, u32[]{:S(2)}) copy-start(f32[512]{0:T(512)} %param.29) | copy-start | bytes 6148
  186.0 58.7 %copy-start.13 = (f32[4]{0:T(128)S(1)}, f32[4]{0:T(128)}, u32[]{:S(2)}) copy-start(f32[4]{0:T(128)} %param.30) | copy-start | bytes 52
  187.9 40.8 %all-to-all-start.4 = ((f32[256,2,512]{2,1,0:T(2,128)}), f32[256,2,512]{2,1,0:T(2,128)S(1)}, u32[]{:S(2)}, u32[]{:S(2)}) async-start(f32[256,2,512]{2,1,0:T(2,128)} %copy.70), calls=%async_computation.4 | async-start | bytes 2097152 | tf_op jit(solution)/shard_map/all_to_all | solution.py:195
  229.2 1.2 collective-permute-start
  230.4 3.6 %collective-permute-start.1 = (f32[2]{0:T(128)S(1)}, f32[2]{0:T(128)S(1)}, u32[]{:S(2)}, u32[]{:S(2)}) collective-permute-start(f32[2]{0:T(128)S(1)} %add.117), channel_id=1, source_target_pairs={{0,2},{1,3},{2,0},{3,1},{4,6},{5,7},{6,4},{7,5},{8,10},{9,11},{10,... | collective-permute-start | bytes 32 | tf_op jit(solution)/shard_map/ppermute | solution.py:78
  234.0 5.1 %collective-permute-start.2 = (f32[2]{0:T(128)S(1)}, f32[2]{0:T(128)S(1)}, u32[]{:S(2)}, u32[]{:S(2)}) collective-permute-start(f32[2]{0:T(128)S(1)} %add.118), channel_id=1, source_target_pairs={{0,4},{1,5},{2,6},{3,7},{4,0},{5,1},{6,2},{7,3},{8,12},{9,13},{10,... | collective-permute-start | bytes 32 | tf_op jit(solution)/shard_map/ppermute | solution.py:78
  239.2 16.7 %copy-start.4 = (bf16[2,512]{1,0:T(2,128)(2,1)}, bf16[2,512]{1,0:T(2,128)(2,1)S(1)}, u32[]{:S(2)}) copy-start(bf16[2,512]{1,0:T(2,128)(2,1)S(1)} %multiply_convert_fusion.1) | copy-start | bytes 6148
  239.8 14.8 %all-to-all-start.5 = ((bf16[32,2,512]{2,1,0:T(2,128)(2,1)}), bf16[32,2,512]{2,1,0:T(2,128)(2,1)S(1)}, u32[]{:S(2)}, u32[]{:S(2)}) async-start(bf16[32,2,512]{2,1,0:T(2,128)(2,1)} %broadcast_in_dim.205), calls=%async_computation.5 | async-start | bytes 131072 | tf_op jit(solution)/shard_map/all_to_all | solution.py:65
Sparse Core Ops, SparseCore 0:
  102.8 68.0 all-gather.2

commit v10 on v8

--- a/solution.py
+++ b/solution.py
@@ -184,8 +184,24 @@
     pooled_part = pooled_part + jnp.where(
         (jnp.arange(span_count) == own_span)[:, None], mixed_sum[None, :], 0.0
     )
-    pooled_cols = a2a_sum(pooled_part, "expert", 1, expert_count)
-    own_cols = a2a_sum(pooled_cols, DP, 0, n_dp)
+    pooled_part = pooled_part.reshape(z_count, y_count, span_local, expert_count, slice_width)
+    pooled_part = pooled_part.transpose(1, 3, 0, 2, 4).reshape(
+        y_count * expert_count, z_count * span_local, slice_width
+    )
+    plane_cols = jnp.sum(
+        lax.all_to_all(pooled_part, ("y", "expert"), split_axis=0, concat_axis=0, tiled=True),
+        axis=0,
+    )
+    own_cols = jnp.sum(
+        lax.all_to_all(
+            plane_cols.reshape(z_count, span_local, slice_width),
+            "z",
+            split_axis=0,
+            concat_axis=0,
+            tiled=True,
+        ),
+        axis=0,
+    )
     squares = doubling_sum(jnp.sum(own_cols * own_cols, axis=-1), "expert", expert_count)
     summary = (
         own_cols * lax.rsqrt(squares / width + EPSILON)[:, None] * summary_gain

time: 256 us -> 257 us (level)
  blocking collectives: 102 us -> 82.7 us
  waiting for transfers between devices: 82.7 us -> 96.5 us
  starting transfers between devices: 30 us -> 34 us
    all_to_all x1 -> x0, blocking collectives: 19.4 us -> none  [a2a_sum(): lax.all_to_all(x.reshape(split), axis, split_axis=dim, concat_axis=dim, t...]
    all_to_all x1 -> x2, waiting for transfers between devices: 10.4 us -> 23.9 us  [the longest x1 15.9 us: shards(): lax.all_to_all(pooled_part, ('y', 'expert'), split_axis=0, concat_axis=0,...]
    all_to_all x1 -> x2, starting transfers between devices: 7.15 us -> 11.7 us  [the longest x1 7.42 us: shards(): lax.all_to_all(pooled_part, ('y', 'expert'), split_axis=0, concat_axis=0,...]
  transfers between devices with their start and end apart: 8 -> 9, of which waited for: 8 -> 9; matrix products, arithmetic and copies ran while one was open for 1% -> 1% of each run, Pallas kernels for 0% -> 0%
where the time goes in v10:
time: 257 us; the launch traced here: 256 us
  waiting for transfers between devices  96.5 us (38%)
  blocking collectives  82.7 us (32%)
  starting transfers between devices  34 us (13%)
  matrix products  17.2 us (7%)
  between operations  14.5 us (6%)
  local copies, waits for them, and re-layouts  9.18 us (4%)
    all_gather x1, blocking collectives, shards(): gathered_weight = lax.all_gather(pool_weight, DP, axis=0, tiled=True)  42.2 us
    all_gather x1, waiting for transfers between devices, dp_gather(): lax.all_gather(lax.all_gather(x, 'y', axis=axis, tiled=True), 'z', axis=a...  25.8 us
    all_to_all x2, waiting for transfers between devices, a2a_gather(): return lax.all_to_all(spread, axis, split_axis=0, concat_axis=0, tiled=True)  23.4 us
    all_to_all x1, waiting for transfers between devices, shards(): lax.all_to_all(pooled_part, ('y', 'expert'), split_axis=0, concat_axis=0,...  15.9 us
    all_to_all x1, waiting for transfers between devices, shards(): lax.all_to_all(head_terms, ('y', 'expert'), split_axis=0, concat_axis=0,...  15.9 us
    all_gather x1, blocking collectives, dp_gather(): lax.all_gather(x, 'y', axis=axis, tiled=True)  14.7 us
    all_to_all x1, blocking collectives, shards(): lax.all_to_all(outgoing, 'expert', split_axis=0, concat_axis=1, tiled=True)  13 us
    all_gather x1, blocking collectives, shards(): attended_row = lax.all_gather(attended, 'y', axis=0, tiled=True)  12.8 us
  transfers between devices with their start and end apart: 9, of which 9 were waited for; matrix products, arithmetic and copies ran while one was open for 1% of the time, Pallas kernels for 0%

profile of v10, /device:TPU:2, one launch (start us, length us, event | category | flops | bytes accessed | tf_op | source)
XLA Modules:
  0.0 255.9 jit_solution(9770141099706596618)
XLA Ops:
  7.2 2.1 broadcast_in_dim.183
  9.3 8.5 %all-to-all-start = ((bf16[8,512,128]{2,1,0:T(8,128)(2,1)}), bf16[8,512,128]{2,1,0:T(8,128)(2,1)S(1)}, u32[]{:S(2)}, u32[]{:S(2)}) async-start(bf16[8,512,128]{2,1,0:T(8,128)(2,1)} %broadcast_in_dim.183), calls=%async_computation | async-start | bytes 2097152 | tf_op jit(solution)/shard_map/all_to_all | solution.py:65
  17.8 0.9 reshape.486
  20.4 12.8 %all_gather.12 = bf16[256,512]{1,0:T(8,128)(2,1)S(1)} all-gather(bf16[64,512]{1,0:T(8,128)(2,1)S(1)} %bitcast.145), channel_id=1, replica_groups=mesh['z'=8,'y'=4,'expert'=8] {'y'}, dimensions={0}, use_global_device_ids=true | all-gather | bytes 327680 | tf_op jit(solution)/shard_map/all_gather | solution.py:109
  33.2 13.4 %all-to-all-done = bf16[8,512,128]{2,1,0:T(8,128)(2,1)S(1)} async-done(((bf16[8,512,128]{2,1,0:T(8,128)(2,1)}), bf16[8,512,128]{2,1,0:T(8,128)(2,1)S(1)}, u32[]{:S(2)}, u32[]{:S(2)}) %all-to-all-start) | async-done | bytes 1048608 | tf_op jit(solution)/shard_map/all_to_all | solution.py:65
  47.0 0.6 copy.78
  47.6 1.1 reshape.492
  48.8 7.6 %all-to-all-start.1 = ((f32[32,8,1024]{2,1,0:T(8,128)}), f32[32,8,1024]{2,1,0:T(8,128)S(1)}, u32[]{:S(2)}, u32[]{:S(2)}) async-start(f32[32,8,1024]{2,1,0:T(8,128)} %reshape.492), calls=%async_computation.1 | async-start | bytes 2097152 | tf_op jit(solution)/shard_map/all_to_all | solution.py:116
  56.5 15.9 %all-to-all-done.1 = f32[32,8,1024]{2,1,0:T(8,128)S(1)} async-done(((f32[32,8,1024]{2,1,0:T(8,128)}), f32[32,8,1024]{2,1,0:T(8,128)S(1)}, u32[]{:S(2)}, u32[]{:S(2)}) %all-to-all-start.1) | async-done | bytes 1048608 | tf_op jit(solution)/shard_map/all_to_all | solution.py:116
  73.2 13.0 %all_to_all.37 = bf16[8,8,4224]{2,1,0:T(8,128)(2,1)S(1)} all-to-all(bf16[8,8,4224]{2,1,0:T(8,128)(2,1)S(1)} %pad_maximum_fusion), channel_id=1, replica_groups=mesh['z'=8,'y'=4,'expert'=8] {'expert'}, dimensions={0} | all-to-all | bytes 1081344 | tf_op jit(solution)/shard_map/all_to_all | solution.py:137
  86.7 14.7 %all_gather.14 = bf16[96,1,4096]{2,0,1:T(8,128)(2,1)} all-gather(bf16[24,1,4096]{2,0,1:T(8,128)(2,1)S(1)} %bitcast.142), channel_id=1, replica_groups=mesh['z'=8,'y'=4,'expert'=8] {'y'}, dimensions={0}, use_global_device_ids=true | all-gather | bytes 983040 | tf_op jit(solution)/shard_map/all_gather | solution.py:69
  102.0 42.2 %all-gather = f32[32,24,2]{1,2,0:T(2,128)S(1)} all-gather(f32[1,24,2]{1,2,0:T(2,128)S(1)} %fusion.57), channel_id=1, replica_groups=mesh['z'=8,'y'=4,'expert'=8] {'z','y'}, dimensions={0}, use_global_device_ids=true | all-gather | bytes 6336 | tf_op jit(solution)/shard_map/all_gather | solution.py:167
  144.1 25.8 %all-gather.3.cloned.1.call-done = bf16[768,1,4096]{2,0,1:T(8,128)(2,1)} async-done(((bf16[96,1,4096]{2,0,1:T(8,128)(2,1)}), bf16[768,1,4096]{2,0,1:T(8,128)(2,1)}) %all-gather.3.cloned.1.call-update) | async-done | bytes 6291472 | tf_op jit(solution)/shard_map/all_gather | solution.py:69
  170.0 7.0 %fusion.3 = f32[768,448]{0,1:T(8,128)S(1)} fusion(bf16[768,1,4096]{2,0,1:T(8,128)(2,1)} %all-gather.3.cloned.1.call-done, bf16[1,4096,448]{1,2,0:T(8,128)(2,1)} %param.26), kind=kOutput, calls=%fused_computation.3 | convolution fusion | flops 2818572288 | bytes 11337728 | tf_op jit(solution)/shard_map/ned,edf->nf/dot_general | solution.py:169
  177.1 3.1 %fusion.14 = bf16[768,448]{0,1:T(8,128)(2,1)S(1)} fusion(bf16[1,4096,448]{1,2,0:T(8,128)(2,1)S(1)} %copy-done.8, bf16[768,1,4096]{2,0,1:T(8,128)(2,1)S(1)} %copy-done.7, f32[768,448]{0,1:T(8,128)S(1)} %fusion.3), kind=kOutput, calls=%fused_computation.13 | convolution fusion | flops 2820636672 | bytes 12025856 | tf_op jit(solution)/shard_map/ned,edf->nf/dot_general | solution.py:170
  181.0 3.4 %convolution_add_fusion = f32[64,4096]{1,0:T(8,128)S(1)} fusion(f32[64,448]{1,0:T(8,128)S(1)} %reshape.502, bf16[1,448,4096]{2,1,0:T(8,128)(2,1)} %param.28, f32[4096]{0:T(1024)S(1)} %get-tuple-element.2, pred[64]{0:T(512)(128)(4,1)S(1)} %iota_compare_fusion.5), kind=kOutput, calls=%fused_computation.5 | convolution fusion | flops 705167360 | bytes 4849728 | tf_op jit(solution)/shard_map/dot_general | solution.py:178
  184.4 0.6 copy.96
  185.2 1.6 copy.83
  186.8 7.4 %all-to-all-start.3 = ((f32[32,16,512]{2,1,0:T(8,128)}), f32[32,16,512]{2,1,0:T(8,128)S(1)}, u32[]{:S(2)}, u32[]{:S(2)}) async-start(f32[32,16,512]{2,1,0:T(8,128)} %copy.83), calls=%async_computation.3 | async-start | bytes 2097152 | tf_op jit(solution)/shard_map/all_to_all | solution.py:192
  194.3 15.9 %all-to-all-done.3 = f32[32,16,512]{2,1,0:T(8,128)S(1)} async-done(((f32[32,16,512]{2,1,0:T(8,128)}), f32[32,16,512]{2,1,0:T(8,128)S(1)}, u32[]{:S(2)}, u32[]{:S(2)}) %all-to-all-start.3) | async-done | bytes 1048608 | tf_op jit(solution)/shard_map/all_to_all | solution.py:192
  210.3 0.6 reshape.505
  210.9 4.3 %all-to-all-start.4 = ((f32[8,2,512]{2,1,0:T(2,128)}), f32[8,2,512]{2,1,0:T(2,128)S(1)}, u32[]{:S(2)}, u32[]{:S(2)}) async-start(f32[8,2,512]{2,1,0:T(2,128)} %reshape.505), calls=%async_computation.4 | async-start | bytes 65536 | tf_op jit(solution)/shard_map/all_to_all | solution.py:196
  215.3 8.0 %all-to-all-done.4 = f32[8,2,512]{2,1,0:T(2,128)S(1)} async-done(((f32[8,2,512]{2,1,0:T(2,128)}), f32[8,2,512]{2,1,0:T(2,128)S(1)}, u32[]{:S(2)}, u32[]{:S(2)}) %all-to-all-start.4) | async-done | bytes 32800 | tf_op jit(solution)/shard_map/all_to_all | solution.py:196
  223.5 1.1 collective-permute-done
  224.6 1.5 collective-permute-start.1
  226.1 2.1 collective-permute-done.1
  228.2 0.8 collective-permute-start.2
  229.0 4.3 %collective-permute-done.2 = f32[2]{0:T(128)S(1)} collective-permute-done((f32[2]{0:T(128)S(1)}, f32[2]{0:T(128)S(1)}, u32[]{:S(2)}, u32[]{:S(2)}) %collective-permute-start.2) | collective-permute-done | bytes 40 | tf_op jit(solution)/shard_map/ppermute | solution.py:75
  233.3 0.7 broadcast_in_dim.198
  234.0 3.9 %all-to-all-start.5 = ((bf16[32,2,512]{2,1,0:T(2,128)(2,1)}), bf16[32,2,512]{2,1,0:T(2,128)(2,1)S(1)}, u32[]{:S(2)}, u32[]{:S(2)}) async-start(bf16[32,2,512]{2,1,0:T(2,128)(2,1)} %broadcast_in_dim.198), calls=%async_computation.5 | async-start | bytes 131072 | tf_op jit(solution)/shard_map/all_to_all | solution.py:65
  237.9 10.0 %all-to-all-done.5 = bf16[32,2,512]{2,1,0:T(2,128)(2,1)S(1)} async-done(((bf16[32,2,512]{2,1,0:T(2,128)(2,1)}), bf16[32,2,512]{2,1,0:T(2,128)(2,1)S(1)}, u32[]{:S(2)}, u32[]{:S(2)}) %all-to-all-start.5) | async-done | bytes 65568 | tf_op jit(solution)/shard_map/all_to_all | solution.py:65
  248.3 0.8 fusion.26
  (86 shorter events, 5.7 us)
Async XLA Ops:
  7.2 11.5 %copy-start = (bf16[2,1024,128]{2,1,0:T(8,128)(2,1)S(1)}, bf16[2,1024,128]{2,1,0:T(8,128)(2,1)}, u32[]{:S(2)}) copy-start(bf16[2,1024,128]{2,1,0:T(8,128)(2,1)} %param.20) | copy-start | bytes 1572868
  7.2 11.9 %copy-start.2 = (bf16[64,128]{1,0:T(8,128)(2,1)S(1)}, bf16[64,128]{1,0:T(8,128)(2,1)}, u32[]{:S(2)}) copy-start(bf16[64,128]{1,0:T(8,128)(2,1)} %param.18) | copy-start | bytes 49156
  7.2 12.5 %copy-start.11 = (bf16[64,128]{1,0:T(8,128)(2,1)S(1)}, bf16[64,128]{1,0:T(8,128)(2,1)}, u32[]{:S(2)}) copy-start(bf16[64,128]{1,0:T(8,128)(2,1)} %param.19) | copy-start | bytes 49156
  7.2 12.7 %copy-start.9 = (bf16[2,1024,128]{2,1,0:T(8,128)(2,1)S(1)}, bf16[2,1024,128]{2,1,0:T(8,128)(2,1)}, u32[]{:S(2)}) copy-start(bf16[2,1024,128]{2,1,0:T(8,128)(2,1)} %param.21) | copy-start | bytes 1572868
  9.3 37.2 %all-to-all-start = ((bf16[8,512,128]{2,1,0:T(8,128)(2,1)}), bf16[8,512,128]{2,1,0:T(8,128)(2,1)S(1)}, u32[]{:S(2)}, u32[]{:S(2)}) async-start(bf16[8,512,128]{2,1,0:T(8,128)(2,1)} %broadcast_in_dim.183), calls=%async_computation | async-start | bytes 2097152 | tf_op jit(solution)/shard_map/all_to_all | solution.py:65
  47.0 9.5 %copy-start.6 = (s32[8,2]{0,1:T(2,128)S(1)}, s32[8,2]{0,1:T(2,128)}, u32[]{:S(2)}) copy-start(s32[8,2]{0,1:T(2,128)} %param.25) | copy-start | bytes 196
  47.0 25.7 %copy-start.1 = (bf16[8,4096]{1,0:T(8,128)(2,1)S(1)}, bf16[8,4096]{1,0:T(8,128)(2,1)}, u32[]{:S(2)}) copy-start(bf16[8,4096]{1,0:T(8,128)(2,1)} %param.16) | copy-start | bytes 196612
  47.6 25.2 %copy-start.3 = (f32[4096]{0:T(1024)S(1)}, f32[4096]{0:T(1024)}, u32[]{:S(2)}) copy-start(f32[4096]{0:T(1024)} %param.23) | copy-start | bytes 49156
  48.8 23.6 %all-to-all-start.1 = ((f32[32,8,1024]{2,1,0:T(8,128)}), f32[32,8,1024]{2,1,0:T(8,128)S(1)}, u32[]{:S(2)}, u32[]{:S(2)}) async-start(f32[32,8,1024]{2,1,0:T(8,128)} %reshape.492), calls=%async_computation.1 | async-start | bytes 2097152 | tf_op jit(solution)/shard_map/all_to_all | solution.py:116
  56.4 113.6 %all-gather.3.cloned.1.call-start = ((), (), s32[]{:S(2)}) async-start(), calls=%async_computation.6 | async-start | bytes 7077888 | tf_op jit(solution)/shard_map/all_gather | solution.py:69
  72.4 29.3 %copy-start.10 = (bf16[4096,8]{0,1:T(8,128)(2,1)S(1)}, bf16[4096,8]{0,1:T(8,128)(2,1)}, u32[]{:S(2)}) copy-start(bf16[4096,8]{0,1:T(8,128)(2,1)} %param.24) | copy-start | bytes 196612
  170.0 7.1 %copy-start.7 = (bf16[768,1,4096]{2,0,1:T(8,128)(2,1)S(1)}, bf16[768,1,4096]{2,0,1:T(8,128)(2,1)}, u32[]{:S(2)}) copy-start(bf16[768,1,4096]{2,0,1:T(8,128)(2,1)} %all-gather.3.cloned.1.call-done) | copy-start | bytes 18874372
  170.0 7.1 %copy-start.8 = (bf16[1,4096,448]{1,2,0:T(8,128)(2,1)S(1)}, bf16[1,4096,448]{1,2,0:T(8,128)(2,1)}, u32[]{:S(2)}) copy-start(bf16[1,4096,448]{1,2,0:T(8,128)(2,1)} %param.27) | copy-start | bytes 11010052
  185.0 9.2 %copy-start.12 = (s32[64]{0:T(128)S(1)}, s32[64]{0:T(128)}, u32[]{:S(2)}) copy-start(s32[64]{0:T(128)} %param.31) | copy-start | bytes 772
  185.0 48.2 %copy-start.5 = (f32[512]{0:T(512)S(1)}, f32[512]{0:T(512)}, u32[]{:S(2)}) copy-start(f32[512]{0:T(512)} %param.29) | copy-start | bytes 6148
  185.0 52.8 %copy-start.13 = (f32[4]{0:T(128)S(1)}, f32[4]{0:T(128)}, u32[]{:S(2)}) copy-start(f32[4]{0:T(128)} %param.30) | copy-start | bytes 52
  186.8 23.4 %all-to-all-start.3 = ((f32[32,16,512]{2,1,0:T(8,128)}), f32[32,16,512]{2,1,0:T(8,128)S(1)}, u32[]{:S(2)}, u32[]{:S(2)}) async-start(f32[32,16,512]{2,1,0:T(8,128)} %copy.83), calls=%async_computation.3 | async-start | bytes 2097152 | tf_op jit(solution)/shard_map/all_to_all | solution.py:192
  210.9 12.3 %all-to-all-start.4 = ((f32[8,2,512]{2,1,0:T(2,128)}), f32[8,2,512]{2,1,0:T(2,128)S(1)}, u32[]{:S(2)}, u32[]{:S(2)}) async-start(f32[8,2,512]{2,1,0:T(2,128)} %reshape.505), calls=%async_computation.4 | async-start | bytes 65536 | tf_op jit(solution)/shard_map/all_to_all | solution.py:196
  223.4 1.2 collective-permute-start
  224.6 3.6 %collective-permute-start.1 = (f32[2]{0:T(128)S(1)}, f32[2]{0:T(128)S(1)}, u32[]{:S(2)}, u32[]{:S(2)}) collective-permute-start(f32[2]{0:T(128)S(1)} %add.117), channel_id=1, source_target_pairs={{0,2},{1,3},{2,0},{3,1},{4,6},{5,7},{6,4},{7,5},{8,10},{9,11},{10,... | collective-permute-start | bytes 32 | tf_op jit(solution)/shard_map/ppermute | solution.py:75
  228.2 5.1 %collective-permute-start.2 = (f32[2]{0:T(128)S(1)}, f32[2]{0:T(128)S(1)}, u32[]{:S(2)}, u32[]{:S(2)}) collective-permute-start(f32[2]{0:T(128)S(1)} %add.118), channel_id=1, source_target_pairs={{0,4},{1,5},{2,6},{3,7},{4,0},{5,1},{6,2},{7,3},{8,12},{9,13},{10,... | collective-permute-start | bytes 32 | tf_op jit(solution)/shard_map/ppermute | solution.py:75
  233.3 15.8 %copy-start.4 = (bf16[2,512]{1,0:T(2,128)(2,1)}, bf16[2,512]{1,0:T(2,128)(2,1)S(1)}, u32[]{:S(2)}) copy-start(bf16[2,512]{1,0:T(2,128)(2,1)S(1)} %multiply_convert_fusion.1) | copy-start | bytes 6148
  234.0 13.9 %all-to-all-start.5 = ((bf16[32,2,512]{2,1,0:T(2,128)(2,1)}), bf16[32,2,512]{2,1,0:T(2,128)(2,1)S(1)}, u32[]{:S(2)}, u32[]{:S(2)}) async-start(bf16[32,2,512]{2,1,0:T(2,128)(2,1)} %broadcast_in_dim.198), calls=%async_computation.5 | async-start | bytes 131072 | tf_op jit(solution)/shard_map/all_to_all | solution.py:65
Sparse Core Ops, SparseCore 0:
  101.6 68.3 all-gather.2

commit v11 on v8

--- a/solution.py
+++ b/solution.py
@@ -67,6 +67,22 @@
 
 def dp_gather(x, axis):
     return lax.all_gather(lax.all_gather(x, "y", axis=axis, tiled=True), "z", axis=axis, tiled=True)
+
+
+def ring_gather(x, axis, count):
+    me = lax.axis_index(axis)
+    to_next = [(a, (a + 1) % count) for a in range(count)]
+    to_prev = [(a, (a - 1) % count) for a in range(count)]
+    from_prev, from_next = x, x
+    by_offset = {0: x}
+    for step in range(1, count // 2 + 1):
+        from_prev = lax.ppermute(from_prev, axis, to_next)
+        by_offset[(count - step) % count] = from_prev
+        if step < count - step:
+            from_next = lax.ppermute(from_next, axis, to_prev)
+            by_offset[step] = from_next
+    relative = jnp.stack([by_offset[d] for d in range(count)])
+    return jnp.roll(relative, me, axis=0)
 
 
 def doubling_sum(x, axis, count):
@@ -107,7 +123,7 @@
     y_count = lax.axis_size("y")
     z_count = lax.axis_size("z")
     attended_row = lax.all_gather(attended, "y", axis=0, tiled=True)
-    weight_row = a2a_gather(out_weight, "z", z_count)
+    weight_row = ring_gather(out_weight, "z", z_count)
     col_block = out_weight.shape[1]
     head_terms = jnp.einsum(
         "th,zhc->tzc", attended_row, weight_row, preferred_element_type=jnp.float32

time: 256 us -> 263 us (1.027)
  starting transfers between devices: 30 us -> 34.5 us
  waiting for transfers between devices: 82.7 us -> 85.8 us
    all_to_all x2 -> x1, waiting for transfers between devices: 23.4 us -> 10 us  [a2a_gather(): return lax.all_to_all(spread, axis, split_axis=0, concat_axis=0, tiled=True)]
    ppermute x0 -> x7, waiting for transfers between devices: none -> 12.8 us  [the longest x4 12.8 us: ring_gather(): from_prev = lax.ppermute(from_prev, axis, to_next)]
    ppermute x0 -> x7, starting transfers between devices: none -> 12.5 us  [the longest x3 10.5 us: ring_gather(): from_next = lax.ppermute(from_next, axis, to_prev)]
    all_to_all x2 -> x1, starting transfers between devices: 12.3 us -> 3.85 us  [a2a_gather(): return lax.all_to_all(spread, axis, split_axis=0, concat_axis=0, tiled=True)]
    all_gather x1, waiting for transfers between devices: 26 us -> 29.7 us  [dp_gather(): lax.all_gather(lax.all_gather(x, 'y', axis=axis, tiled=True), 'z', axis=a...]
  transfers between devices with their start and end apart: 8 -> 14, of which waited for: 8 -> 10; matrix products, arithmetic and copies ran while one was open for 1% -> 1% of each run, Pallas kernels for 0% -> 0%
where the time goes in v11:
time: 263 us
  blocking collectives  102 us (39%)
  waiting for transfers between devices  85.8 us (33%)
  starting transfers between devices  34.5 us (13%)
  matrix products  17.9 us (7%)
  between operations  14.6 us (6%)
  local copies, waits for them, and re-layouts  5.74 us (2%)
    all_gather x1, blocking collectives, shards(): gathered_weight = lax.all_gather(pool_weight, DP, axis=0, tiled=True)  42.2 us
    all_gather x1, waiting for transfers between devices, dp_gather(): lax.all_gather(lax.all_gather(x, 'y', axis=axis, tiled=True), 'z', axis=a...  29.7 us
    all_to_all x1, blocking collectives, a2a_sum(): lax.all_to_all(x.reshape(split), axis, split_axis=dim, concat_axis=dim, t...  19.3 us
    all_to_all x1, waiting for transfers between devices, shards(): lax.all_to_all(head_terms, ('y', 'expert'), split_axis=0, concat_axis=0,...  15.9 us
    all_gather x1, blocking collectives, dp_gather(): lax.all_gather(x, 'y', axis=axis, tiled=True)  14.7 us
    all_to_all x1, blocking collectives, shards(): lax.all_to_all(outgoing, 'expert', split_axis=0, concat_axis=1, tiled=True)  13.1 us
    ppermute x4, waiting for transfers between devices, ring_gather(): from_prev = lax.ppermute(from_prev, axis, to_next)  12.8 us
    all_gather x1, blocking collectives, shards(): attended_row = lax.all_gather(attended, 'y', axis=0, tiled=True)  12.8 us
  transfers between devices with their start and end apart: 14, of which 10 were waited for; matrix products, arithmetic and copies ran while one was open for 1% of the time, Pallas kernels for 0%

profile of v11, /device:TPU:2, one launch (start us, length us, event | category | flops | bytes accessed | tf_op | source)
XLA Modules:
  0.0 262.6 jit_solution(15660239210888640616)
XLA Ops:
  7.2 2.0 collective-permute-start.3
  9.2 4.0 %collective-permute-start = (bf16[512,128]{1,0:T(8,128)(2,1)}, bf16[512,128]{1,0:T(8,128)(2,1)S(1)}, u32[]{:S(2)}, u32[]{:S(2)}) collective-permute-start(bf16[512,128]{1,0:T(8,128)(2,1)} %param.22), channel_id=1, source_target_pairs={{0,224},{32,0},{64,32},{96,64},{128,96},{160,128},{192,160},{224,1... | collective-permute-start | bytes 393224 | tf_op jit(solution)/shard_map/ppermute | solution.py:82
  13.2 0.9 reshape.482
  14.5 1.0 fusion.62
  17.1 12.8 %all_gather.12 = bf16[256,512]{1,0:T(8,128)(2,1)S(1)} all-gather(bf16[64,512]{1,0:T(8,128)(2,1)S(1)} %bitcast.165), channel_id=1, replica_groups=mesh['z'=8,'y'=4,'expert'=8] {'y'}, dimensions={0}, use_global_device_ids=true | all-gather | bytes 327680 | tf_op jit(solution)/shard_map/all_gather | solution.py:125
  29.9 3.2 %collective-permute-start.1 = (bf16[512,128]{1,0:T(8,128)(2,1)S(1)}, bf16[512,128]{1,0:T(8,128)(2,1)S(1)}, u32[]{:S(2)}, u32[]{:S(2)}) collective-permute-start(bf16[512,128]{1,0:T(8,128)(2,1)S(1)} %collective-permute-done), channel_id=1, source_target_pairs={{0,224},{32,0},{64,32},{96,64},{128,96},{160,128},{192,160},{224,1... | collective-permute-start | bytes 393224 | tf_op jit(solution)/shard_map/ppermute | solution.py:82
  33.1 2.9 %collective-permute-done.4 = bf16[512,128]{1,0:T(8,128)(2,1)S(1)} collective-permute-done((bf16[512,128]{1,0:T(8,128)(2,1)S(1)}, bf16[512,128]{1,0:T(8,128)(2,1)S(1)}, u32[]{:S(2)}, u32[]{:S(2)}) %collective-permute-start.4) | collective-permute-done | bytes 131104 | tf_op jit(solution)/shard_map/ppermute | solution.py:79
  36.0 3.2 %collective-permute-start.2 = (bf16[512,128]{1,0:T(8,128)(2,1)S(1)}, bf16[512,128]{1,0:T(8,128)(2,1)S(1)}, u32[]{:S(2)}, u32[]{:S(2)}) collective-permute-start(bf16[512,128]{1,0:T(8,128)(2,1)S(1)} %collective-permute-done.1), channel_id=1, source_target_pairs={{0,224},{32,0},{64,32},{96,64},{128,96},{160,128},{192,160},{224,1... | collective-permute-start | bytes 393224 | tf_op jit(solution)/shard_map/ppermute | solution.py:82
  39.3 3.8 %collective-permute-done.5 = bf16[512,128]{1,0:T(8,128)(2,1)S(1)} collective-permute-done((bf16[512,128]{1,0:T(8,128)(2,1)S(1)}, bf16[512,128]{1,0:T(8,128)(2,1)S(1)}, u32[]{:S(2)}, u32[]{:S(2)}) %collective-permute-start.5) | collective-permute-done | bytes 131104 | tf_op jit(solution)/shard_map/ppermute | solution.py:79
  43.1 6.1 %collective-permute-done.6 = bf16[512,128]{1,0:T(8,128)(2,1)S(1)} collective-permute-done((bf16[512,128]{1,0:T(8,128)(2,1)S(1)}, bf16[512,128]{1,0:T(8,128)(2,1)S(1)}, u32[]{:S(2)}, u32[]{:S(2)}) %collective-permute-start.6) | collective-permute-done | bytes 131104 | tf_op jit(solution)/shard_map/ppermute | solution.py:79
  50.6 1.1 reshape.488
  51.8 8.1 %all-to-all-start = ((f32[32,8,1024]{2,1,0:T(8,128)}), f32[32,8,1024]{2,1,0:T(8,128)S(1)}, u32[]{:S(2)}, u32[]{:S(2)}) async-start(f32[32,8,1024]{2,1,0:T(8,128)} %reshape.488), calls=%async_computation | async-start | bytes 2097152 | tf_op jit(solution)/shard_map/all_to_all | solution.py:132
  60.0 15.9 %all-to-all-done = f32[32,8,1024]{2,1,0:T(8,128)S(1)} async-done(((f32[32,8,1024]{2,1,0:T(8,128)}), f32[32,8,1024]{2,1,0:T(8,128)S(1)}, u32[]{:S(2)}, u32[]{:S(2)}) %all-to-all-start) | async-done | bytes 1048608 | tf_op jit(solution)/shard_map/all_to_all | solution.py:132
  76.7 13.1 %all_to_all.32 = bf16[8,8,4224]{2,1,0:T(8,128)(2,1)S(1)} all-to-all(bf16[8,8,4224]{2,1,0:T(8,128)(2,1)S(1)} %pad_maximum_fusion), channel_id=1, replica_groups=mesh['z'=8,'y'=4,'expert'=8] {'expert'}, dimensions={0} | all-to-all | bytes 1081344 | tf_op jit(solution)/shard_map/all_to_all | solution.py:153
  90.4 14.7 %all_gather.14 = bf16[96,1,4096]{2,0,1:T(8,128)(2,1)} all-gather(bf16[24,1,4096]{2,0,1:T(8,128)(2,1)S(1)} %bitcast.162), channel_id=1, replica_groups=mesh['z'=8,'y'=4,'expert'=8] {'y'}, dimensions={0}, use_global_device_ids=true | all-gather | bytes 983040 | tf_op jit(solution)/shard_map/all_gather | solution.py:69
  105.6 42.2 %all-gather = f32[32,24,2]{1,2,0:T(2,128)S(1)} all-gather(f32[1,24,2]{1,2,0:T(2,128)S(1)} %fusion.58), channel_id=1, replica_groups=mesh['z'=8,'y'=4,'expert'=8] {'z','y'}, dimensions={0}, use_global_device_ids=true | all-gather | bytes 6336 | tf_op jit(solution)/shard_map/all_gather | solution.py:183
  147.8 29.7 %all-gather.3.cloned.1.call-done = bf16[768,1,4096]{2,0,1:T(8,128)(2,1)} async-done(((bf16[96,1,4096]{2,0,1:T(8,128)(2,1)}), bf16[768,1,4096]{2,0,1:T(8,128)(2,1)}) %all-gather.3.cloned.1.call-update) | async-done | bytes 6291472 | tf_op jit(solution)/shard_map/all_gather | solution.py:69
  177.5 7.0 %fusion.3 = f32[768,448]{0,1:T(8,128)S(1)} fusion(bf16[768,1,4096]{2,0,1:T(8,128)(2,1)} %all-gather.3.cloned.1.call-done, bf16[1,4096,448]{1,2,0:T(8,128)(2,1)} %param.26), kind=kOutput, calls=%fused_computation.3 | convolution fusion | flops 2818572288 | bytes 11337728 | tf_op jit(solution)/shard_map/ned,edf->nf/dot_general | solution.py:185
  184.5 3.1 %fusion.14 = bf16[768,448]{0,1:T(8,128)(2,1)S(1)} fusion(bf16[1,4096,448]{1,2,0:T(8,128)(2,1)S(1)} %copy-done.8, bf16[768,1,4096]{2,0,1:T(8,128)(2,1)S(1)} %copy-done.7, f32[768,448]{0,1:T(8,128)S(1)} %fusion.3), kind=kOutput, calls=%fused_computation.13 | convolution fusion | flops 2820636672 | bytes 12025856 | tf_op jit(solution)/shard_map/ned,edf->nf/dot_general | solution.py:186
  188.4 3.4 %convolution_add_fusion = f32[64,4096]{1,0:T(8,128)S(1)} fusion(f32[64,448]{1,0:T(8,128)S(1)} %reshape.498, bf16[1,448,4096]{2,1,0:T(8,128)(2,1)} %param.28, f32[4096]{0:T(1024)S(1)} %get-tuple-element.2, pred[64]{0:T(512)(128)(4,1)S(1)} %iota_compare_fusion.5), kind=kOutput, calls=%fused_computation.5 | convolution fusion | flops 705167360 | bytes 4849728 | tf_op jit(solution)/shard_map/dot_general | solution.py:194
  192.0 19.3 %all_to_all.33 = f32[64,8,512]{2,0,1:T(8,128)S(1)} all-to-all(f32[64,8,512]{2,0,1:T(8,128)S(1)} %bitcast.157), channel_id=1, replica_groups=mesh['z'=8,'y'=4,'expert'=8] {'expert'}, dimensions={1} | all-to-all | bytes 2097152 | tf_op jit(solution)/shard_map/all_to_all | solution.py:59
  211.4 0.7 reshape.500
  212.1 7.2 %all-to-all-start.3 = ((f32[32,2,512]{2,1,0:T(2,128)}), f32[32,2,512]{2,1,0:T(2,128)S(1)}, u32[]{:S(2)}, u32[]{:S(2)}) async-start(f32[32,2,512]{2,1,0:T(2,128)} %reshape.500), calls=%async_computation.3 | async-start | bytes 262144 | tf_op jit(solution)/shard_map/all_to_all | solution.py:59
  219.5 10.4 %all-to-all-done.3 = f32[32,2,512]{2,1,0:T(2,128)S(1)} async-done(((f32[32,2,512]{2,1,0:T(2,128)}), f32[32,2,512]{2,1,0:T(2,128)S(1)}, u32[]{:S(2)}, u32[]{:S(2)}) %all-to-all-start.3) | async-done | bytes 131104 | tf_op jit(solution)/shard_map/all_to_all | solution.py:59
  230.1 1.1 collective-permute-done.7
  231.3 1.4 collective-permute-start.8
  232.7 2.2 collective-permute-done.8
  234.8 1.4 collective-permute-start.9
  236.2 3.7 %collective-permute-done.9 = f32[2]{0:T(128)S(1)} collective-permute-done((f32[2]{0:T(128)S(1)}, f32[2]{0:T(128)S(1)}, u32[]{:S(2)}, u32[]{:S(2)}) %collective-permute-start.9) | collective-permute-done | bytes 40 | tf_op jit(solution)/shard_map/ppermute | solution.py:91
  240.7 3.9 %all-to-all-start.4 = ((bf16[32,2,512]{2,1,0:T(2,128)(2,1)}), bf16[32,2,512]{2,1,0:T(2,128)(2,1)S(1)}, u32[]{:S(2)}, u32[]{:S(2)}) async-start(bf16[32,2,512]{2,1,0:T(2,128)(2,1)} %broadcast_in_dim.191), calls=%async_computation.4 | async-start | bytes 131072 | tf_op jit(solution)/shard_map/all_to_all | solution.py:65
  244.5 10.0 %all-to-all-done.4 = bf16[32,2,512]{2,1,0:T(2,128)(2,1)S(1)} async-done(((bf16[32,2,512]{2,1,0:T(2,128)(2,1)}), bf16[32,2,512]{2,1,0:T(2,128)(2,1)S(1)}, u32[]{:S(2)}, u32[]{:S(2)}) %all-to-all-start.4) | async-done | bytes 65568 | tf_op jit(solution)/shard_map/all_to_all | solution.py:65
  254.9 0.8 fusion.26
  (110 shorter events, 7.6 us)
Async XLA Ops:
  7.2 6.9 %copy-start = (bf16[2,1024,128]{2,1,0:T(8,128)(2,1)S(1)}, bf16[2,1024,128]{2,1,0:T(8,128)(2,1)}, u32[]{:S(2)}) copy-start(bf16[2,1024,128]{2,1,0:T(8,128)(2,1)} %param.20) | copy-start | bytes 1572868
  7.2 8.6 %copy-start.11 = (bf16[64,128]{1,0:T(8,128)(2,1)S(1)}, bf16[64,128]{1,0:T(8,128)(2,1)}, u32[]{:S(2)}) copy-start(bf16[64,128]{1,0:T(8,128)(2,1)} %param.19) | copy-start | bytes 49156
  7.2 8.9 %copy-start.9 = (bf16[2,1024,128]{2,1,0:T(8,128)(2,1)S(1)}, bf16[2,1024,128]{2,1,0:T(8,128)(2,1)}, u32[]{:S(2)}) copy-start(bf16[2,1024,128]{2,1,0:T(8,128)(2,1)} %param.21) | copy-start | bytes 1572868
  7.2 22.7 %collective-permute-start.3 = (bf16[512,128]{1,0:T(8,128)(2,1)}, bf16[512,128]{1,0:T(8,128)(2,1)S(1)}, u32[]{:S(2)}, u32[]{:S(2)}) collective-permute-start(bf16[512,128]{1,0:T(8,128)(2,1)} %param.22), channel_id=1, source_target_pairs={{0,32},{32,64},{64,96},{96,128},{128,160},{160,192},{192,224},{224... | collective-permute-start | bytes 393224 | tf_op jit(solution)/shard_map/ppermute | solution.py:79
  9.2 20.7 %collective-permute-start = (bf16[512,128]{1,0:T(8,128)(2,1)}, bf16[512,128]{1,0:T(8,128)(2,1)S(1)}, u32[]{:S(2)}, u32[]{:S(2)}) collective-permute-start(bf16[512,128]{1,0:T(8,128)(2,1)} %param.22), channel_id=1, source_target_pairs={{0,224},{32,0},{64,32},{96,64},{128,96},{160,128},{192,160},{224,1... | collective-permute-start | bytes 393224 | tf_op jit(solution)/shard_map/ppermute | solution.py:82
  16.1 0.9 copy-start.1
  29.9 6.2 %collective-permute-start.4 = (bf16[512,128]{1,0:T(8,128)(2,1)S(1)}, bf16[512,128]{1,0:T(8,128)(2,1)S(1)}, u32[]{:S(2)}, u32[]{:S(2)}) collective-permute-start(bf16[512,128]{1,0:T(8,128)(2,1)S(1)} %collective-permute-done.3), channel_id=1, source_target_pairs={{0,32},{32,64},{64,96},{96,128},{128,160},{160,192},{192,224},{224... | collective-permute-start | bytes 393224 | tf_op jit(solution)/shard_map/ppermute | solution.py:79
  29.9 6.2 %collective-permute-start.1 = (bf16[512,128]{1,0:T(8,128)(2,1)S(1)}, bf16[512,128]{1,0:T(8,128)(2,1)S(1)}, u32[]{:S(2)}, u32[]{:S(2)}) collective-permute-start(bf16[512,128]{1,0:T(8,128)(2,1)S(1)} %collective-permute-done), channel_id=1, source_target_pairs={{0,224},{32,0},{64,32},{96,64},{128,96},{160,128},{192,160},{224,1... | collective-permute-start | bytes 393224 | tf_op jit(solution)/shard_map/ppermute | solution.py:82
  36.0 7.0 %collective-permute-start.5 = (bf16[512,128]{1,0:T(8,128)(2,1)S(1)}, bf16[512,128]{1,0:T(8,128)(2,1)S(1)}, u32[]{:S(2)}, u32[]{:S(2)}) collective-permute-start(bf16[512,128]{1,0:T(8,128)(2,1)S(1)} %collective-permute-done.4), channel_id=1, source_target_pairs={{0,32},{32,64},{64,96},{96,128},{128,160},{160,192},{192,224},{224... | collective-permute-start | bytes 393224 | tf_op jit(solution)/shard_map/ppermute | solution.py:79
  36.0 7.0 %collective-permute-start.2 = (bf16[512,128]{1,0:T(8,128)(2,1)S(1)}, bf16[512,128]{1,0:T(8,128)(2,1)S(1)}, u32[]{:S(2)}, u32[]{:S(2)}) collective-permute-start(bf16[512,128]{1,0:T(8,128)(2,1)S(1)} %collective-permute-done.1), channel_id=1, source_target_pairs={{0,224},{32,0},{64,32},{96,64},{128,96},{160,128},{192,160},{224,1... | collective-permute-start | bytes 393224 | tf_op jit(solution)/shard_map/ppermute | solution.py:82
  43.1 6.2 %collective-permute-start.6 = (bf16[512,128]{1,0:T(8,128)(2,1)S(1)}, bf16[512,128]{1,0:T(8,128)(2,1)S(1)}, u32[]{:S(2)}, u32[]{:S(2)}) collective-permute-start(bf16[512,128]{1,0:T(8,128)(2,1)S(1)} %collective-permute-done.5), channel_id=1, source_target_pairs={{0,32},{32,64},{64,96},{96,128},{128,160},{160,192},{192,224},{224... | collective-permute-start | bytes 393224 | tf_op jit(solution)/shard_map/ppermute | solution.py:79
  50.6 9.3 %copy-start.6 = (s32[8,2]{0,1:T(2,128)S(1)}, s32[8,2]{0,1:T(2,128)}, u32[]{:S(2)}) copy-start(s32[8,2]{0,1:T(2,128)} %param.25) | copy-start | bytes 196
  51.8 24.4 %copy-start.2 = (bf16[8,4096]{1,0:T(8,128)(2,1)S(1)}, bf16[8,4096]{1,0:T(8,128)(2,1)}, u32[]{:S(2)}) copy-start(bf16[8,4096]{1,0:T(8,128)(2,1)} %param.16) | copy-start | bytes 196612
  51.8 24.5 %copy-start.3 = (f32[4096]{0:T(1024)S(1)}, f32[4096]{0:T(1024)}, u32[]{:S(2)}) copy-start(f32[4096]{0:T(1024)} %param.23) | copy-start | bytes 49156
  51.8 24.1 %all-to-all-start = ((f32[32,8,1024]{2,1,0:T(8,128)}), f32[32,8,1024]{2,1,0:T(8,128)S(1)}, u32[]{:S(2)}, u32[]{:S(2)}) async-start(f32[32,8,1024]{2,1,0:T(8,128)} %reshape.488), calls=%async_computation | async-start | bytes 2097152 | tf_op jit(solution)/shard_map/all_to_all | solution.py:132
  59.9 117.5 %all-gather.3.cloned.1.call-start = ((), (), s32[]{:S(2)}) async-start(), calls=%async_computation.5 | async-start | bytes 7077888 | tf_op jit(solution)/shard_map/all_gather | solution.py:69
  76.7 28.7 %copy-start.10 = (bf16[4096,8]{0,1:T(8,128)(2,1)S(1)}, bf16[4096,8]{0,1:T(8,128)(2,1)}, u32[]{:S(2)}) copy-start(bf16[4096,8]{0,1:T(8,128)(2,1)} %param.24) | copy-start | bytes 196612
  177.5 7.1 %copy-start.7 = (bf16[768,1,4096]{2,0,1:T(8,128)(2,1)S(1)}, bf16[768,1,4096]{2,0,1:T(8,128)(2,1)}, u32[]{:S(2)}) copy-start(bf16[768,1,4096]{2,0,1:T(8,128)(2,1)} %all-gather.3.cloned.1.call-done) | copy-start | bytes 18874372
  177.5 7.1 %copy-start.8 = (bf16[1,4096,448]{1,2,0:T(8,128)(2,1)S(1)}, bf16[1,4096,448]{1,2,0:T(8,128)(2,1)}, u32[]{:S(2)}) copy-start(bf16[1,4096,448]{1,2,0:T(8,128)(2,1)} %param.27) | copy-start | bytes 11010052
  192.0 27.3 %copy-start.12 = (s32[64]{0:T(128)S(1)}, s32[64]{0:T(128)}, u32[]{:S(2)}) copy-start(s32[64]{0:T(128)} %param.31) | copy-start | bytes 772
  192.0 47.9 %copy-start.5 = (f32[512]{0:T(512)S(1)}, f32[512]{0:T(512)}, u32[]{:S(2)}) copy-start(f32[512]{0:T(512)} %param.29) | copy-start | bytes 6148
  192.0 52.5 %copy-start.13 = (f32[4]{0:T(128)S(1)}, f32[4]{0:T(128)}, u32[]{:S(2)}) copy-start(f32[4]{0:T(128)} %param.30) | copy-start | bytes 52
  212.1 17.7 %all-to-all-start.3 = ((f32[32,2,512]{2,1,0:T(2,128)}), f32[32,2,512]{2,1,0:T(2,128)S(1)}, u32[]{:S(2)}, u32[]{:S(2)}) async-start(f32[32,2,512]{2,1,0:T(2,128)} %reshape.500), calls=%async_computation.3 | async-start | bytes 262144 | tf_op jit(solution)/shard_map/all_to_all | solution.py:59
  230.0 1.2 collective-permute-start.7
  231.3 3.6 %collective-permute-start.8 = (f32[2]{0:T(128)S(1)}, f32[2]{0:T(128)S(1)}, u32[]{:S(2)}, u32[]{:S(2)}) collective-permute-start(f32[2]{0:T(128)S(1)} %add.129), channel_id=1, source_target_pairs={{0,2},{1,3},{2,0},{3,1},{4,6},{5,7},{6,4},{7,5},{8,10},{9,11},{10,... | collective-permute-start | bytes 32 | tf_op jit(solution)/shard_map/ppermute | solution.py:91
  234.8 5.1 %collective-permute-start.9 = (f32[2]{0:T(128)S(1)}, f32[2]{0:T(128)S(1)}, u32[]{:S(2)}, u32[]{:S(2)}) collective-permute-start(f32[2]{0:T(128)S(1)} %add.130), channel_id=1, source_target_pairs={{0,4},{1,5},{2,6},{3,7},{4,0},{5,1},{6,2},{7,3},{8,12},{9,13},{10,... | collective-permute-start | bytes 32 | tf_op jit(solution)/shard_map/ppermute | solution.py:91
  240.0 15.8 %copy-start.4 = (bf16[2,512]{1,0:T(2,128)(2,1)}, bf16[2,512]{1,0:T(2,128)(2,1)S(1)}, u32[]{:S(2)}) copy-start(bf16[2,512]{1,0:T(2,128)(2,1)S(1)} %multiply_convert_fusion.1) | copy-start | bytes 6148
  240.7 13.9 %all-to-all-start.4 = ((bf16[32,2,512]{2,1,0:T(2,128)(2,1)}), bf16[32,2,512]{2,1,0:T(2,128)(2,1)S(1)}, u32[]{:S(2)}, u32[]{:S(2)}) async-start(bf16[32,2,512]{2,1,0:T(2,128)(2,1)} %broadcast_in_dim.191), calls=%async_computation.4 | async-start | bytes 131072 | tf_op jit(solution)/shard_map/all_to_all | solution.py:65
Sparse Core Ops, SparseCore 0:
  105.2 72.1 all-gather.2

commit v12 on v8

--- a/solution.py
+++ b/solution.py
@@ -186,7 +186,9 @@
     )
     pooled_cols = a2a_sum(pooled_part, "expert", 1, expert_count)
     own_cols = a2a_sum(pooled_cols, DP, 0, n_dp)
-    squares = doubling_sum(jnp.sum(own_cols * own_cols, axis=-1), "expert", expert_count)
+    squares = jnp.sum(
+        a2a_gather(jnp.sum(own_cols * own_cols, axis=-1), "expert", expert_count), axis=0
+    )
     summary = (
         own_cols * lax.rsqrt(squares / width + EPSILON)[:, None] * summary_gain
     ).astype(jnp.bfloat16)

time: 256 us -> 255 us (level)
  waiting for transfers between devices: 82.7 us -> 79.5 us
    ppermute x3 -> x0, waiting for transfers between devices: 7.02 us -> none  [doubling_sum(): x = x + lax.ppermute(x, axis, [(a, a ^ step) for a in range(count)])]
    all_to_all x2 -> x3, starting transfers between devices: 12.3 us -> 16.9 us  [a2a_gather(): return lax.all_to_all(spread, axis, split_axis=0, concat_axis=0, tiled=True)]
    all_to_all x2 -> x3, waiting for transfers between devices: 23.4 us -> 27.2 us  [a2a_gather(): return lax.all_to_all(spread, axis, split_axis=0, concat_axis=0, tiled=True)]
    ppermute x3 -> x0, starting transfers between devices: 2.85 us -> none  [doubling_sum(): x = x + lax.ppermute(x, axis, [(a, a ^ step) for a in range(count)])]
  transfers between devices with their start and end apart: 8 -> 6, of which waited for: 8 -> 6; matrix products, arithmetic and copies ran while one was open for 1% -> 1% of each run, Pallas kernels for 0% -> 0%
where the time goes in v12:
time: 255 us; the launch traced here: 254 us
  blocking collectives  102 us (40%)
  waiting for transfers between devices  79.5 us (31%)
  starting transfers between devices  31.8 us (12%)
  matrix products  17.2 us (7%)
  between operations  14.5 us (6%)
  local copies, waits for them, and re-layouts  7.65 us (3%)
    all_gather x1, blocking collectives, shards(): gathered_weight = lax.all_gather(pool_weight, DP, axis=0, tiled=True)  42 us
    all_to_all x3, waiting for transfers between devices, a2a_gather(): return lax.all_to_all(spread, axis, split_axis=0, concat_axis=0, tiled=True)  27.2 us
    all_gather x1, waiting for transfers between devices, dp_gather(): lax.all_gather(lax.all_gather(x, 'y', axis=axis, tiled=True), 'z', axis=a...  26 us
    all_to_all x1, blocking collectives, a2a_sum(): lax.all_to_all(x.reshape(split), axis, split_axis=dim, concat_axis=dim, t...  19.2 us
    all_to_all x3, starting transfers between devices, a2a_gather(): return lax.all_to_all(spread, axis, split_axis=0, concat_axis=0, tiled=True)  16.9 us
    all_to_all x1, waiting for transfers between devices, shards(): lax.all_to_all(head_terms, ('y', 'expert'), split_axis=0, concat_axis=0,...  15.9 us
    all_gather x1, blocking collectives, dp_gather(): lax.all_gather(x, 'y', axis=axis, tiled=True)  14.7 us
    all_to_all x1, blocking collectives, shards(): lax.all_to_all(outgoing, 'expert', split_axis=0, concat_axis=1, tiled=True)  13 us
  transfers between devices with their start and end apart: 6, of which 6 were waited for; matrix products, arithmetic and copies ran while one was open for 1% of the time, Pallas kernels for 0%

profile of v12, /device:TPU:2, one launch (start us, length us, event | category | flops | bytes accessed | tf_op | source)
XLA Modules:
  0.0 254.2 jit_solution(14680711108975570106)
XLA Ops:
  7.2 2.1 broadcast_in_dim.189
  9.3 8.5 %all-to-all-start = ((bf16[8,512,128]{2,1,0:T(8,128)(2,1)}), bf16[8,512,128]{2,1,0:T(8,128)(2,1)S(1)}, u32[]{:S(2)}, u32[]{:S(2)}) async-start(bf16[8,512,128]{2,1,0:T(8,128)(2,1)} %broadcast_in_dim.189), calls=%async_computation | async-start | bytes 2097152 | tf_op jit(solution)/shard_map/all_to_all | solution.py:65
  17.8 0.9 reshape.497
  18.7 0.4 fusion.59
  19.9 0.4 fusion.22
  20.4 12.8 %all_gather.12 = bf16[256,512]{1,0:T(8,128)(2,1)S(1)} all-gather(bf16[64,512]{1,0:T(8,128)(2,1)S(1)} %bitcast.142), channel_id=1, replica_groups=mesh['z'=8,'y'=4,'expert'=8] {'y'}, dimensions={0}, use_global_device_ids=true | all-gather | bytes 327680 | tf_op jit(solution)/shard_map/all_gather | solution.py:109
  33.2 13.4 %all-to-all-done = bf16[8,512,128]{2,1,0:T(8,128)(2,1)S(1)} async-done(((bf16[8,512,128]{2,1,0:T(8,128)(2,1)}), bf16[8,512,128]{2,1,0:T(8,128)(2,1)S(1)}, u32[]{:S(2)}, u32[]{:S(2)}) %all-to-all-start) | async-done | bytes 1048608 | tf_op jit(solution)/shard_map/all_to_all | solution.py:65
  46.5 0.4 fusion.31
  47.0 0.6 copy.87
  47.6 1.1 reshape.503
  48.8 7.6 %all-to-all-start.1 = ((f32[32,8,1024]{2,1,0:T(8,128)}), f32[32,8,1024]{2,1,0:T(8,128)S(1)}, u32[]{:S(2)}, u32[]{:S(2)}) async-start(f32[32,8,1024]{2,1,0:T(8,128)} %reshape.503), calls=%async_computation.1 | async-start | bytes 2097152 | tf_op jit(solution)/shard_map/all_to_all | solution.py:116
  56.5 15.9 %all-to-all-done.1 = f32[32,8,1024]{2,1,0:T(8,128)S(1)} async-done(((f32[32,8,1024]{2,1,0:T(8,128)}), f32[32,8,1024]{2,1,0:T(8,128)S(1)}, u32[]{:S(2)}, u32[]{:S(2)}) %all-to-all-start.1) | async-done | bytes 1048608 | tf_op jit(solution)/shard_map/all_to_all | solution.py:116
  73.2 13.0 %all_to_all.43 = bf16[8,8,4224]{2,1,0:T(8,128)(2,1)S(1)} all-to-all(bf16[8,8,4224]{2,1,0:T(8,128)(2,1)S(1)} %pad_maximum_fusion), channel_id=1, replica_groups=mesh['z'=8,'y'=4,'expert'=8] {'expert'}, dimensions={0} | all-to-all | bytes 1081344 | tf_op jit(solution)/shard_map/all_to_all | solution.py:137
  86.7 14.7 %all_gather.14 = bf16[96,1,4096]{2,0,1:T(8,128)(2,1)} all-gather(bf16[24,1,4096]{2,0,1:T(8,128)(2,1)S(1)} %bitcast.139), channel_id=1, replica_groups=mesh['z'=8,'y'=4,'expert'=8] {'y'}, dimensions={0}, use_global_device_ids=true | all-gather | bytes 983040 | tf_op jit(solution)/shard_map/all_gather | solution.py:69
  102.0 42.0 %all-gather = f32[32,24,2]{1,2,0:T(2,128)S(1)} all-gather(f32[1,24,2]{1,2,0:T(2,128)S(1)} %fusion.57), channel_id=1, replica_groups=mesh['z'=8,'y'=4,'expert'=8] {'z','y'}, dimensions={0}, use_global_device_ids=true | all-gather | bytes 6336 | tf_op jit(solution)/shard_map/all_gather | solution.py:167
  144.0 26.0 %all-gather.3.cloned.1.call-done = bf16[768,1,4096]{2,0,1:T(8,128)(2,1)} async-done(((bf16[96,1,4096]{2,0,1:T(8,128)(2,1)}), bf16[768,1,4096]{2,0,1:T(8,128)(2,1)}) %all-gather.3.cloned.1.call-update) | async-done | bytes 6291472 | tf_op jit(solution)/shard_map/all_gather | solution.py:69
  170.0 7.0 %fusion.3 = f32[768,448]{0,1:T(8,128)S(1)} fusion(bf16[768,1,4096]{2,0,1:T(8,128)(2,1)} %all-gather.3.cloned.1.call-done, bf16[1,4096,448]{1,2,0:T(8,128)(2,1)} %param.26), kind=kOutput, calls=%fused_computation.3 | convolution fusion | flops 2818572288 | bytes 11337728 | tf_op jit(solution)/shard_map/ned,edf->nf/dot_general | solution.py:169
  177.0 3.1 %fusion.14 = bf16[768,448]{0,1:T(8,128)(2,1)S(1)} fusion(bf16[1,4096,448]{1,2,0:T(8,128)(2,1)S(1)} %copy-done.8, bf16[768,1,4096]{2,0,1:T(8,128)(2,1)S(1)} %copy-done.7, f32[768,448]{0,1:T(8,128)S(1)} %fusion.3), kind=kOutput, calls=%fused_computation.13 | convolution fusion | flops 2820636672 | bytes 12025856 | tf_op jit(solution)/shard_map/ned,edf->nf/dot_general | solution.py:170
  180.4 0.4 fusion.66
  181.0 3.4 %convolution_add_fusion = f32[64,4096]{1,0:T(8,128)S(1)} fusion(f32[64,448]{1,0:T(8,128)S(1)} %reshape.513, bf16[1,448,4096]{2,1,0:T(8,128)(2,1)} %param.28, f32[4096]{0:T(1024)S(1)} %get-tuple-element.2, pred[64]{0:T(512)(128)(4,1)S(1)} %iota_compare_fusion.5), kind=kOutput, calls=%fused_computation.5 | convolution fusion | flops 705167360 | bytes 4849728 | tf_op jit(solution)/shard_map/dot_general | solution.py:178
  184.5 19.2 %all_to_all.44 = f32[64,8,512]{2,0,1:T(8,128)S(1)} all-to-all(f32[64,8,512]{2,0,1:T(8,128)S(1)} %bitcast.134), channel_id=1, replica_groups=mesh['z'=8,'y'=4,'expert'=8] {'expert'}, dimensions={1} | all-to-all | bytes 2097152 | tf_op jit(solution)/shard_map/all_to_all | solution.py:59
  203.8 0.7 reshape.515
  204.5 7.1 %all-to-all-start.4 = ((f32[32,2,512]{2,1,0:T(2,128)}), f32[32,2,512]{2,1,0:T(2,128)S(1)}, u32[]{:S(2)}, u32[]{:S(2)}) async-start(f32[32,2,512]{2,1,0:T(2,128)} %reshape.515), calls=%async_computation.4 | async-start | bytes 262144 | tf_op jit(solution)/shard_map/all_to_all | solution.py:59
  211.8 10.4 %all-to-all-done.4 = f32[32,2,512]{2,1,0:T(2,128)S(1)} async-done(((f32[32,2,512]{2,1,0:T(2,128)}), f32[32,2,512]{2,1,0:T(2,128)S(1)}, u32[]{:S(2)}, u32[]{:S(2)}) %all-to-all-start.4) | async-done | bytes 131104 | tf_op jit(solution)/shard_map/all_to_all | solution.py:59
  222.4 0.6 broadcast_in_dim.204
  223.0 4.6 %all-to-all-start.5 = ((f32[8,1,2]{2,1,0:T(1,128)}), f32[8,1,2]{2,1,0:T(1,128)S(1)}, u32[]{:S(2)}, u32[]{:S(2)}) async-start(f32[8,1,2]{2,1,0:T(1,128)} %broadcast_in_dim.204), calls=%async_computation.5 | async-start | bytes 8192 | tf_op jit(solution)/shard_map/all_to_all | solution.py:65
  227.7 3.8 %all-to-all-done.5 = f32[8,1,2]{2,1,0:T(1,128)S(1)} async-done(((f32[8,1,2]{2,1,0:T(1,128)}), f32[8,1,2]{2,1,0:T(1,128)S(1)}, u32[]{:S(2)}, u32[]{:S(2)}) %all-to-all-start.5) | async-done | bytes 96 | tf_op jit(solution)/shard_map/all_to_all | solution.py:65
  231.6 0.7 broadcast_in_dim.205
  232.3 3.9 %all-to-all-start.6 = ((bf16[32,2,512]{2,1,0:T(2,128)(2,1)}), bf16[32,2,512]{2,1,0:T(2,128)(2,1)S(1)}, u32[]{:S(2)}, u32[]{:S(2)}) async-start(bf16[32,2,512]{2,1,0:T(2,128)(2,1)} %broadcast_in_dim.205), calls=%async_computation.6 | async-start | bytes 131072 | tf_op jit(solution)/shard_map/all_to_all | solution.py:65
  236.2 10.0 %all-to-all-done.6 = bf16[32,2,512]{2,1,0:T(2,128)(2,1)S(1)} async-done(((bf16[32,2,512]{2,1,0:T(2,128)(2,1)}), bf16[32,2,512]{2,1,0:T(2,128)(2,1)S(1)}, u32[]{:S(2)}, u32[]{:S(2)}) %all-to-all-start.6) | async-done | bytes 65568 | tf_op jit(solution)/shard_map/all_to_all | solution.py:65
  246.2 0.4 fusion.61
  246.6 0.8 fusion.26
  (79 shorter events, 3.7 us)
Async XLA Ops:
  7.2 11.5 %copy-start = (bf16[2,1024,128]{2,1,0:T(8,128)(2,1)S(1)}, bf16[2,1024,128]{2,1,0:T(8,128)(2,1)}, u32[]{:S(2)}) copy-start(bf16[2,1024,128]{2,1,0:T(8,128)(2,1)} %param.20) | copy-start | bytes 1572868
  7.2 11.9 %copy-start.2 = (bf16[64,128]{1,0:T(8,128)(2,1)S(1)}, bf16[64,128]{1,0:T(8,128)(2,1)}, u32[]{:S(2)}) copy-start(bf16[64,128]{1,0:T(8,128)(2,1)} %param.18) | copy-start | bytes 49156
  7.2 12.5 %copy-start.11 = (bf16[64,128]{1,0:T(8,128)(2,1)S(1)}, bf16[64,128]{1,0:T(8,128)(2,1)}, u32[]{:S(2)}) copy-start(bf16[64,128]{1,0:T(8,128)(2,1)} %param.19) | copy-start | bytes 49156
  7.2 12.7 %copy-start.9 = (bf16[2,1024,128]{2,1,0:T(8,128)(2,1)S(1)}, bf16[2,1024,128]{2,1,0:T(8,128)(2,1)}, u32[]{:S(2)}) copy-start(bf16[2,1024,128]{2,1,0:T(8,128)(2,1)} %param.21) | copy-start | bytes 1572868
  9.3 37.2 %all-to-all-start = ((bf16[8,512,128]{2,1,0:T(8,128)(2,1)}), bf16[8,512,128]{2,1,0:T(8,128)(2,1)S(1)}, u32[]{:S(2)}, u32[]{:S(2)}) async-start(bf16[8,512,128]{2,1,0:T(8,128)(2,1)} %broadcast_in_dim.189), calls=%async_computation | async-start | bytes 2097152 | tf_op jit(solution)/shard_map/all_to_all | solution.py:65
  47.0 9.5 %copy-start.6 = (s32[8,2]{0,1:T(2,128)S(1)}, s32[8,2]{0,1:T(2,128)}, u32[]{:S(2)}) copy-start(s32[8,2]{0,1:T(2,128)} %param.25) | copy-start | bytes 196
  47.0 25.7 %copy-start.1 = (bf16[8,4096]{1,0:T(8,128)(2,1)S(1)}, bf16[8,4096]{1,0:T(8,128)(2,1)}, u32[]{:S(2)}) copy-start(bf16[8,4096]{1,0:T(8,128)(2,1)} %param.16) | copy-start | bytes 196612
  47.6 25.2 %copy-start.3 = (f32[4096]{0:T(1024)S(1)}, f32[4096]{0:T(1024)}, u32[]{:S(2)}) copy-start(f32[4096]{0:T(1024)} %param.23) | copy-start | bytes 49156
  48.8 23.6 %all-to-all-start.1 = ((f32[32,8,1024]{2,1,0:T(8,128)}), f32[32,8,1024]{2,1,0:T(8,128)S(1)}, u32[]{:S(2)}, u32[]{:S(2)}) async-start(f32[32,8,1024]{2,1,0:T(8,128)} %reshape.503), calls=%async_computation.1 | async-start | bytes 2097152 | tf_op jit(solution)/shard_map/all_to_all | solution.py:116
  56.4 113.6 %all-gather.3.cloned.1.call-start = ((), (), s32[]{:S(2)}) async-start(), calls=%async_computation.7 | async-start | bytes 7077888 | tf_op jit(solution)/shard_map/all_gather | solution.py:69
  72.4 29.3 %copy-start.10 = (bf16[4096,8]{0,1:T(8,128)(2,1)S(1)}, bf16[4096,8]{0,1:T(8,128)(2,1)}, u32[]{:S(2)}) copy-start(bf16[4096,8]{0,1:T(8,128)(2,1)} %param.24) | copy-start | bytes 196612
  170.0 7.0 %copy-start.7 = (bf16[768,1,4096]{2,0,1:T(8,128)(2,1)S(1)}, bf16[768,1,4096]{2,0,1:T(8,128)(2,1)}, u32[]{:S(2)}) copy-start(bf16[768,1,4096]{2,0,1:T(8,128)(2,1)} %all-gather.3.cloned.1.call-done) | copy-start | bytes 18874372
  170.0 7.1 %copy-start.8 = (bf16[1,4096,448]{1,2,0:T(8,128)(2,1)S(1)}, bf16[1,4096,448]{1,2,0:T(8,128)(2,1)}, u32[]{:S(2)}) copy-start(bf16[1,4096,448]{1,2,0:T(8,128)(2,1)} %param.27) | copy-start | bytes 11010052
  184.4 27.3 %copy-start.12 = (s32[64]{0:T(128)S(1)}, s32[64]{0:T(128)}, u32[]{:S(2)}) copy-start(s32[64]{0:T(128)} %param.31) | copy-start | bytes 772
  184.4 47.1 %copy-start.5 = (f32[512]{0:T(512)S(1)}, f32[512]{0:T(512)}, u32[]{:S(2)}) copy-start(f32[512]{0:T(512)} %param.29) | copy-start | bytes 6148
  184.4 51.7 %copy-start.13 = (f32[4]{0:T(128)S(1)}, f32[4]{0:T(128)}, u32[]{:S(2)}) copy-start(f32[4]{0:T(128)} %param.30) | copy-start | bytes 52
  204.5 17.7 %all-to-all-start.4 = ((f32[32,2,512]{2,1,0:T(2,128)}), f32[32,2,512]{2,1,0:T(2,128)S(1)}, u32[]{:S(2)}, u32[]{:S(2)}) async-start(f32[32,2,512]{2,1,0:T(2,128)} %reshape.515), calls=%async_computation.4 | async-start | bytes 262144 | tf_op jit(solution)/shard_map/all_to_all | solution.py:59
  223.0 8.5 %all-to-all-start.5 = ((f32[8,1,2]{2,1,0:T(1,128)}), f32[8,1,2]{2,1,0:T(1,128)S(1)}, u32[]{:S(2)}, u32[]{:S(2)}) async-start(f32[8,1,2]{2,1,0:T(1,128)} %broadcast_in_dim.204), calls=%async_computation.5 | async-start | bytes 8192 | tf_op jit(solution)/shard_map/all_to_all | solution.py:65
  231.6 15.8 %copy-start.4 = (bf16[2,512]{1,0:T(2,128)(2,1)}, bf16[2,512]{1,0:T(2,128)(2,1)S(1)}, u32[]{:S(2)}) copy-start(bf16[2,512]{1,0:T(2,128)(2,1)S(1)} %multiply_convert_fusion.1) | copy-start | bytes 6148
  232.3 13.9 %all-to-all-start.6 = ((bf16[32,2,512]{2,1,0:T(2,128)(2,1)}), bf16[32,2,512]{2,1,0:T(2,128)(2,1)S(1)}, u32[]{:S(2)}, u32[]{:S(2)}) async-start(bf16[32,2,512]{2,1,0:T(2,128)(2,1)} %broadcast_in_dim.205), calls=%async_computation.6 | async-start | bytes 131072 | tf_op jit(solution)/shard_map/all_to_all | solution.py:65
Sparse Core Ops, SparseCore 0:
  101.6 68.3 all-gather.2
